TPU v7x, 128 devices: a whole 4x4x4 slice. The times are simulated.
128 devices in a mesh: gx: 8 (over x, core), gy: 16 (over y, z).
Axes of the slice: x: 4, y: 4, z: 4, core: 2. Of those that a mesh axis runs over, the one named last changes fastest.
Arguments:
- coeffs: bfloat16 [3072, 2, 2, 2160], P(('gx', 'gy')), may hold values from -0.00390625 to 0.00390625
- legendre: bfloat16 [3072, 2160, 128], P(('gx', 'gy')), may hold values from -6 to 6
- orders: int32 [3072], P(('gx', 'gy')), may hold values from -1 to 2159, as said below
- lat_map: int32 [256], replicated, may hold values from 0 to 255, each once
- weights: float32 [128], replicated, may hold values from 0.5 to 2
Outputs:
- grid_square: bfloat16 [256, 2, 4320], P(('gx', 'gy'))
- spectra: bfloat16 [3072, 2, 2, 2160], P(('gx', 'gy'))
Inputs may be any that keep to these rules, and one draw needn't show every extreme that they name: Every order 0 to 2159 stands in exactly one slot and the other slots hold -1; in every draw the 24 slots of some device all hold orders. `lat_map`: each latitude stands in exactly one row.
All inputs are finite; a program needn't handle non-finite values.
Results may differ from a plain program's by a relative error of at most 0.012.
Values may be sent and summed in bfloat16 or wider, within the bound.
No kernel may reach another device: no remote copies, remote signals or barrier semaphores. Data moves between devices by JAX's collectives and lax.ppermute only.
A program may use at most 128 MiB of HBM per device.

v0:
```python
import math

import jax
import jax.numpy as jnp
from jax import lax
from jax.sharding import PartitionSpec as P

ORDER_BASE = 64


def slot_masks(orders, deg_count):
    degrees = jnp.arange(deg_count, dtype=jnp.int32)
    usable = (orders[:, None] >= 0) & (degrees[None, :] >= orders[:, None])
    even_pair = (degrees[None, :] + orders[:, None]) % 2 == 0
    return (usable, even_pair)


def inner_length(lon_count):
    best = 1
    for factor in range(1, math.isqrt(lon_count) + 1):
        if lon_count % factor == 0:
            best = factor
    return best


def phase_tables(order_vals, stride, count, lon_count):
    positions = jnp.arange(count, dtype=jnp.int32) * stride
    phase_int = positions[:, None] * order_vals[None, :] % lon_count
    angles = phase_int.astype(jnp.float32) * jnp.float32(2.0 * math.pi / lon_count)
    filled = order_vals[None, :] >= 0
    cosine = jnp.where(filled, jnp.cos(angles), jnp.float32(0.0))
    sine_tab = jnp.where(filled, jnp.sin(angles), jnp.float32(0.0))
    return (cosine, sine_tab)


def one_hot_rows(lat_map, lat_rows):
    return (lat_map[None, :] == jnp.arange(lat_rows, dtype=jnp.int32)[:, None]).astype(jnp.bfloat16)


def transform_rows(coef, order_vals, lon_count):
    high = lax.Precision.HIGH
    inner_len = inner_length(lon_count)
    outer_len = lon_count // inner_len
    cos_outer, sin_outer = phase_tables(order_vals, inner_len, outer_len, lon_count)
    cos_inner, sin_inner = phase_tables(order_vals, 1, inner_len, lon_count)
    coef_cos = coef[:, 0, :]
    coef_sin = coef[:, 1, :]
    y_real = coef_cos.T[:, None, :] * cos_outer[None] + coef_sin.T[:, None, :] * sin_outer[None]
    y_imag = coef_cos.T[:, None, :] * sin_outer[None] - coef_sin.T[:, None, :] * cos_outer[None]
    y_both = jnp.concatenate([y_real, y_imag], axis=-1)
    inner_both = jnp.concatenate([cos_inner, -sin_inner], axis=-1)
    grid_field = jnp.einsum("ras,bs->rab", y_both, inner_both, precision=high)
    signals = grid_field.shape[0]
    squared = (grid_field * grid_field).astype(jnp.bfloat16)
    sq_wide = squared.astype(jnp.float32)
    g_real = jnp.einsum("rab,bs->ras", sq_wide, cos_inner, precision=high)
    g_imag = -jnp.einsum("rab,bs->ras", sq_wide, sin_inner, precision=high)
    four_cos = jnp.sum(g_real * cos_outer[None] + g_imag * sin_outer[None], axis=1)
    four_sin = jnp.sum(g_real * sin_outer[None] - g_imag * cos_outer[None], axis=1)
    scaling = jnp.where(order_vals == 0, 1.0, 2.0).astype(jnp.float32) / lon_count
    fourier = jnp.stack([four_cos, four_sin], axis=1) * scaling[None, None, :]
    return squared.reshape(signals, lon_count), fourier


def shards(coeffs, legendre, orders, lat_map, weights):
    slot_cap = coeffs.shape[0]
    epoch_count = coeffs.shape[1]
    deg_count = legendre.shape[1]
    half_lats = legendre.shape[2]
    lon_count = 2 * deg_count
    lat_rows = lat_map.shape[0]
    devices = lax.axis_size(("gx", "gy"))
    rows_each = lat_rows // devices
    usable, even_pair = slot_masks(orders, deg_count)

    zero_half = jnp.zeros((), jnp.bfloat16)
    masked = jnp.where(usable[:, None, None, :], coeffs, zero_half)
    signed = jnp.where(even_pair[:, None, None, :], masked, -masked)
    stacked = jnp.concatenate([masked, signed], axis=1).reshape(slot_cap, 2 * epoch_count * 2, deg_count)
    synth = jnp.einsum("sxl,slk->sxk", stacked, legendre, preferred_element_type=jnp.float32)
    synth = synth.astype(jnp.bfloat16).reshape(slot_cap, 2, epoch_count * 2, half_lats)
    full_lats = jnp.concatenate([synth[:, 0], synth[:, 1, :, ::-1]], axis=-1)

    onehot = one_hot_rows(lat_map, lat_rows)
    permuted = jnp.einsum(
        "sxk,kr->sxr", full_lats, onehot, preferred_element_type=jnp.float32
    ).astype(jnp.bfloat16)
    sends = permuted.reshape(slot_cap, epoch_count * 2, devices, rows_each)
    sends = jnp.transpose(sends, (2, 0, 1, 3)).reshape(devices, slot_cap, epoch_count * 2 * rows_each)
    coded = orders + 1
    order_code = jnp.stack([coded // ORDER_BASE, coded % ORDER_BASE], axis=-1).astype(jnp.bfloat16)
    order_code = jnp.broadcast_to(order_code[None], (devices, slot_cap, 2))
    payload = jnp.concatenate([sends, order_code], axis=-1)
    got = lax.all_to_all(payload, ("gx", "gy"), 0, 0, tiled=True)
    got = got.reshape(devices * slot_cap, -1)
    code = got[:, -2:].astype(jnp.int32)
    all_orders = code[:, 0] * ORDER_BASE + code[:, 1] - 1
    received = got[:, :-2].reshape(devices * slot_cap, epoch_count, 2, rows_each)
    coef = jnp.transpose(received, (0, 2, 3, 1)).reshape(devices * slot_cap, 2, rows_each * epoch_count)
    squared, fourier = transform_rows(coef.astype(jnp.float32), all_orders, lon_count)
    grid_rows = squared.reshape(rows_each, epoch_count, lon_count)

    back = jnp.transpose(fourier, (2, 1, 0)).astype(jnp.bfloat16).reshape(devices, slot_cap, 2, rows_each, epoch_count)
    back = lax.all_to_all(back, ("gx", "gy"), 0, 0, tiled=True)
    returned = jnp.transpose(back, (1, 4, 2, 0, 3)).reshape(slot_cap, epoch_count * 2, lat_rows)
    natural = jnp.einsum(
        "sxr,kr->sxk", returned, onehot, preferred_element_type=jnp.float32
    )
    northern = natural[..., :half_lats]
    southern = natural[..., half_lats:][..., ::-1]
    sym_part = ((northern + southern) * weights).astype(jnp.bfloat16)
    anti_part = ((northern - southern) * weights).astype(jnp.bfloat16)
    both = jnp.concatenate([sym_part, anti_part], axis=1)
    out = jnp.einsum("sxk,slk->sxl", both, legendre, preferred_element_type=jnp.float32)
    out = out.reshape(slot_cap, 2, epoch_count, 2, deg_count)
    chosen = jnp.where(even_pair[:, None, None, :], out[:, 0], out[:, 1])
    spectra = jnp.where(usable[:, None, None, :], chosen, jnp.float32(0.0)).astype(jnp.bfloat16)
    return (grid_rows, spectra)


def solution(mesh):
    placed = (
        P(("gx", "gy"), None, None, None),
        P(("gx", "gy"), None, None),
        P(("gx", "gy")),
        P(),
        P(),
    )
    return jax.shard_map(
        shards,
        mesh=mesh,
        in_specs=placed,
        out_specs=(P(("gx", "gy"), None, None), P(("gx", "gy"), None, None, None)),
        check_vma=False,
    )
```

profile of v0, /device:TPU:1, one launch (start us, length us, event | category | flops | bytes accessed | tf_op | source)
XLA Modules:
  0.0 94.1 jit_solution(3519454398482724665)
XLA Ops:
  0.6 0.7 broadcast_compare_fusion.1
  1.3 0.7 convert_bitcast_fusion
  2.0 0.9 fusion.44
  2.8 2.2 %broadcast_select_fusion = (bf16[24,2,2,2160]{3,2,1,0:T(2,128)(2,1)S(1)}, bf16[24,2,2,2160]{3,2,1,0:T(2,128)(2,1)S(1)}) fusion(pred[24,2160]{1,0:T(8,128)(4,1)S(1)} %get-tuple-element.21, bf16[24,2,2,2160]{3,2,1,0:T(2,128)(2,1)} %param.5, pred[24,2160]{1,0:T(8,128)(4,1)S(1)} %get-tuple-element.20), kind=kLoop, calls=%fused_computation.32 | loop fusion | flops 622080 | bytes 1347840 | tf_op jit(solution)/shard_map/jit(_where)/select_n | solution.py:78
  5.0 1.1 %pad_maximum_fusion = bf16[24,4,2,2160]{3,2,1,0:T(2,128)(2,1)S(1)} fusion(bf16[24,2,2,2160]{3,2,1,0:T(2,128)(2,1)S(1)} %get-tuple-element.4, bf16[24,2,2,2160]{3,2,1,0:T(2,128)(2,1)S(1)} %get-tuple-element.5), kind=kLoop, calls=%fused_computation.31 | loop fusion | flops 414720 | bytes 1658880 | tf_op jit(solution)/shard_map/concatenate | solution.py:79
  6.1 0.6 reshape.249
  6.8 0.0 copy-start
  6.8 5.9 %convolution_convert_fusion.1 = bf16[24,8,128]{2,1,0:T(8,128)(2,1)S(1)} fusion(bf16[24,8,2160]{2,1,0:T(8,128)(2,1)S(1)} %reshape.249, bf16[24,2160,128]{2,1,0:T(8,128)(2,1)} %param.6), kind=kOutput, calls=%fused_computation.17 | convolution fusion | flops 106192896 | bytes 14149632 | tf_op jit(solution)/shard_map/sxl,slk->sxk/dot_general | solution.py:80
  12.8 0.1 rev.6
  12.9 0.0 copy-done
  12.9 0.2 convolution_convert_fusion
  13.0 0.2 copy.37
  13.2 0.1 copy.38
  13.4 0.1 broadcast_in_dim.77
  13.5 1.2 %copy.39 = bf16[128,24,10]{1,2,0:T(8,128)(2,1)} copy(bf16[128,24,10]{0,1,2:T(8,128)(2,1)S(1)} %pad_maximum_fusion.1) | data formatting | bytes 122880 | tf_op jit(solution)/shard_map/concatenate | solution.py:93
  14.7 11.7 %all-to-all-start = ((bf16[128,24,10]{1,2,0:T(8,128)(2,1)}), bf16[128,24,10]{1,2,0:T(8,128)(2,1)S(1)}, u32[]{:S(2)}, u32[]{:S(2)}) async-start(bf16[128,24,10]{1,2,0:T(8,128)(2,1)} %copy.39), calls=%async_computation | async-start | bytes 1048576 | tf_op jit(solution)/shard_map/all_to_all | solution.py:94
  26.4 13.7 %all-to-all-done = bf16[128,24,10]{1,2,0:T(8,128)(2,1)S(1)} async-done(((bf16[128,24,10]{1,2,0:T(8,128)(2,1)}), bf16[128,24,10]{1,2,0:T(8,128)(2,1)S(1)}, u32[]{:S(2)}, u32[]{:S(2)}) %all-to-all-start) | async-done | bytes 61472 | tf_op jit(solution)/shard_map/all_to_all | solution.py:94
  40.0 0.1 copy.40
  40.1 0.4 reshape.253
  40.6 0.6 slice_convert_fusion
  41.3 3.2 %cosine_select_fusion.1 = (f32[60,3072]{1,0:T(8,128)S(1)}, f32[60,3072]{1,0:T(8,128)S(1)}) fusion(s32[3072]{0:T(1024)S(1)} %bitcast.82, pred[3072]{0:T(1024)(128)(4,1)S(1)} %broadcast_compare_fusion), kind=kLoop, calls=%fused_computation.40 | loop fusion | flops 2211840 | bytes 1489920 | tf_op jit(solution)/shard_map/jit(_where)/select_n | solution.py:31
  44.5 3.7 %cosine_select_fusion = (f32[72,3072]{1,0:T(8,128)S(1)}, f32[72,3072]{1,0:T(8,128)S(1)}) fusion(s32[3072]{0:T(1024)S(1)} %bitcast.83, s32[72]{0:T(128)S(1)} %iota_multiply_fusion, pred[3072]{0:T(1024)(128)(4,1)S(1)} %broadcast_compare_fusion), kind=kLoop, calls=%fused_computation.21 | loop fusion | flops 2433024 | bytes 1785120 | tf_op jit(solution)/shard_map/jit(_where)/select_n | solution.py:31
  48.2 1.6 %reshape.258 = f32[3072,2,2,2]{0,3,2,1:T(2,128)} reshape(f32[3072,8]{0,1:T(8,128)} %slice_convert_fusion) | data formatting | bytes 196608 | tf_op jit(solution)/shard_map/convert_element_type | solution.py:100
  49.8 0.9 %copy.41 = f32[3072,2,2,2]{0,1,3,2:T(2,128)S(1)} copy(f32[3072,2,2,2]{0,2,1,3:T(2,128)} %bitcast.87) | data formatting | bytes 196608 | tf_op jit(solution)/shard_map/convert_element_type | solution.py:100
  50.8 0.1 fusion.67
  50.9 1.0 %multiply_add_fusion = (f32[4,72,3072]{2,1,0:T(8,128)S(1)}, f32[4,72,3072]{2,1,0:T(8,128)S(1)}) fusion(f32[72,3072]{1,0:T(8,128)S(1)} %get-tuple-element.17, f32[4,3072]{1,0:T(4,128)S(1)} %get-tuple-element.22, f32[72,3072]{1,0:T(8,128)S(1)} %get-tuple-element.16, f32[4,3072]{1,0:T(4,128)S(1)} %get-tuple-element.23), kind=kLoop, calls=%fused_computation.8 | loop fusion | flops 5308416 | bytes 8945664 | tf_op jit(solution)/shard_map/add | solution.py:48
  51.9 5.0 %fusion.9 = bf16[4,72,60]{1,2,0:T(8,128)(2,1)S(1)} fusion(f32[60,3072]{1,0:T(8,128)S(1)} %get-tuple-element.19, f32[60,3072]{1,0:T(8,128)S(1)} %get-tuple-element.18, f32[4,72,3072]{2,1,0:T(8,128)S(1)} %get-tuple-element.9, f32[4,72,3072]{2,1,0:T(8,128)S(1)} %get-tuple-element.8), kind=kOutput, calls=%fused_computation.15 | convolution fusion | flops 639182592 | bytes 8587008 | tf_op jit(solution)/shard_map/ras,bs->rab/dot_general | solution.py:52
  56.9 3.8 %fusion.23 = f32[4,72,3072]{2,1,0:T(8,128)S(1)} fusion(bf16[4,72,60]{1,2,0:T(8,128)(2,1)S(1)} %fusion.9, s32[3072]{0:T(1024)S(1)} %bitcast.84, pred[3072]{0:T(1024)(128)(4,1)S(1)} %broadcast_compare_fusion), kind=kOutput, calls=%fused_computation.37 | convolution fusion | flops 320348160 | bytes 3588864 | tf_op jit(solution)/shard_map/rab,bs->ras/dot_general | solution.py:56
  60.8 0.0 copy-start.1
  60.8 5.3 %add_reduce_fusion = (f32[4,3072]{1,0:T(4,128)S(1)}, f32[4,3072]{1,0:T(4,128)S(1)}) fusion(f32[4,72,3072]{2,1,0:T(8,128)S(1)} %fusion.23, f32[72,3072]{1,0:T(8,128)S(1)} %get-tuple-element.17, f32[72,3072]{1,0:T(8,128)S(1)} %get-tuple-element.16, bf16[4,72,60]{1,2,0:T(8,128)(2,1)S(1)} %fusion.9, s32[3072]{0:T(1024)S(1)} %bitcast.85, ...), kind=kOutput, calls=%fused_computation.6 | convolution fusion | flops 328286208 | bytes 5456640 | tf_op jit(solution)/shard_map/rab,bs->ras/dot_general | solution.py:57
  66.2 0.4 reshape.254
  66.5 1.0 %copy.43 = bf16[128,24,2,2,2]{1,4,3,2,0:T(2,128)(2,1)} copy(bf16[128,24,2,2,2]{1,0,4,3,2:T(8,128)(2,1)S(1)} %reshape.254) | data formatting | bytes 98304 | tf_op jit(solution)/shard_map/reshape | solution.py:103
  67.5 4.2 %all-to-all-start.1 = ((bf16[128,24,2,2,2]{1,4,3,2,0:T(2,128)(2,1)}), bf16[128,24,2,2,2]{1,4,3,2,0:T(2,128)(2,1)S(1)}, u32[]{:S(2)}, u32[]{:S(2)}) async-start(bf16[128,24,2,2,2]{1,4,3,2,0:T(2,128)(2,1)} %copy.43), calls=%async_computation.1 | async-start | bytes 524288 | tf_op jit(solution)/shard_map/all_to_all | solution.py:104
  71.7 0.1 copy.42
  71.8 0.8 reshape_reshape.3
  72.6 10.5 %all-to-all-done.1 = bf16[128,24,2,2,2]{1,4,3,2,0:T(2,128)(2,1)S(1)} async-done(((bf16[128,24,2,2,2]{1,4,3,2,0:T(2,128)(2,1)}), bf16[128,24,2,2,2]{1,4,3,2,0:T(2,128)(2,1)S(1)}, u32[]{:S(2)}, u32[]{:S(2)}) %all-to-all-start.1) | async-done | bytes 49184 | tf_op jit(solution)/shard_map/all_to_all | solution.py:104
  83.1 0.1 copy.44
  83.2 0.2 fusion.36
  83.5 0.1 rev.7
  83.5 0.0 copy-done.1
  83.6 8.5 %fusion.52 = bf16[24,8,2160]{2,1,0:T(8,128)(2,1)S(1)} fusion(bf16[24,2160,128]{2,1,0:T(8,128)(2,1)} %param.6, bf16[24,8,128]{2,0,1:T(8,128)(2,1)S(1)} %pad_maximum_fusion.2), kind=kOutput, calls=%fused_computation.77 | convolution fusion | flops 106168320 | bytes 14149632 | tf_op jit(solution)/shard_map/sxk,slk->sxl/dot_general | solution.py:114
  92.1 0.3 reshape.256
  92.4 1.7 %fusion.19 = bf16[24,2,2,2160]{3,2,1,0:T(2,128)(2,1)} fusion(bf16[24,2,2,2,2160]{4,3,2,1,0:T(2,128)(2,1)S(1)} %reshape.256, pred[24,2160]{1,0:T(8,128)(4,1)S(1)} %get-tuple-element.21, pred[24,2160]{1,0:T(8,128)(4,1)S(1)} %get-tuple-element.20), kind=kLoop, calls=%fused_computation.29 | loop fusion | flops 414720 | bytes 1347840 | tf_op jit(solution)/shard_map/convert_element_type | solution.py:117
  (16 shorter events, 0.2 us)
Async XLA Ops:
  6.8 6.1 %copy-start = (s32[256]{0:T(256)S(1)}, s32[256]{0:T(256)}, u32[]{:S(2)}) copy-start(s32[256]{0:T(256)} %param.8) | copy-start | bytes 3076
  14.7 25.4 %all-to-all-start = ((bf16[128,24,10]{1,2,0:T(8,128)(2,1)}), bf16[128,24,10]{1,2,0:T(8,128)(2,1)S(1)}, u32[]{:S(2)}, u32[]{:S(2)}) async-start(bf16[128,24,10]{1,2,0:T(8,128)(2,1)} %copy.39), calls=%async_computation | async-start | bytes 1048576 | tf_op jit(solution)/shard_map/all_to_all | solution.py:94
  60.8 22.8 %copy-start.1 = (f32[128]{0:T(128)S(1)}, f32[128]{0:T(128)}, u32[]{:S(2)}) copy-start(f32[128]{0:T(128)} %param.9) | copy-start | bytes 1540
  67.5 15.6 %all-to-all-start.1 = ((bf16[128,24,2,2,2]{1,4,3,2,0:T(2,128)(2,1)}), bf16[128,24,2,2,2]{1,4,3,2,0:T(2,128)(2,1)S(1)}, u32[]{:S(2)}, u32[]{:S(2)}) async-start(bf16[128,24,2,2,2]{1,4,3,2,0:T(2,128)(2,1)} %copy.43), calls=%async_computation.1 | async-start | bytes 524288 | tf_op jit(solution)/shard_map/all_to_all | solution.py:104
where the time goes:
time: 94.4 us; the launch traced here: 94.1 us
  matrix products  28.9 us (31%)
  waiting for transfers between devices  24.2 us (26%)
  other arithmetic  15.9 us (17%)
  starting transfers between devices  15.9 us (17%)
  local copies, waits for them, and re-layouts  8.29 us (9%)
    all_to_all x1, waiting for transfers between devices, shards(): got = lax.all_to_all(payload, ('gx', 'gy'), 0, 0, tiled=True)  13.7 us
    all_to_all x1, starting transfers between devices, shards(): got = lax.all_to_all(payload, ('gx', 'gy'), 0, 0, tiled=True)  11.7 us
    all_to_all x1, waiting for transfers between devices, shards(): back = lax.all_to_all(back, ('gx', 'gy'), 0, 0, tiled=True)  10.5 us
    dot_general x1, matrix products, shards(): jnp.einsum('sxk,slk->sxl', both, legendre, preferred_element_type=jnp.flo...  8.47 us
    select_n x2, other arithmetic, phase_tables(): cosine = jnp.where(filled, jnp.cos(angles), jnp.float32(0.0))  6.91 us
    dot_general x1, matrix products, shards(): jnp.einsum('sxl,slk->sxk', stacked, legendre, preferred_element_type=jnp....  5.94 us
    dot_general x1, matrix products, transform_rows(): g_imag = -jnp.einsum('rab,bs->ras', sq_wide, sin_inner, precision=high)  5.32 us
    dot_general x1, matrix products, transform_rows(): grid_field = jnp.einsum('ras,bs->rab', y_both, inner_both, precision=high)  5.01 us
  transfers between devices with their start and end apart: 2, of which 2 were waited for; matrix products, arithmetic and copies ran while one was open for 1% of the time, Pallas kernels for 0%

commit v1 on v0

--- a/solution.py
+++ b/solution.py
@@ -3,16 +3,103 @@
 import jax
 import jax.numpy as jnp
 from jax import lax
+from jax.experimental import pallas as pl
+from jax.experimental.pallas import tpu as pltpu
 from jax.sharding import PartitionSpec as P
 
 ORDER_BASE = 64
 
-
-def slot_masks(orders, deg_count):
-    degrees = jnp.arange(deg_count, dtype=jnp.int32)
-    usable = (orders[:, None] >= 0) & (degrees[None, :] >= orders[:, None])
-    even_pair = (degrees[None, :] + orders[:, None]) % 2 == 0
-    return (usable, even_pair)
+SLOTS_PER_STEP = 6
+
+
+def _masks(order, deg_count):
+    degrees = lax.broadcasted_iota(jnp.int32, (1, deg_count), 1)
+    usable = (degrees >= order) & (order >= 0)
+    even = ((degrees + order) & 1) == 0
+    return usable, even
+
+
+def _synth_kernel(orders_ref, coef_ref, leg_ref, out_ref):
+    step = pl.program_id(0)
+    block, epochs, _, deg_count = coef_ref.shape
+    zero = jnp.zeros((), coef_ref.dtype)
+    for i in range(block):
+        order = orders_ref[step * block + i]
+        usable, even = _masks(order, deg_count)
+        rows = jnp.concatenate([coef_ref[i, e] for e in range(epochs)], axis=0)
+        masked = jnp.where(usable, rows, zero)
+        signed = jnp.where(even, masked, -masked)
+        lhs = jnp.concatenate([masked, signed], axis=0)
+        out_ref[i] = jnp.dot(lhs, leg_ref[i], preferred_element_type=jnp.float32).astype(out_ref.dtype)
+
+
+def synthesize(coeffs, legendre, orders):
+    slot_cap, epochs, parts, deg_count = coeffs.shape
+    half_lats = legendre.shape[2]
+    block = SLOTS_PER_STEP
+    rows = 2 * epochs * parts
+    grid_spec = pltpu.PrefetchScalarGridSpec(
+        num_scalar_prefetch=1,
+        grid=(slot_cap // block,),
+        in_specs=[
+            pl.BlockSpec((block, epochs, parts, deg_count), lambda g, o: (g, 0, 0, 0)),
+            pl.BlockSpec((block, deg_count, half_lats), lambda g, o: (g, 0, 0)),
+        ],
+        out_specs=pl.BlockSpec((block, rows, half_lats), lambda g, o: (g, 0, 0)),
+    )
+    return pl.pallas_call(
+        _synth_kernel,
+        grid_spec=grid_spec,
+        out_shape=jax.ShapeDtypeStruct((slot_cap, rows, half_lats), jnp.bfloat16),
+        compiler_params=pltpu.CompilerParams(dimension_semantics=("arbitrary",)),
+        cost_estimate=pl.CostEstimate(
+            flops=2 * slot_cap * rows * deg_count * half_lats,
+            bytes_accessed=legendre.size * 2 + coeffs.size * 2 + slot_cap * rows * half_lats * 2,
+            transcendentals=0,
+        ),
+    )(orders, coeffs, legendre)
+
+
+def _analysis_kernel(orders_ref, both_ref, leg_ref, out_ref):
+    step = pl.program_id(0)
+    block, epochs, parts, deg_count = out_ref.shape
+    half = epochs * parts
+    for i in range(block):
+        order = orders_ref[step * block + i]
+        usable, even = _masks(order, deg_count)
+        res = lax.dot_general(
+            both_ref[i], leg_ref[i], (((1,), (1,)), ((), ())), preferred_element_type=jnp.float32
+        )
+        chosen = jnp.where(even, res[:half], res[half:])
+        chosen = jnp.where(usable, chosen, jnp.float32(0.0)).astype(out_ref.dtype)
+        for e in range(epochs):
+            out_ref[i, e] = chosen[e * parts:(e + 1) * parts]
+
+
+def analyze(both, legendre, orders, epochs, parts):
+    slot_cap, rows, half_lats = both.shape
+    deg_count = legendre.shape[1]
+    block = SLOTS_PER_STEP
+    grid_spec = pltpu.PrefetchScalarGridSpec(
+        num_scalar_prefetch=1,
+        grid=(slot_cap // block,),
+        in_specs=[
+            pl.BlockSpec((block, rows, half_lats), lambda g, o: (g, 0, 0)),
+            pl.BlockSpec((block, deg_count, half_lats), lambda g, o: (g, 0, 0)),
+        ],
+        out_specs=pl.BlockSpec((block, epochs, parts, deg_count), lambda g, o: (g, 0, 0, 0)),
+    )
+    return pl.pallas_call(
+        _analysis_kernel,
+        grid_spec=grid_spec,
+        out_shape=jax.ShapeDtypeStruct((slot_cap, epochs, parts, deg_count), jnp.bfloat16),
+        compiler_params=pltpu.CompilerParams(dimension_semantics=("arbitrary",)),
+        cost_estimate=pl.CostEstimate(
+            flops=2 * slot_cap * rows * deg_count * half_lats,
+            bytes_accessed=legendre.size * 2 + both.size * 2 + slot_cap * epochs * parts * deg_count * 2,
+            transcendentals=0,
+        ),
+    )(orders, both, legendre)
 
 
 def inner_length(lon_count):
@@ -71,14 +158,8 @@
     lat_rows = lat_map.shape[0]
     devices = lax.axis_size(("gx", "gy"))
     rows_each = lat_rows // devices
-    usable, even_pair = slot_masks(orders, deg_count)
-
-    zero_half = jnp.zeros((), jnp.bfloat16)
-    masked = jnp.where(usable[:, None, None, :], coeffs, zero_half)
-    signed = jnp.where(even_pair[:, None, None, :], masked, -masked)
-    stacked = jnp.concatenate([masked, signed], axis=1).reshape(slot_cap, 2 * epoch_count * 2, deg_count)
-    synth = jnp.einsum("sxl,slk->sxk", stacked, legendre, preferred_element_type=jnp.float32)
-    synth = synth.astype(jnp.bfloat16).reshape(slot_cap, 2, epoch_count * 2, half_lats)
+
+    synth = synthesize(coeffs, legendre, orders).reshape(slot_cap, 2, epoch_count * 2, half_lats)
     full_lats = jnp.concatenate([synth[:, 0], synth[:, 1, :, ::-1]], axis=-1)
 
     onehot = one_hot_rows(lat_map, lat_rows)
@@ -111,10 +192,7 @@
     sym_part = ((northern + southern) * weights).astype(jnp.bfloat16)
     anti_part = ((northern - southern) * weights).astype(jnp.bfloat16)
     both = jnp.concatenate([sym_part, anti_part], axis=1)
-    out = jnp.einsum("sxk,slk->sxl", both, legendre, preferred_element_type=jnp.float32)
-    out = out.reshape(slot_cap, 2, epoch_count, 2, deg_count)
-    chosen = jnp.where(even_pair[:, None, None, :], out[:, 0], out[:, 1])
-    spectra = jnp.where(usable[:, None, None, :], chosen, jnp.float32(0.0)).astype(jnp.bfloat16)
+    spectra = analyze(both, legendre, orders, epoch_count, 2)
     return (grid_rows, spectra)
 
 

time: 94.4 us -> 88 us (0.932)
  Pallas kernels: 0 us -> 16.4 us
  matrix products: 28.9 us -> 14.5 us
  other arithmetic: 15.9 us -> 10 us
  local copies, waits for them, and re-layouts: 8.29 us -> 5.73 us
    pallas_call x0 -> x2, Pallas kernels: none -> 16.4 us  [the longest x1 8.61 us: analyze(): pl.pallas_call(_analysis_kernel, grid_spec=grid_spec, out_shape=jax.Shape...]
    dot_general x2 -> x0, matrix products: 14.4 us -> none  [the longest x1 8.47 us: shards(): jnp.einsum('sxk,slk->sxl', both, legendre, preferred_element_type=jnp.flo...]
    convert_element_type x2, local copies, waits for them, and re-layouts: 2.53 us -> 0.12 us  [shards(): coef.astype(jnp.float32)]
    select_n x1 -> x0, other arithmetic: 2.18 us -> none  [shards(): signed = jnp.where(even_pair[:, None, None, :], masked, -masked)]
    convert_element_type x1 -> x0, other arithmetic: 1.67 us -> none  [shards(): jnp.where(usable[:, None, None, :], chosen, jnp.float32(0.0))]
    concatenate x1 -> x0, other arithmetic: 1.09 us -> none  [shards(): jnp.concatenate([masked, signed], axis=1)]
    reshape x2 -> x0, local copies, waits for them, and re-layouts: 0.98 us -> none  [the longest x1 0.64 us: shards(): jnp.concatenate([masked, signed], axis=1)]
where the time goes in v1:
time: 88 us; the launch traced here: 87.6 us
  waiting for transfers between devices  24.4 us (28%)
  Pallas kernels  16.4 us (19%)
  starting transfers between devices  15.7 us (18%)
  matrix products  14.5 us (16%)
  other arithmetic  10 us (11%)
  local copies, waits for them, and re-layouts  5.73 us (7%)
  between operations  0.91 us (1%)
    all_to_all x1, waiting for transfers between devices, shards(): got = lax.all_to_all(payload, ('gx', 'gy'), 0, 0, tiled=True)  13.9 us
    all_to_all x1, starting transfers between devices, shards(): got = lax.all_to_all(payload, ('gx', 'gy'), 0, 0, tiled=True)  11.5 us
    all_to_all x1, waiting for transfers between devices, shards(): back = lax.all_to_all(back, ('gx', 'gy'), 0, 0, tiled=True)  10.5 us
    pallas_call x1, Pallas kernels, analyze(): pl.pallas_call(_analysis_kernel, grid_spec=grid_spec, out_shape=jax.Shape...  8.61 us
    pallas_call x1, Pallas kernels, synthesize(): pl.pallas_call(_synth_kernel, grid_spec=grid_spec, out_shape=jax.ShapeDty...  7.83 us
    select_n x2, other arithmetic, phase_tables(): cosine = jnp.where(filled, jnp.cos(angles), jnp.float32(0.0))  6.91 us
    dot_general x1, matrix products, transform_rows(): g_imag = -jnp.einsum('rab,bs->ras', sq_wide, sin_inner, precision=high)  5.31 us
    dot_general x1, matrix products, transform_rows(): grid_field = jnp.einsum('ras,bs->rab', y_both, inner_both, precision=high)  4.96 us
  transfers between devices with their start and end apart: 2, of which 2 were waited for; matrix products, arithmetic and copies ran while one was open for 1% of the time, Pallas kernels for 0%

profile of v1, /device:TPU:1, one launch (start us, length us, event | category | flops | bytes accessed | tf_op | source)
XLA Modules:
  0.0 87.6 jit_solution(6566861468044566029)
XLA Ops:
  0.6 0.7 convert_bitcast_fusion
  1.3 0.0 copy-start.1
  1.3 7.8 %shard_map.68 = bf16[24,8,128]{2,1,0:T(8,128)(2,1)} custom-call(s32[24]{0:T(128)} %orders_ref.3, bf16[24,2,2,2160]{3,2,1,0:T(2,128)(2,1)} %coef_ref.1, bf16[24,2160,128]{2,1,0:T(8,128)(2,1)} %leg_ref.3), custom_call_target="tpu_custom_call" | custom-call | flops 106168320 | bytes 13734912 | tf_op jit(solution)/shard_map/pallas_call | solution.py:50
  9.1 0.8 fusion.58
  9.9 0.1 rev.6
  10.0 0.0 copy-done.1
  10.0 0.2 convolution_convert_fusion
  10.2 0.2 copy.34
  10.4 0.1 copy.35
  10.5 0.1 broadcast_in_dim.40
  10.6 1.2 %copy.36 = bf16[128,24,10]{1,2,0:T(8,128)(2,1)} copy(bf16[128,24,10]{0,1,2:T(8,128)(2,1)S(1)} %pad_maximum_fusion) | data formatting | bytes 122880 | tf_op jit(solution)/shard_map/concatenate | solution.py:174
  11.8 11.5 %all-to-all-start = ((bf16[128,24,10]{1,2,0:T(8,128)(2,1)}), bf16[128,24,10]{1,2,0:T(8,128)(2,1)S(1)}, u32[]{:S(2)}, u32[]{:S(2)}) async-start(bf16[128,24,10]{1,2,0:T(8,128)(2,1)} %copy.36), calls=%async_computation | async-start | bytes 1048576 | tf_op jit(solution)/shard_map/all_to_all | solution.py:175
  23.3 13.9 %all-to-all-done = bf16[128,24,10]{1,2,0:T(8,128)(2,1)S(1)} async-done(((bf16[128,24,10]{1,2,0:T(8,128)(2,1)}), bf16[128,24,10]{1,2,0:T(8,128)(2,1)S(1)}, u32[]{:S(2)}, u32[]{:S(2)}) %all-to-all-start) | async-done | bytes 61472 | tf_op jit(solution)/shard_map/all_to_all | solution.py:175
  37.2 0.1 copy.37
  37.3 0.4 reshape.189
  37.8 0.6 select_multiply_fusion
  38.4 3.2 %cosine_select_fusion.1 = (f32[60,3072]{1,0:T(8,128)S(1)}, f32[60,3072]{1,0:T(8,128)S(1)}) fusion(s32[3072]{0:T(1024)S(1)} %bitcast.63, pred[3072]{0:T(1024)(128)(4,1)S(1)} %broadcast_compare_fusion), kind=kLoop, calls=%fused_computation.31 | loop fusion | flops 2211840 | bytes 1489920 | tf_op jit(solution)/shard_map/jit(_where)/select_n | solution.py:118
  41.7 3.7 %cosine_select_fusion = (f32[72,3072]{1,0:T(8,128)S(1)}, f32[72,3072]{1,0:T(8,128)S(1)}) fusion(s32[3072]{0:T(1024)S(1)} %bitcast.64, s32[72]{0:T(128)S(1)} %iota_multiply_fusion, pred[3072]{0:T(1024)(128)(4,1)S(1)} %broadcast_compare_fusion), kind=kLoop, calls=%fused_computation.20 | loop fusion | flops 2433024 | bytes 1785120 | tf_op jit(solution)/shard_map/jit(_where)/select_n | solution.py:118
  45.4 0.1 reshape.193
  45.4 0.1 copy.38
  45.5 0.1 fusion.57
  45.6 1.0 %multiply_add_fusion = (f32[4,72,3072]{2,1,0:T(8,128)S(1)}, f32[4,72,3072]{2,1,0:T(8,128)S(1)}) fusion(f32[72,3072]{1,0:T(8,128)S(1)} %get-tuple-element.17, f32[4,3072]{1,0:T(4,128)S(1)} %get-tuple-element.20, f32[72,3072]{1,0:T(8,128)S(1)} %get-tuple-element.16, f32[4,3072]{1,0:T(4,128)S(1)} %get-tuple-element.21), kind=kLoop, calls=%fused_computation.8 | loop fusion | flops 5308416 | bytes 8945664 | tf_op jit(solution)/shard_map/add | solution.py:135
  46.7 5.0 %fusion.9 = bf16[4,72,60]{1,2,0:T(8,128)(2,1)S(1)} fusion(f32[60,3072]{1,0:T(8,128)S(1)} %get-tuple-element.19, f32[60,3072]{1,0:T(8,128)S(1)} %get-tuple-element.18, f32[4,72,3072]{2,1,0:T(8,128)S(1)} %get-tuple-element.7, f32[4,72,3072]{2,1,0:T(8,128)S(1)} %get-tuple-element.6), kind=kOutput, calls=%fused_computation.15 | convolution fusion | flops 639182592 | bytes 8587008 | tf_op jit(solution)/shard_map/ras,bs->rab/dot_general | solution.py:139
  51.6 3.8 %fusion.20 = f32[4,72,3072]{2,1,0:T(8,128)S(1)} fusion(bf16[4,72,60]{1,2,0:T(8,128)(2,1)S(1)} %fusion.9, s32[3072]{0:T(1024)S(1)} %bitcast.65, pred[3072]{0:T(1024)(128)(4,1)S(1)} %broadcast_compare_fusion), kind=kOutput, calls=%fused_computation.28 | convolution fusion | flops 320348160 | bytes 3588864 | tf_op jit(solution)/shard_map/rab,bs->ras/dot_general | solution.py:143
  55.4 0.0 copy-start
  55.5 0.0 copy-start.2
  55.5 0.0 copy-start.3
  55.5 5.3 %add_reduce_fusion = (f32[4,3072]{1,0:T(4,128)S(1)}, f32[4,3072]{1,0:T(4,128)S(1)}) fusion(f32[4,72,3072]{2,1,0:T(8,128)S(1)} %fusion.20, f32[72,3072]{1,0:T(8,128)S(1)} %get-tuple-element.17, f32[72,3072]{1,0:T(8,128)S(1)} %get-tuple-element.16, bf16[4,72,60]{1,2,0:T(8,128)(2,1)S(1)} %fusion.9, s32[3072]{0:T(1024)S(1)} %bitcast.66, ...), kind=kOutput, calls=%fused_computation.6 | convolution fusion | flops 328286208 | bytes 5456640 | tf_op jit(solution)/shard_map/rab,bs->ras/dot_general | solution.py:144
  60.8 0.0 copy-done
  60.8 0.4 reshape.190
  61.2 1.0 %copy.40 = bf16[128,24,2,2,2]{1,4,3,2,0:T(2,128)(2,1)} copy(bf16[128,24,2,2,2]{1,0,4,3,2:T(8,128)(2,1)S(1)} %reshape.190) | data formatting | bytes 98304 | tf_op jit(solution)/shard_map/reshape | solution.py:184
  62.2 4.2 %all-to-all-start.1 = ((bf16[128,24,2,2,2]{1,4,3,2,0:T(2,128)(2,1)}), bf16[128,24,2,2,2]{1,4,3,2,0:T(2,128)(2,1)S(1)}, u32[]{:S(2)}, u32[]{:S(2)}) async-start(bf16[128,24,2,2,2]{1,4,3,2,0:T(2,128)(2,1)} %copy.40), calls=%async_computation.1 | async-start | bytes 524288 | tf_op jit(solution)/shard_map/all_to_all | solution.py:185
  66.4 0.1 copy.39
  66.5 0.8 reshape_reshape.3
  67.3 10.5 %all-to-all-done.1 = bf16[128,24,2,2,2]{1,4,3,2,0:T(2,128)(2,1)S(1)} async-done(((bf16[128,24,2,2,2]{1,4,3,2,0:T(2,128)(2,1)}), bf16[128,24,2,2,2]{1,4,3,2,0:T(2,128)(2,1)S(1)}, u32[]{:S(2)}, u32[]{:S(2)}) %all-to-all-start.1) | async-done | bytes 49184 | tf_op jit(solution)/shard_map/all_to_all | solution.py:185
  77.8 0.1 copy.41
  77.9 0.0 copy-done.2
  77.9 0.2 fusion.33
  78.2 0.1 rev.7
  78.3 0.0 copy-done.3
  78.4 0.6 pad_maximum_fusion.1.both_ref
  79.0 8.6 %shard_map.69 = bf16[24,2,2,2160]{3,2,1,0:T(2,128)(2,1)} custom-call(s32[24]{0:T(128)} %orders_ref.3, bf16[24,8,128]{2,1,0:T(8,128)(2,1)} %pad_maximum_fusion.1.both_ref, bf16[24,2160,128]{2,1,0:T(8,128)(2,1)} %leg_ref.3), custom_call_target="tpu_custom_call" | custom-call | flops 106168320 | bytes 13734912 | tf_op jit(solution)/shard_map/pallas_call | solution.py:92
  (15 shorter events, 0.2 us)
Async XLA Ops:
  1.3 8.7 %copy-start.1 = (s32[256]{0:T(256)S(1)}, s32[256]{0:T(256)}, u32[]{:S(2)}) copy-start(s32[256]{0:T(256)} %param.8) | copy-start | bytes 3076
  11.8 25.4 %all-to-all-start = ((bf16[128,24,10]{1,2,0:T(8,128)(2,1)}), bf16[128,24,10]{1,2,0:T(8,128)(2,1)S(1)}, u32[]{:S(2)}, u32[]{:S(2)}) async-start(bf16[128,24,10]{1,2,0:T(8,128)(2,1)} %copy.36), calls=%async_computation | async-start | bytes 1048576 | tf_op jit(solution)/shard_map/all_to_all | solution.py:175
  55.4 5.4 %copy-start = (f32[3072]{0:T(1024)S(1)}, f32[3072]{0:T(1024)}, u32[]{:S(2)}) copy-start(f32[3072]{0:T(1024)} %select_multiply_fusion) | copy-start | bytes 36868
  55.5 22.5 %copy-start.2 = (s32[256]{0:T(256)S(1)}, s32[256]{0:T(256)}, u32[]{:S(2)}) copy-start(s32[256]{0:T(256)} %param.8) | copy-start | bytes 3076
  55.5 22.9 %copy-start.3 = (f32[128]{0:T(128)S(1)}, f32[128]{0:T(128)}, u32[]{:S(2)}) copy-start(f32[128]{0:T(128)} %param.9) | copy-start | bytes 1540
  62.2 15.6 %all-to-all-start.1 = ((bf16[128,24,2,2,2]{1,4,3,2,0:T(2,128)(2,1)}), bf16[128,24,2,2,2]{1,4,3,2,0:T(2,128)(2,1)S(1)}, u32[]{:S(2)}, u32[]{:S(2)}) async-start(bf16[128,24,2,2,2]{1,4,3,2,0:T(2,128)(2,1)} %copy.40), calls=%async_computation.1 | async-start | bytes 524288 | tf_op jit(solution)/shard_map/all_to_all | solution.py:185

commit v2 on v1

--- a/solution.py
+++ b/solution.py
@@ -110,43 +110,54 @@
     return best
 
 
-def phase_tables(order_vals, stride, count, lon_count):
-    positions = jnp.arange(count, dtype=jnp.int32) * stride
-    phase_int = positions[:, None] * order_vals[None, :] % lon_count
-    angles = phase_int.astype(jnp.float32) * jnp.float32(2.0 * math.pi / lon_count)
-    filled = order_vals[None, :] >= 0
-    cosine = jnp.where(filled, jnp.cos(angles), jnp.float32(0.0))
-    sine_tab = jnp.where(filled, jnp.sin(angles), jnp.float32(0.0))
-    return (cosine, sine_tab)
-
-
 def one_hot_rows(lat_map, lat_rows):
     return (lat_map[None, :] == jnp.arange(lat_rows, dtype=jnp.int32)[:, None]).astype(jnp.bfloat16)
 
 
-def transform_rows(coef, order_vals, lon_count):
-    high = lax.Precision.HIGH
-    inner_len = inner_length(lon_count)
-    outer_len = lon_count // inner_len
-    cos_outer, sin_outer = phase_tables(order_vals, inner_len, outer_len, lon_count)
-    cos_inner, sin_inner = phase_tables(order_vals, 1, inner_len, lon_count)
-    coef_cos = coef[:, 0, :]
-    coef_sin = coef[:, 1, :]
-    y_real = coef_cos.T[:, None, :] * cos_outer[None] + coef_sin.T[:, None, :] * sin_outer[None]
-    y_imag = coef_cos.T[:, None, :] * sin_outer[None] - coef_sin.T[:, None, :] * cos_outer[None]
-    y_both = jnp.concatenate([y_real, y_imag], axis=-1)
-    inner_both = jnp.concatenate([cos_inner, -sin_inner], axis=-1)
-    grid_field = jnp.einsum("ras,bs->rab", y_both, inner_both, precision=high)
-    signals = grid_field.shape[0]
-    squared = (grid_field * grid_field).astype(jnp.bfloat16)
-    sq_wide = squared.astype(jnp.float32)
-    g_real = jnp.einsum("rab,bs->ras", sq_wide, cos_inner, precision=high)
-    g_imag = -jnp.einsum("rab,bs->ras", sq_wide, sin_inner, precision=high)
-    four_cos = jnp.sum(g_real * cos_outer[None] + g_imag * sin_outer[None], axis=1)
-    four_sin = jnp.sum(g_real * sin_outer[None] - g_imag * cos_outer[None], axis=1)
-    scaling = jnp.where(order_vals == 0, 1.0, 2.0).astype(jnp.float32) / lon_count
-    fourier = jnp.stack([four_cos, four_sin], axis=1) * scaling[None, None, :]
-    return squared.reshape(signals, lon_count), fourier
+def angle(numer, denom):
+    return jnp.float32(2.0 * math.pi) * (numer % denom).astype(jnp.float32) / jnp.float32(denom)
+
+
+def transform_dense(dense, lon_count):
+    highest = lax.Precision.HIGHEST
+    deg_count, _, signals = dense.shape
+    inner = inner_length(lon_count)
+    outer = lon_count // inner
+    blocks = deg_count // outer
+    a_idx = jnp.arange(outer, dtype=jnp.int32)
+    b_idx = jnp.arange(inner, dtype=jnp.int32)
+    c_idx = jnp.arange(blocks, dtype=jnp.int32)
+    w1 = angle(b_idx[:, None] * c_idx[None, :], inner)
+    w1c, w1s = jnp.cos(w1), jnp.sin(w1)
+    tw = angle(b_idx[:, None] * a_idx[None, :], lon_count)
+    twc, tws = jnp.cos(tw)[:, :, None], jnp.sin(tw)[:, :, None]
+    w2 = angle(a_idx[:, None] * a_idx[None, :], outer)
+    w2c, w2s = jnp.cos(w2), jnp.sin(w2)
+    x_re = dense[:, 0, :].reshape(blocks, outer, signals)
+    x_im = -dense[:, 1, :].reshape(blocks, outer, signals)
+
+    def mm(spec, left, right):
+        return jnp.einsum(spec, left, right, precision=highest)
+
+    y_re = mm("bc,cdq->bdq", w1c, x_re) - mm("bc,cdq->bdq", w1s, x_im)
+    y_im = mm("bc,cdq->bdq", w1c, x_im) + mm("bc,cdq->bdq", w1s, x_re)
+    t_re = y_re * twc - y_im * tws
+    t_im = y_re * tws + y_im * twc
+    field = mm("ad,bdq->abq", w2c, t_re) - mm("ad,bdq->abq", w2s, t_im)
+    squared = (field * field).astype(jnp.bfloat16)
+    sq = squared.astype(jnp.float32)
+    z_re = mm("da,abq->bdq", w2c, sq)
+    z_im = -mm("da,abq->bdq", w2s, sq)
+    u_re = z_re * twc + z_im * tws
+    u_im = z_im * twc - z_re * tws
+    f_re = mm("bc,bdq->cdq", w1c, u_re) + mm("bc,bdq->cdq", w1s, u_im)
+    f_im = mm("bc,bdq->cdq", w1c, u_im) - mm("bc,bdq->cdq", w1s, u_re)
+    m_idx = jnp.arange(deg_count, dtype=jnp.int32)
+    scaling = jnp.where(m_idx == 0, 1.0, 2.0).astype(jnp.float32)[:, None] / lon_count
+    four_cos = f_re.reshape(deg_count, signals) * scaling
+    four_sin = -f_im.reshape(deg_count, signals) * scaling
+    grid = jnp.transpose(squared, (2, 0, 1)).reshape(signals, lon_count)
+    return grid, jnp.stack([four_cos, four_sin], axis=1)
 
 
 def shards(coeffs, legendre, orders, lat_map, weights):
@@ -176,14 +187,20 @@
     got = got.reshape(devices * slot_cap, -1)
     code = got[:, -2:].astype(jnp.int32)
     all_orders = code[:, 0] * ORDER_BASE + code[:, 1] - 1
-    received = got[:, :-2].reshape(devices * slot_cap, epoch_count, 2, rows_each)
-    coef = jnp.transpose(received, (0, 2, 3, 1)).reshape(devices * slot_cap, 2, rows_each * epoch_count)
-    squared, fourier = transform_rows(coef.astype(jnp.float32), all_orders, lon_count)
-    grid_rows = squared.reshape(rows_each, epoch_count, lon_count)
-
-    back = jnp.transpose(fourier, (2, 1, 0)).astype(jnp.bfloat16).reshape(devices, slot_cap, 2, rows_each, epoch_count)
+    data = got[:, :-2]
+    dense_map = (all_orders[:, None] == jnp.arange(deg_count, dtype=jnp.int32)[None, :]).astype(jnp.bfloat16)
+    dense = jnp.einsum("sm,sr->mr", dense_map, data, preferred_element_type=jnp.float32)
+    dense = dense.reshape(deg_count, epoch_count, 2, rows_each)
+    dense = jnp.transpose(dense, (0, 2, 1, 3)).reshape(deg_count, 2, epoch_count * rows_each)
+    grid, fourier = transform_dense(dense, lon_count)
+    grid_rows = jnp.transpose(grid.reshape(epoch_count, rows_each, lon_count), (1, 0, 2))
+
+    fourier = fourier.astype(jnp.bfloat16).reshape(deg_count, 2, epoch_count, rows_each)
+    fourier = jnp.transpose(fourier, (0, 2, 1, 3)).reshape(deg_count, -1)
+    by_slot = jnp.einsum("sm,mr->sr", dense_map, fourier, preferred_element_type=jnp.float32)
+    back = by_slot.astype(jnp.bfloat16).reshape(devices, slot_cap, epoch_count, 2, rows_each)
     back = lax.all_to_all(back, ("gx", "gy"), 0, 0, tiled=True)
-    returned = jnp.transpose(back, (1, 4, 2, 0, 3)).reshape(slot_cap, epoch_count * 2, lat_rows)
+    returned = jnp.transpose(back, (1, 2, 3, 0, 4)).reshape(slot_cap, epoch_count * 2, lat_rows)
     natural = jnp.einsum(
         "sxr,kr->sxk", returned, onehot, preferred_element_type=jnp.float32
     )

time: 88 us -> 80.1 us (0.910)
  other arithmetic: 10 us -> 1.85 us
    select_n x2 -> x0, other arithmetic: 6.91 us -> none  [phase_tables(): cosine = jnp.where(filled, jnp.cos(angles), jnp.float32(0.0))]
    add x1 -> x0, other arithmetic: 1.05 us -> none  [transform_rows(): coef_cos.T[:, None, :] * cos_outer[None]]
    dot_general x3 -> x14, matrix products: 14.1 us -> 14.3 us  [the longest x1 5.37 us: shards(): jnp.einsum('sm,mr->sr', dense_map, fourier, preferred_element_type=jnp.fl...]
where the time goes in v2:
time: 80.1 us; the launch traced here: 79.8 us
  waiting for transfers between devices  24.2 us (30%)
  Pallas kernels  16.3 us (20%)
  starting transfers between devices  15.7 us (20%)
  matrix products  14.7 us (18%)
  local copies, waits for them, and re-layouts  6.17 us (8%)
  other arithmetic  1.85 us (2%)
  between operations  0.95 us (1%)
    all_to_all x1, waiting for transfers between devices, shards(): got = lax.all_to_all(payload, ('gx', 'gy'), 0, 0, tiled=True)  13.7 us
    all_to_all x1, starting transfers between devices, shards(): got = lax.all_to_all(payload, ('gx', 'gy'), 0, 0, tiled=True)  11.5 us
    all_to_all x1, waiting for transfers between devices, shards(): back = lax.all_to_all(back, ('gx', 'gy'), 0, 0, tiled=True)  10.5 us
    pallas_call x1, Pallas kernels, analyze(): pl.pallas_call(_analysis_kernel, grid_spec=grid_spec, out_shape=jax.Shape...  8.61 us
    pallas_call x1, Pallas kernels, synthesize(): pl.pallas_call(_synth_kernel, grid_spec=grid_spec, out_shape=jax.ShapeDty...  7.69 us
    dot_general x1, matrix products, shards(): jnp.einsum('sm,mr->sr', dense_map, fourier, preferred_element_type=jnp.fl...  5.37 us
    dot_general x1, matrix products, shards(): jnp.einsum('sm,sr->mr', dense_map, data, preferred_element_type=jnp.float32)  4.48 us
    dot_general x12, matrix products, mm(): return jnp.einsum(spec, left, right, precision=highest)  4.42 us
  transfers between devices with their start and end apart: 2, of which 2 were waited for; matrix products, arithmetic and copies ran while one was open for 1% of the time, Pallas kernels for 0%

profile of v2, /device:TPU:1, one launch (start us, length us, event | category | flops | bytes accessed | tf_op | source)
XLA Modules:
  0.0 79.8 jit_solution(11773036402902604009)
XLA Ops:
  0.6 0.7 convert_bitcast_fusion
  1.3 7.7 %shard_map.68 = bf16[24,8,128]{2,1,0:T(8,128)(2,1)} custom-call(s32[24]{0:T(128)} %orders_ref.3, bf16[24,2,2,2160]{3,2,1,0:T(2,128)(2,1)} %coef_ref.1, bf16[24,2160,128]{2,1,0:T(8,128)(2,1)} %leg_ref.3), custom_call_target="tpu_custom_call" | custom-call | flops 106168320 | bytes 13734912 | tf_op jit(solution)/shard_map/pallas_call | solution.py:50
  9.0 0.8 fusion.161
  9.8 0.1 rev.6
  9.9 0.2 convolution_convert_fusion
  10.1 0.2 copy.40
  10.3 0.1 copy.41
  10.4 0.1 broadcast_in_dim.8
  10.5 0.0 copy-start.1
  10.5 1.2 %copy.42 = bf16[128,24,10]{1,2,0:T(8,128)(2,1)} copy(bf16[128,24,10]{0,1,2:T(8,128)(2,1)S(1)} %pad_maximum_fusion) | data formatting | bytes 122880 | tf_op jit(solution)/shard_map/concatenate | solution.py:185
  11.7 11.5 %all-to-all-start = ((bf16[128,24,10]{1,2,0:T(8,128)(2,1)}), bf16[128,24,10]{1,2,0:T(8,128)(2,1)S(1)}, u32[]{:S(2)}, u32[]{:S(2)}) async-start(bf16[128,24,10]{1,2,0:T(8,128)(2,1)} %copy.42), calls=%async_computation | async-start | bytes 1048576 | tf_op jit(solution)/shard_map/all_to_all | solution.py:186
  23.2 0.2 fusion.56
  23.4 13.7 %all-to-all-done = bf16[128,24,10]{1,2,0:T(8,128)(2,1)S(1)} async-done(((bf16[128,24,10]{1,2,0:T(8,128)(2,1)}), bf16[128,24,10]{1,2,0:T(8,128)(2,1)S(1)}, u32[]{:S(2)}, u32[]{:S(2)}) %all-to-all-start) | async-done | bytes 61472 | tf_op jit(solution)/shard_map/all_to_all | solution.py:186
  37.1 0.1 copy.43
  37.2 0.4 reshape.149
  37.7 4.5 %fusion.1 = f32[2160,8]{0,1:T(8,128)S(1)} fusion(s32[3072]{0:T(1024)S(1)} %bitcast.99, bf16[3072,10]{0,1:T(8,128)(2,1)S(1)} %reshape.149), kind=kOutput, calls=%fused_computation.2 | convolution fusion | flops 112803840 | bytes 130560 | tf_op jit(solution)/shard_map/sm,sr->mr/dot_general | solution.py:192
  42.2 0.1 reshape.150
  42.3 0.2 slice_reduce_fusion
  42.5 0.1 reshape_squeeze.4
  42.6 0.4 fusion.81
  43.0 0.1 neg.25
  43.1 0.4 fusion.79
  43.5 0.4 convolution_subtract_fusion.1
  43.9 0.4 convolution_add_fusion
  44.3 0.4 fusion.21
  44.7 0.4 fusion.6
  45.2 0.4 convolution_negate_fusion
  45.5 0.4 fusion.39
  45.9 0.3 fusion.12
  46.2 0.3 fusion.16
  46.5 0.3 fusion.7
  46.9 0.1 neg.28
  47.0 0.3 convolution_add_fusion.1
  47.3 0.1 reshape.152
  47.4 0.1 maximum_bitcast_fusion
  47.6 5.4 %fusion.4 = bf16[3072,8]{0,1:T(8,128)(2,1)S(1)} fusion(bf16[2160,8]{0,1:T(8,128)(2,1)S(1)} %reshape.153, s32[3072]{0:T(1024)S(1)} %bitcast.100), kind=kOutput, calls=%fused_computation.5 | convolution fusion | flops 112828416 | bytes 96000 | tf_op jit(solution)/shard_map/sm,mr->sr/dot_general | solution.py:200
  52.9 0.4 reshape.154
  53.3 1.0 %copy.47 = bf16[128,24,2,2,2]{1,4,3,2,0:T(2,128)(2,1)} copy(bf16[128,24,2,2,2]{1,0,4,3,2:T(8,128)(2,1)S(1)} %reshape.154) | data formatting | bytes 98304 | tf_op jit(solution)/shard_map/reshape | solution.py:201
  54.3 4.2 %all-to-all-start.1 = ((bf16[128,24,2,2,2]{1,4,3,2,0:T(2,128)(2,1)}), bf16[128,24,2,2,2]{1,4,3,2,0:T(2,128)(2,1)S(1)}, u32[]{:S(2)}, u32[]{:S(2)}) async-start(bf16[128,24,2,2,2]{1,4,3,2,0:T(2,128)(2,1)} %copy.47), calls=%async_computation.1 | async-start | bytes 524288 | tf_op jit(solution)/shard_map/all_to_all | solution.py:202
  58.5 0.1 copy.45
  58.7 0.2 reshape_reshape.3
  58.8 0.6 copy.52
  59.5 10.5 %all-to-all-done.1 = bf16[128,24,2,2,2]{1,4,3,2,0:T(2,128)(2,1)S(1)} async-done(((bf16[128,24,2,2,2]{1,4,3,2,0:T(2,128)(2,1)}), bf16[128,24,2,2,2]{1,4,3,2,0:T(2,128)(2,1)S(1)}, u32[]{:S(2)}, u32[]{:S(2)}) %all-to-all-start.1) | async-done | bytes 49184 | tf_op jit(solution)/shard_map/all_to_all | solution.py:202
  69.9 0.2 copy.48
  70.1 0.2 fusion.9
  70.4 0.1 rev.7
  70.5 0.6 pad_maximum_fusion.1.both_ref
  71.2 8.6 %shard_map.69 = bf16[24,2,2,2160]{3,2,1,0:T(2,128)(2,1)} custom-call(s32[24]{0:T(128)} %orders_ref.3, bf16[24,8,128]{2,1,0:T(8,128)(2,1)} %pad_maximum_fusion.1.both_ref, bf16[24,2160,128]{2,1,0:T(8,128)(2,1)} %leg_ref.3), custom_call_target="tpu_custom_call" | custom-call | flops 106168320 | bytes 13734912 | tf_op jit(solution)/shard_map/pallas_call | solution.py:92
  (18 shorter events, 0.3 us)
Async XLA Ops:
  0.6 9.3 %copy-start = (s32[256]{0:T(256)S(1)}, s32[256]{0:T(256)}, u32[]{:S(2)}) copy-start(s32[256]{0:T(256)} %param.8) | copy-start | bytes 3076
  10.5 60.0 %copy-start.1 = (f32[128]{0:T(128)S(1)}, f32[128]{0:T(128)}, u32[]{:S(2)}) copy-start(f32[128]{0:T(128)} %param.9) | copy-start | bytes 1540
  11.7 25.4 %all-to-all-start = ((bf16[128,24,10]{1,2,0:T(8,128)(2,1)}), bf16[128,24,10]{1,2,0:T(8,128)(2,1)S(1)}, u32[]{:S(2)}, u32[]{:S(2)}) async-start(bf16[128,24,10]{1,2,0:T(8,128)(2,1)} %copy.42), calls=%async_computation | async-start | bytes 1048576 | tf_op jit(solution)/shard_map/all_to_all | solution.py:186
  54.3 15.6 %all-to-all-start.1 = ((bf16[128,24,2,2,2]{1,4,3,2,0:T(2,128)(2,1)}), bf16[128,24,2,2,2]{1,4,3,2,0:T(2,128)(2,1)S(1)}, u32[]{:S(2)}, u32[]{:S(2)}) async-start(bf16[128,24,2,2,2]{1,4,3,2,0:T(2,128)(2,1)} %copy.47), calls=%async_computation.1 | async-start | bytes 524288 | tf_op jit(solution)/shard_map/all_to_all | solution.py:202

commit v3 on v2

--- a/solution.py
+++ b/solution.py
@@ -7,7 +7,6 @@
 from jax.experimental.pallas import tpu as pltpu
 from jax.sharding import PartitionSpec as P
 
-ORDER_BASE = 64
 
 SLOTS_PER_STEP = 6
 
@@ -118,12 +117,10 @@
     return jnp.float32(2.0 * math.pi) * (numer % denom).astype(jnp.float32) / jnp.float32(denom)
 
 
-def transform_dense(dense, lon_count):
+def transform_blocks(x_parts, lon_count):
     highest = lax.Precision.HIGHEST
-    deg_count, _, signals = dense.shape
-    inner = inner_length(lon_count)
-    outer = lon_count // inner
-    blocks = deg_count // outer
+    _, outer, blocks, signals = x_parts.shape
+    inner = lon_count // outer
     a_idx = jnp.arange(outer, dtype=jnp.int32)
     b_idx = jnp.arange(inner, dtype=jnp.int32)
     c_idx = jnp.arange(blocks, dtype=jnp.int32)
@@ -133,31 +130,28 @@
     twc, tws = jnp.cos(tw)[:, :, None], jnp.sin(tw)[:, :, None]
     w2 = angle(a_idx[:, None] * a_idx[None, :], outer)
     w2c, w2s = jnp.cos(w2), jnp.sin(w2)
-    x_re = dense[:, 0, :].reshape(blocks, outer, signals)
-    x_im = -dense[:, 1, :].reshape(blocks, outer, signals)
 
     def mm(spec, left, right):
         return jnp.einsum(spec, left, right, precision=highest)
 
-    y_re = mm("bc,cdq->bdq", w1c, x_re) - mm("bc,cdq->bdq", w1s, x_im)
-    y_im = mm("bc,cdq->bdq", w1c, x_im) + mm("bc,cdq->bdq", w1s, x_re)
-    t_re = y_re * twc - y_im * tws
-    t_im = y_re * tws + y_im * twc
-    field = mm("ad,bdq->abq", w2c, t_re) - mm("ad,bdq->abq", w2s, t_im)
+    rot1 = jnp.stack([jnp.stack([w1c, -w1s]), jnp.stack([w1s, w1c])])
+    y = mm("kjbc,jdcq->kbdq", rot1, x_parts)
+    t_re = y[0] * twc - y[1] * tws
+    t_im = y[0] * tws + y[1] * twc
+    field = mm("jad,jbdq->abq", jnp.stack([w2c, -w2s]), jnp.stack([t_re, t_im]))
     squared = (field * field).astype(jnp.bfloat16)
     sq = squared.astype(jnp.float32)
-    z_re = mm("da,abq->bdq", w2c, sq)
-    z_im = -mm("da,abq->bdq", w2s, sq)
-    u_re = z_re * twc + z_im * tws
-    u_im = z_im * twc - z_re * tws
-    f_re = mm("bc,bdq->cdq", w1c, u_re) + mm("bc,bdq->cdq", w1s, u_im)
-    f_im = mm("bc,bdq->cdq", w1c, u_im) - mm("bc,bdq->cdq", w1s, u_re)
-    m_idx = jnp.arange(deg_count, dtype=jnp.int32)
-    scaling = jnp.where(m_idx == 0, 1.0, 2.0).astype(jnp.float32)[:, None] / lon_count
-    four_cos = f_re.reshape(deg_count, signals) * scaling
-    four_sin = -f_im.reshape(deg_count, signals) * scaling
+    z = mm("kda,abq->kbdq", jnp.stack([w2c, -w2s]), sq)
+    u_re = z[0] * twc + z[1] * tws
+    u_im = z[1] * twc - z[0] * tws
+    rot2 = jnp.stack([jnp.stack([w1c, w1s]), jnp.stack([-w1s, w1c])])
+    f = mm("kjbc,jbdq->kcdq", rot2, jnp.stack([u_re, u_im]))
+    first = (c_idx[:, None] == 0) & (a_idx[None, :] == 0)
+    scaling = jnp.where(first, 1.0, 2.0).astype(jnp.float32)[:, :, None] / lon_count
+    four_cos = f[0] * scaling
+    four_sin = -f[1] * scaling
     grid = jnp.transpose(squared, (2, 0, 1)).reshape(signals, lon_count)
-    return grid, jnp.stack([four_cos, four_sin], axis=1)
+    return grid, four_cos, four_sin
 
 
 def shards(coeffs, legendre, orders, lat_map, weights):
@@ -179,27 +173,41 @@
     ).astype(jnp.bfloat16)
     sends = permuted.reshape(slot_cap, epoch_count * 2, devices, rows_each)
     sends = jnp.transpose(sends, (2, 0, 1, 3)).reshape(devices, slot_cap, epoch_count * 2 * rows_each)
-    coded = orders + 1
-    order_code = jnp.stack([coded // ORDER_BASE, coded % ORDER_BASE], axis=-1).astype(jnp.bfloat16)
+    inner = inner_length(lon_count)
+    outer = lon_count // inner
+    blocks = deg_count // outer
+    block_of = jnp.where(orders >= 0, orders // outer, -1)
+    order_code = jnp.stack([block_of, orders % outer], axis=-1).astype(jnp.bfloat16)
     order_code = jnp.broadcast_to(order_code[None], (devices, slot_cap, 2))
-    payload = jnp.concatenate([sends, order_code], axis=-1)
+    payload = jnp.concatenate([sends, order_code], axis=-1).reshape(devices, -1)
+    width = payload.shape[1]
+    padded = -(-width // 256) * 256
+    payload = jnp.pad(payload, ((0, 0), (0, padded - width))).reshape(devices, padded // 128, 128)
     got = lax.all_to_all(payload, ("gx", "gy"), 0, 0, tiled=True)
-    got = got.reshape(devices * slot_cap, -1)
+    got = got.reshape(devices, padded)[:, :width].reshape(devices * slot_cap, -1)
     code = got[:, -2:].astype(jnp.int32)
-    all_orders = code[:, 0] * ORDER_BASE + code[:, 1] - 1
     data = got[:, :-2]
-    dense_map = (all_orders[:, None] == jnp.arange(deg_count, dtype=jnp.int32)[None, :]).astype(jnp.bfloat16)
-    dense = jnp.einsum("sm,sr->mr", dense_map, data, preferred_element_type=jnp.float32)
-    dense = dense.reshape(deg_count, epoch_count, 2, rows_each)
-    dense = jnp.transpose(dense, (0, 2, 1, 3)).reshape(deg_count, 2, epoch_count * rows_each)
-    grid, fourier = transform_dense(dense, lon_count)
+    by_d = (code[:, 1:2] == jnp.arange(outer, dtype=jnp.int32)[None, :]).astype(jnp.bfloat16)
+    in_c = code[:, 0:1] == jnp.arange(blocks, dtype=jnp.int32)[None, :]
+    spread = jnp.where(in_c[:, :, None], data[:, None, :], jnp.zeros((), jnp.bfloat16))
+    dense = jnp.einsum("sd,scr->dcr", by_d, spread, preferred_element_type=jnp.float32)
+    dense = dense.reshape(outer, blocks, epoch_count, 2, rows_each)
+    x_parts = jnp.stack([dense[:, :, :, 0, :], -dense[:, :, :, 1, :]])
+    x_parts = x_parts.reshape(2, outer, blocks, epoch_count * rows_each)
+    grid, four_cos, four_sin = transform_blocks(x_parts, lon_count)
     grid_rows = jnp.transpose(grid.reshape(epoch_count, rows_each, lon_count), (1, 0, 2))
 
-    fourier = fourier.astype(jnp.bfloat16).reshape(deg_count, 2, epoch_count, rows_each)
-    fourier = jnp.transpose(fourier, (0, 2, 1, 3)).reshape(deg_count, -1)
-    by_slot = jnp.einsum("sm,mr->sr", dense_map, fourier, preferred_element_type=jnp.float32)
-    back = by_slot.astype(jnp.bfloat16).reshape(devices, slot_cap, epoch_count, 2, rows_each)
+    split = (blocks, outer, epoch_count, rows_each)
+    fourier = jnp.stack([four_cos.reshape(split), four_sin.reshape(split)], axis=3)
+    fourier = fourier.astype(jnp.bfloat16).reshape(blocks, outer, -1)
+    picked = jnp.einsum("sd,cdr->scr", by_d, fourier, preferred_element_type=jnp.float32)
+    by_slot = jnp.sum(jnp.where(in_c[:, :, None], picked, jnp.float32(0.0)), axis=1)
+    back = by_slot.astype(jnp.bfloat16).reshape(devices, -1)
+    width = back.shape[1]
+    padded = -(-width // 256) * 256
+    back = jnp.pad(back, ((0, 0), (0, padded - width))).reshape(devices, padded // 128, 128)
     back = lax.all_to_all(back, ("gx", "gy"), 0, 0, tiled=True)
+    back = back.reshape(devices, padded)[:, :width].reshape(devices, slot_cap, epoch_count, 2, rows_each)
     returned = jnp.transpose(back, (1, 2, 3, 0, 4)).reshape(slot_cap, epoch_count * 2, lat_rows)
     natural = jnp.einsum(
         "sxr,kr->sxk", returned, onehot, preferred_element_type=jnp.float32

time: 80.1 us -> 63.9 us (0.80)
  matrix products: 14.7 us -> 3.1 us
  waiting for transfers between devices: 24.2 us -> 17.5 us
  local copies, waits for them, and re-layouts: 6.17 us -> 7.13 us
    dot_general x2, matrix products: 9.86 us -> 1.29 us  [the longest x1 0.71 us: shards(): jnp.einsum('sd,cdr->scr', by_d, fourier, preferred_element_type=jnp.float32)]
    all_to_all x1, waiting for transfers between devices: 13.7 us -> 8.87 us  [shards(): got = lax.all_to_all(payload, ('gx', 'gy'), 0, 0, tiled=True)]
    dot_general x12 -> x4, matrix products: 4.42 us -> 1.42 us  [mm(): return jnp.einsum(spec, left, right, precision=highest)]
    all_to_all x1, waiting for transfers between devices: 10.5 us -> 8.59 us  [shards(): back = lax.all_to_all(back, ('gx', 'gy'), 0, 0, tiled=True)]
    slice x0 -> x3, local copies, waits for them, and re-layouts: none -> 1.55 us  [the longest x1 1.31 us: shards(): code[:, 1:2] == jnp.arange(outer, dtype=jnp.int32)[None, :]]
    concatenate x1, local copies, waits for them, and re-layouts: 1.19 us -> 0.02 us  [shards(): payload = jnp.concatenate([sends, order_code], axis=-1).reshape(devices, -1)]
    convert_element_type x1 -> x3, local copies, waits for them, and re-layouts: 0.13 us -> 0.99 us  [the longest x2 0.86 us: shards(): back = by_slot.astype(jnp.bfloat16).reshape(devices, -1)]
    reshape x7 -> x4, local copies, waits for them, and re-layouts: 2.04 us -> 2.04 us  [the longest x1 0.76 us: shards(): jnp.pad(payload, ((0, 0), (0, padded - width)))]
  transfers between devices with their start and end apart: 2 -> 2, of which waited for: 2 -> 2; matrix products, arithmetic and copies ran while one was open for 1% -> 2% of each run, Pallas kernels for 0% -> 0%
where the time goes in v3:
time: 63.9 us; the launch traced here: 63.6 us
  waiting for transfers between devices  17.5 us (27%)
  Pallas kernels  16.4 us (26%)
  starting transfers between devices  16 us (25%)
  local copies, waits for them, and re-layouts  7.13 us (11%)
  matrix products  3.1 us (5%)
  other arithmetic  2.52 us (4%)
  between operations  0.98 us (2%)
    all_to_all x1, starting transfers between devices, shards(): got = lax.all_to_all(payload, ('gx', 'gy'), 0, 0, tiled=True)  11.5 us
    all_to_all x1, waiting for transfers between devices, shards(): got = lax.all_to_all(payload, ('gx', 'gy'), 0, 0, tiled=True)  8.87 us
    pallas_call x1, Pallas kernels, analyze(): pl.pallas_call(_analysis_kernel, grid_spec=grid_spec, out_shape=jax.Shape...  8.61 us
    all_to_all x1, waiting for transfers between devices, shards(): back = lax.all_to_all(back, ('gx', 'gy'), 0, 0, tiled=True)  8.59 us
    pallas_call x1, Pallas kernels, synthesize(): pl.pallas_call(_synth_kernel, grid_spec=grid_spec, out_shape=jax.ShapeDty...  7.83 us
    all_to_all x1, starting transfers between devices, shards(): back = lax.all_to_all(back, ('gx', 'gy'), 0, 0, tiled=True)  4.48 us
    dot_general x4, matrix products, mm(): return jnp.einsum(spec, left, right, precision=highest)  1.42 us
    slice x1, local copies, waits for them, and re-layouts, shards(): code[:, 1:2] == jnp.arange(outer, dtype=jnp.int32)[None, :]  1.31 us
  transfers between devices with their start and end apart: 2, of which 2 were waited for; matrix products, arithmetic and copies ran while one was open for 2% of the time, Pallas kernels for 0%

profile of v3, /device:TPU:1, one launch (start us, length us, event | category | flops | bytes accessed | tf_op | source)
XLA Modules:
  0.0 63.6 jit_solution(1637114815747798512)
XLA Ops:
  0.6 0.7 %convert_bitcast_fusion = (bf16[24,1]{0,1:T(2,128)(2,1)S(1)}, bf16[24,1]{0,1:T(2,128)(2,1)S(1)}) fusion(s32[24]{0:T(128)} %orders_ref.3), kind=kLoop, calls=%fused_computation.109 | loop fusion | flops 384 | bytes 192 | tf_op jit(solution)/shard_map/stack | solution.py:180
  1.3 0.0 copy-start
  1.3 7.8 %shard_map.68 = bf16[24,8,128]{2,1,0:T(8,128)(2,1)} custom-call(s32[24]{0:T(128)} %orders_ref.3, bf16[24,2,2,2160]{3,2,1,0:T(2,128)(2,1)} %coef_ref.1, bf16[24,2160,128]{2,1,0:T(8,128)(2,1)} %leg_ref.3), custom_call_target="tpu_custom_call" | custom-call | flops 106168320 | bytes 13734912 | tf_op jit(solution)/shard_map/pallas_call | solution.py:49
  9.1 0.8 %fusion.72 = (bf16[24,1,4,128]{3,2,1,0:T(4,128)(2,1)S(1)}, bf16[24,1,4,128]{3,2,1,0:T(4,128)(2,1)S(1)}) fusion(bf16[24,2,4,128]{3,2,1,0:T(4,128)(2,1)} %bitcast.110), kind=kLoop, calls=%fused_computation.119 | loop fusion | bytes 98304 | tf_op jit(solution)/shard_map/slice | solution.py:168
  9.9 0.1 rev.6
  10.0 0.0 copy-done
  10.0 0.2 convolution_convert_fusion
  10.2 0.2 copy.54
  10.4 0.1 copy.55
  10.5 0.1 broadcast_in_dim.36
  10.7 0.8 %copy.57 = bf16[128,2,128]{2,1,0:T(2,128)(2,1)} copy(bf16[128,2,128]{0,2,1:T(8,128)(2,1)S(1)} %bitcast.105) | data formatting | bytes 131072 | tf_op jit(solution)/shard_map/reshape | solution.py:185
  11.5 11.5 %all-to-all-start = ((bf16[128,2,128]{2,1,0:T(2,128)(2,1)}), bf16[128,2,128]{2,1,0:T(2,128)(2,1)S(1)}, u32[]{:S(2)}, u32[]{:S(2)}) async-start(bf16[128,2,128]{2,1,0:T(2,128)(2,1)} %copy.57), calls=%async_computation | async-start | bytes 131072 | tf_op jit(solution)/shard_map/all_to_all | solution.py:186
  23.0 0.1 fusion.57
  23.1 0.1 fusion.60
  23.2 0.2 sine_negate_fusion
  23.4 0.1 select_multiply_fusion
  23.4 0.2 fusion.50
  23.6 8.9 %all-to-all-done = bf16[128,2,128]{2,1,0:T(2,128)(2,1)S(1)} async-done(((bf16[128,2,128]{2,1,0:T(2,128)(2,1)}), bf16[128,2,128]{2,1,0:T(2,128)(2,1)S(1)}, u32[]{:S(2)}, u32[]{:S(2)}) %all-to-all-start) | async-done | bytes 65568 | tf_op jit(solution)/shard_map/all_to_all | solution.py:186
  32.5 0.6 reshape.326
  33.1 0.4 slice_convert_fusion
  33.5 1.3 %slice_reduce_fusion.1 = (s32[3072]{0:T(1024)S(1)}, s32[3072]{0:T(1024)S(1)}) fusion(s32[3072,2]{1,0:T(8,128)S(1)} %slice_convert_fusion), kind=kLoop, calls=%fused_computation.2 | loop fusion | bytes 49152 | tf_op jit(solution)/shard_map/slice | solution.py:190
  34.8 0.1 iota_compare_fusion.1
  34.8 0.2 copy.58
  35.1 0.6 fusion
  35.7 0.4 convolution_bitcast_fusion.1
  36.2 0.4 fusion.5
  36.5 0.3 convolution_bitcast_fusion
  36.9 0.3 convolution_bitcast_fusion.3
  37.3 0.7 %fusion.3 = bf16[3072,8]{0,1:T(8,128)(2,1)S(1)} fusion(bf16[30,72,8]{1,0,2:T(8,128)(2,1)S(1)} %bitcast.115, pred[3072,30]{0,1:T(8,128)(4,1)S(1)} %iota_compare_fusion.1, s32[3072]{0:T(1024)S(1)} %get-tuple-element.8), kind=kOutput, calls=%fused_computation.6 | convolution fusion | flops 107839488 | bytes 188160 | tf_op jit(solution)/shard_map/sd,cdr->scr/dot_general | solution.py:203
  38.0 0.4 copy.64
  38.4 0.0 copy-start.1
  38.4 0.5 convert_element_type.124
  38.9 0.7 %reshape.328 = bf16[128,2,128]{2,1,0:T(2,128)(2,1)} reshape(bf16[128,256]{1,0:T(8,128)(2,1)S(1)} %pad.9) | data formatting | bytes 131072 | tf_op jit(solution)/shard_map/reshape | solution.py:208
  39.6 4.5 %all-to-all-start.1 = ((bf16[128,2,128]{2,1,0:T(2,128)(2,1)}), bf16[128,2,128]{2,1,0:T(2,128)(2,1)S(1)}, u32[]{:S(2)}, u32[]{:S(2)}) async-start(bf16[128,2,128]{2,1,0:T(2,128)(2,1)} %reshape.328), calls=%async_computation.1 | async-start | bytes 131072 | tf_op jit(solution)/shard_map/all_to_all | solution.py:209
  44.1 0.1 copy.60
  44.2 0.2 reshape_reshape.3
  44.4 0.6 %copy.70 = bf16[2,2,4320]{2,1,0:T(2,128)(2,1)} copy(bf16[2,2,4320]{2,0,1:T(2,128)(2,1)S(1)} %bitcast.113) | data formatting | bytes 69120
  45.0 8.6 %all-to-all-done.1 = bf16[128,2,128]{2,1,0:T(2,128)(2,1)S(1)} async-done(((bf16[128,2,128]{2,1,0:T(2,128)(2,1)}), bf16[128,2,128]{2,1,0:T(2,128)(2,1)S(1)}, u32[]{:S(2)}, u32[]{:S(2)}) %all-to-all-start.1) | async-done | bytes 65568 | tf_op jit(solution)/shard_map/all_to_all | solution.py:209
  53.6 0.1 copy.65
  53.7 0.2 copy.66
  53.9 0.2 fusion.19
  54.2 0.1 rev.7
  54.3 0.0 copy-done.1
  54.3 0.6 %pad_maximum_fusion.6.both_ref = bf16[24,8,128]{2,1,0:T(8,128)(2,1)} fusion(bf16[24,4,128]{2,1,0:T(4,128)(2,1)S(1)} %get-tuple-element.19, bf16[24,4,128]{2,1,0:T(4,128)(2,1)S(1)} %get-tuple-element.18), kind=kLoop, calls=%fused_computation.61 | loop fusion | flops 98304 | bytes 98304 | tf_op jit(solution)/shard_map/concatenate | solution.py:219
  55.0 8.6 %shard_map.69 = bf16[24,2,2,2160]{3,2,1,0:T(2,128)(2,1)} custom-call(s32[24]{0:T(128)} %orders_ref.3, bf16[24,8,128]{2,1,0:T(8,128)(2,1)} %pad_maximum_fusion.6.both_ref, bf16[24,2160,128]{2,1,0:T(8,128)(2,1)} %leg_ref.3), custom_call_target="tpu_custom_call" | custom-call | flops 106168320 | bytes 13734912 | tf_op jit(solution)/shard_map/pallas_call | solution.py:91
  (23 shorter events, 0.3 us)
Async XLA Ops:
  1.3 8.7 %copy-start = (s32[256]{0:T(256)S(1)}, s32[256]{0:T(256)}, u32[]{:S(2)}) copy-start(s32[256]{0:T(256)} %param.8) | copy-start | bytes 3076
  11.5 21.0 %all-to-all-start = ((bf16[128,2,128]{2,1,0:T(2,128)(2,1)}), bf16[128,2,128]{2,1,0:T(2,128)(2,1)S(1)}, u32[]{:S(2)}, u32[]{:S(2)}) async-start(bf16[128,2,128]{2,1,0:T(2,128)(2,1)} %copy.57), calls=%async_computation | async-start | bytes 131072 | tf_op jit(solution)/shard_map/all_to_all | solution.py:186
  38.4 15.9 %copy-start.1 = (f32[128]{0:T(128)S(1)}, f32[128]{0:T(128)}, u32[]{:S(2)}) copy-start(f32[128]{0:T(128)} %param.9) | copy-start | bytes 1540
  39.6 14.0 %all-to-all-start.1 = ((bf16[128,2,128]{2,1,0:T(2,128)(2,1)}), bf16[128,2,128]{2,1,0:T(2,128)(2,1)S(1)}, u32[]{:S(2)}, u32[]{:S(2)}) async-start(bf16[128,2,128]{2,1,0:T(2,128)(2,1)} %reshape.328), calls=%async_computation.1 | async-start | bytes 131072 | tf_op jit(solution)/shard_map/all_to_all | solution.py:209

commit v4 on v3

--- a/solution.py
+++ b/solution.py
@@ -8,7 +8,7 @@
 from jax.sharding import PartitionSpec as P
 
 
-SLOTS_PER_STEP = 6
+SLOTS_PER_STEP = 12
 
 
 def _masks(order, deg_count):
@@ -185,20 +185,20 @@
     payload = jnp.pad(payload, ((0, 0), (0, padded - width))).reshape(devices, padded // 128, 128)
     got = lax.all_to_all(payload, ("gx", "gy"), 0, 0, tiled=True)
     got = got.reshape(devices, padded)[:, :width].reshape(devices * slot_cap, -1)
-    code = got[:, -2:].astype(jnp.int32)
     data = got[:, :-2]
-    by_d = (code[:, 1:2] == jnp.arange(outer, dtype=jnp.int32)[None, :]).astype(jnp.bfloat16)
-    in_c = code[:, 0:1] == jnp.arange(blocks, dtype=jnp.int32)[None, :]
+    by_d = (got[:, -1:] == jnp.arange(outer, dtype=jnp.bfloat16)[None, :]).astype(jnp.bfloat16)
+    in_c = got[:, -2:-1] == jnp.arange(blocks, dtype=jnp.bfloat16)[None, :]
     spread = jnp.where(in_c[:, :, None], data[:, None, :], jnp.zeros((), jnp.bfloat16))
     dense = jnp.einsum("sd,scr->dcr", by_d, spread, preferred_element_type=jnp.float32)
     dense = dense.reshape(outer, blocks, epoch_count, 2, rows_each)
     x_parts = jnp.stack([dense[:, :, :, 0, :], -dense[:, :, :, 1, :]])
-    x_parts = x_parts.reshape(2, outer, blocks, epoch_count * rows_each)
+    x_parts = jnp.transpose(x_parts, (0, 1, 2, 4, 3)).reshape(2, outer, blocks, rows_each * epoch_count)
     grid, four_cos, four_sin = transform_blocks(x_parts, lon_count)
-    grid_rows = jnp.transpose(grid.reshape(epoch_count, rows_each, lon_count), (1, 0, 2))
-
-    split = (blocks, outer, epoch_count, rows_each)
-    fourier = jnp.stack([four_cos.reshape(split), four_sin.reshape(split)], axis=3)
+    grid_rows = grid.reshape(rows_each, epoch_count, lon_count)
+
+    split = (blocks, outer, rows_each, epoch_count)
+    fourier = jnp.stack([four_cos.reshape(split), four_sin.reshape(split)], axis=4)
+    fourier = jnp.transpose(fourier, (0, 1, 3, 4, 2))
     fourier = fourier.astype(jnp.bfloat16).reshape(blocks, outer, -1)
     picked = jnp.einsum("sd,cdr->scr", by_d, fourier, preferred_element_type=jnp.float32)
     by_slot = jnp.sum(jnp.where(in_c[:, :, None], picked, jnp.float32(0.0)), axis=1)

time: 63.9 us -> 62.4 us (0.977)
  Pallas kernels: 16.4 us -> 15.6 us
    unnamed x9 -> x8, local copies, waits for them, and re-layouts: 0.69 us -> 0.05 us
where the time goes in v4:
time: 62.4 us; the launch traced here: 62.1 us
  waiting for transfers between devices  17.5 us (28%)
  starting transfers between devices  16 us (26%)
  Pallas kernels  15.6 us (25%)
  local copies, waits for them, and re-layouts  6.82 us (11%)
  matrix products  3.11 us (5%)
  other arithmetic  2.17 us (3%)
  between operations  0.99 us (2%)
    all_to_all x1, starting transfers between devices, shards(): got = lax.all_to_all(payload, ('gx', 'gy'), 0, 0, tiled=True)  11.5 us
    all_to_all x1, waiting for transfers between devices, shards(): got = lax.all_to_all(payload, ('gx', 'gy'), 0, 0, tiled=True)  8.87 us
    all_to_all x1, waiting for transfers between devices, shards(): back = lax.all_to_all(back, ('gx', 'gy'), 0, 0, tiled=True)  8.62 us
    pallas_call x1, Pallas kernels, analyze(): pl.pallas_call(_analysis_kernel, grid_spec=grid_spec, out_shape=jax.Shape...  8.13 us
    pallas_call x1, Pallas kernels, synthesize(): pl.pallas_call(_synth_kernel, grid_spec=grid_spec, out_shape=jax.ShapeDty...  7.45 us
    all_to_all x1, starting transfers between devices, shards(): back = lax.all_to_all(back, ('gx', 'gy'), 0, 0, tiled=True)  4.48 us
    dot_general x4, matrix products, mm(): return jnp.einsum(spec, left, right, precision=highest)  1.42 us
  transfers between devices with their start and end apart: 2, of which 2 were waited for; matrix products, arithmetic and copies ran while one was open for 2% of the time, Pallas kernels for 0%

profile of v4, /device:TPU:1, one launch (start us, length us, event | category | flops | bytes accessed | tf_op | source)
XLA Modules:
  0.0 62.1 jit_solution(7737077605434346838)
XLA Ops:
  0.6 0.7 %convert_bitcast_fusion = (bf16[24,1]{0,1:T(2,128)(2,1)S(1)}, bf16[24,1]{0,1:T(2,128)(2,1)S(1)}) fusion(s32[24]{0:T(128)} %orders_ref.3), kind=kLoop, calls=%fused_computation.109 | loop fusion | flops 384 | bytes 192 | tf_op jit(solution)/shard_map/stack | solution.py:180
  1.3 0.0 copy-start
  1.3 7.5 %shard_map.68 = bf16[24,8,128]{2,1,0:T(8,128)(2,1)} custom-call(s32[24]{0:T(128)} %orders_ref.3, bf16[24,2,2,2160]{3,2,1,0:T(2,128)(2,1)} %coef_ref.1, bf16[24,2160,128]{2,1,0:T(8,128)(2,1)} %leg_ref.3), custom_call_target="tpu_custom_call" | custom-call | flops 106168320 | bytes 13734912 | tf_op jit(solution)/shard_map/pallas_call | solution.py:49
  8.8 0.8 %fusion.69 = (bf16[24,1,4,128]{3,2,1,0:T(4,128)(2,1)S(1)}, bf16[24,1,4,128]{3,2,1,0:T(4,128)(2,1)S(1)}) fusion(bf16[24,2,4,128]{3,2,1,0:T(4,128)(2,1)} %bitcast.118), kind=kLoop, calls=%fused_computation.118 | loop fusion | bytes 98304 | tf_op jit(solution)/shard_map/slice | solution.py:168
  9.6 0.1 rev.6
  9.7 0.0 copy-done
  9.7 0.2 convolution_convert_fusion
  9.8 0.2 copy.58
  10.0 0.1 copy.59
  10.2 0.1 broadcast_in_dim.36
  10.3 0.8 %copy.61 = bf16[128,2,128]{2,1,0:T(2,128)(2,1)} copy(bf16[128,2,128]{0,2,1:T(8,128)(2,1)S(1)} %bitcast.113) | data formatting | bytes 131072 | tf_op jit(solution)/shard_map/reshape | solution.py:185
  11.1 11.5 %all-to-all-start = ((bf16[128,2,128]{2,1,0:T(2,128)(2,1)}), bf16[128,2,128]{2,1,0:T(2,128)(2,1)S(1)}, u32[]{:S(2)}, u32[]{:S(2)}) async-start(bf16[128,2,128]{2,1,0:T(2,128)(2,1)} %copy.61), calls=%async_computation | async-start | bytes 131072 | tf_op jit(solution)/shard_map/all_to_all | solution.py:186
  22.6 0.1 fusion.55
  22.7 0.1 fusion.58
  22.8 0.2 sine_negate_fusion
  23.0 0.1 select_multiply_fusion
  23.1 0.2 fusion.48
  23.2 8.9 %all-to-all-done = bf16[128,2,128]{2,1,0:T(2,128)(2,1)S(1)} async-done(((bf16[128,2,128]{2,1,0:T(2,128)(2,1)}), bf16[128,2,128]{2,1,0:T(2,128)(2,1)S(1)}, u32[]{:S(2)}, u32[]{:S(2)}) %all-to-all-start) | async-done | bytes 65568 | tf_op jit(solution)/shard_map/all_to_all | solution.py:186
  32.1 0.6 reshape.324
  32.7 1.0 %slice_reduce_fusion.1 = (bf16[3072]{0:T(1024)(128)(2,1)S(1)}, bf16[3072]{0:T(1024)(128)(2,1)S(1)}) fusion(bf16[3072,10]{1,0:T(8,128)(2,1)S(1)} %reshape.324), kind=kLoop, calls=%fused_computation.15 | loop fusion | bytes 24576 | tf_op jit(solution)/shard_map/slice | solution.py:189
  33.7 0.1 iota_compare_fusion.4
  33.8 0.2 copy.62
  34.0 0.6 fusion
  34.7 0.4 convolution_bitcast_fusion.1
  35.2 0.4 fusion.5
  35.5 0.3 convolution_bitcast_fusion
  35.9 0.3 convolution_bitcast_fusion.3
  36.3 0.0 copy-start.1
  36.3 0.7 %fusion.3 = bf16[3072,8]{0,1:T(8,128)(2,1)S(1)} fusion(bf16[30,72,8]{1,0,2:T(8,128)(2,1)S(1)} %bitcast.122, pred[3072,30]{0,1:T(8,128)(4,1)S(1)} %iota_compare_fusion.4, bf16[3072]{0:T(1024)(128)(2,1)S(1)} %get-tuple-element.2), kind=kOutput, calls=%fused_computation.4 | convolution fusion | flops 108281856 | bytes 182016 | tf_op jit(solution)/shard_map/sd,cdr->scr/dot_general | solution.py:203
  37.0 0.4 copy.70
  37.4 0.5 convert_element_type.119
  37.9 0.7 %reshape.328 = bf16[128,2,128]{2,1,0:T(2,128)(2,1)} reshape(bf16[128,256]{1,0:T(8,128)(2,1)S(1)} %pad.9) | data formatting | bytes 131072 | tf_op jit(solution)/shard_map/reshape | solution.py:208
  38.6 4.5 %all-to-all-start.1 = ((bf16[128,2,128]{2,1,0:T(2,128)(2,1)}), bf16[128,2,128]{2,1,0:T(2,128)(2,1)S(1)}, u32[]{:S(2)}, u32[]{:S(2)}) async-start(bf16[128,2,128]{2,1,0:T(2,128)(2,1)} %reshape.328), calls=%async_computation.1 | async-start | bytes 131072 | tf_op jit(solution)/shard_map/all_to_all | solution.py:209
  43.1 0.1 copy.66
  43.2 0.8 %reshape_reshape.3 = bf16[2,2,4320]{2,1,0:T(2,128)(2,1)} reshape(bf16[4,72,60]{2,1,0:T(8,128)(2,1)S(1)} %copy.66) | data formatting | bytes 69120 | tf_op jit(solution)/shard_map/reshape;reshape | solution.py:197
  44.0 8.6 %all-to-all-done.1 = bf16[128,2,128]{2,1,0:T(2,128)(2,1)S(1)} async-done(((bf16[128,2,128]{2,1,0:T(2,128)(2,1)}), bf16[128,2,128]{2,1,0:T(2,128)(2,1)S(1)}, u32[]{:S(2)}, u32[]{:S(2)}) %all-to-all-start.1) | async-done | bytes 65568 | tf_op jit(solution)/shard_map/all_to_all | solution.py:209
  52.6 0.1 copy.71
  52.7 0.2 copy.72
  52.9 0.2 fusion.16
  53.2 0.1 rev.7
  53.3 0.0 copy-done.1
  53.4 0.6 %pad_maximum_fusion.5.both_ref = bf16[24,8,128]{2,1,0:T(8,128)(2,1)} fusion(bf16[24,4,128]{2,1,0:T(4,128)(2,1)S(1)} %get-tuple-element.13, bf16[24,4,128]{2,1,0:T(4,128)(2,1)S(1)} %get-tuple-element.12), kind=kLoop, calls=%fused_computation.61 | loop fusion | flops 98304 | bytes 98304 | tf_op jit(solution)/shard_map/concatenate | solution.py:219
  54.0 8.1 %shard_map.69 = bf16[24,2,2,2160]{3,2,1,0:T(2,128)(2,1)} custom-call(s32[24]{0:T(128)} %orders_ref.3, bf16[24,8,128]{2,1,0:T(8,128)(2,1)} %pad_maximum_fusion.5.both_ref, bf16[24,2160,128]{2,1,0:T(8,128)(2,1)} %leg_ref.3), custom_call_target="tpu_custom_call" | custom-call | flops 106168320 | bytes 13734912 | tf_op jit(solution)/shard_map/pallas_call | solution.py:91
  (25 shorter events, 0.4 us)
Async XLA Ops:
  1.3 8.4 %copy-start = (s32[256]{0:T(256)S(1)}, s32[256]{0:T(256)}, u32[]{:S(2)}) copy-start(s32[256]{0:T(256)} %param.8) | copy-start | bytes 3076
  11.1 21.0 %all-to-all-start = ((bf16[128,2,128]{2,1,0:T(2,128)(2,1)}), bf16[128,2,128]{2,1,0:T(2,128)(2,1)S(1)}, u32[]{:S(2)}, u32[]{:S(2)}) async-start(bf16[128,2,128]{2,1,0:T(2,128)(2,1)} %copy.61), calls=%async_computation | async-start | bytes 131072 | tf_op jit(solution)/shard_map/all_to_all | solution.py:186
  36.3 17.0 %copy-start.1 = (f32[128]{0:T(128)S(1)}, f32[128]{0:T(128)}, u32[]{:S(2)}) copy-start(f32[128]{0:T(128)} %param.9) | copy-start | bytes 1540
  38.6 14.0 %all-to-all-start.1 = ((bf16[128,2,128]{2,1,0:T(2,128)(2,1)}), bf16[128,2,128]{2,1,0:T(2,128)(2,1)S(1)}, u32[]{:S(2)}, u32[]{:S(2)}) async-start(bf16[128,2,128]{2,1,0:T(2,128)(2,1)} %reshape.328), calls=%async_computation.1 | async-start | bytes 131072 | tf_op jit(solution)/shard_map/all_to_all | solution.py:209

commit v5 on v4

--- a/solution.py
+++ b/solution.py
@@ -32,31 +32,87 @@
         out_ref[i] = jnp.dot(lhs, leg_ref[i], preferred_element_type=jnp.float32).astype(out_ref.dtype)
 
 
-def synthesize(coeffs, legendre, orders):
+def _payload_kernel(orders_ref, coef_ref, leg_ref, aux_ref, out_ref, north_ref, south_ref):
+    step = pl.program_id(0)
+    block, epochs, _, deg_count = coef_ref.shape
+    steps = orders_ref.shape[0] // block
+    per = 2 * epochs
+    half_lats = leg_ref.shape[2]
+    devices, width = out_ref.shape
+    rows_each = width // 128 - 2
+    zero = jnp.zeros((), coef_ref.dtype)
+
+    @pl.when(step == 0)
+    def _():
+        north_ref[...] = jnp.zeros_like(north_ref)
+        south_ref[...] = jnp.zeros_like(south_ref)
+
+    for i in range(block):
+        order = orders_ref[step * block + i]
+        usable, even = _masks(order, deg_count)
+        rows = jnp.concatenate([coef_ref[i, e] for e in range(epochs)], axis=0)
+        masked = jnp.where(usable, rows, zero)
+        signed = jnp.where(even, masked, -masked)
+        lhs = jnp.concatenate([masked, signed], axis=0)
+        res = jnp.dot(lhs, leg_ref[i], preferred_element_type=jnp.float32)
+        res = res.astype(jnp.bfloat16).astype(jnp.float32)
+        for g in range(steps):
+
+            @pl.when(step == g)
+            def _(g=g, i=i, res=res):
+                first = (g * block + i) * per
+                north_ref[first:first + per, :] = res[:per]
+                south_ref[first:first + per, :] = res[per:]
+
+    @pl.when(step == steps - 1)
+    def _():
+        lat = lax.broadcasted_iota(jnp.int32, (half_lats, 1), 0)
+        north = north_ref[...].astype(jnp.bfloat16)
+        south = south_ref[...].astype(jnp.bfloat16)
+        dims = (((1,), (1,)), ((), ()))
+        for t in range(rows_each):
+            held = aux_ref[t:t + 1, :]
+            pick_n = (held == lat).astype(jnp.float32).T.astype(jnp.bfloat16)
+            pick_s = (held == 2 * half_lats - 1 - lat).astype(jnp.float32).T.astype(jnp.bfloat16)
+            rows_t = lax.dot_general(pick_n, north, dims, preferred_element_type=jnp.float32)
+            rows_t += lax.dot_general(pick_s, south, dims, preferred_element_type=jnp.float32)
+            out_ref[:, t * 128:(t + 1) * 128] = rows_t.astype(out_ref.dtype)
+        for j in range(2):
+            code = aux_ref[rows_each + j:rows_each + j + 1, :].astype(jnp.float32)
+            out_ref[:, (rows_each + j) * 128:(rows_each + j + 1) * 128] = jnp.broadcast_to(
+                code, (devices, 128)
+            ).astype(out_ref.dtype)
+
+
+def synthesize_payload(coeffs, legendre, orders, aux, devices):
     slot_cap, epochs, parts, deg_count = coeffs.shape
     half_lats = legendre.shape[2]
     block = SLOTS_PER_STEP
-    rows = 2 * epochs * parts
+    rows_each = aux.shape[0] - 2
+    width = (rows_each + 2) * 128
     grid_spec = pltpu.PrefetchScalarGridSpec(
         num_scalar_prefetch=1,
         grid=(slot_cap // block,),
         in_specs=[
             pl.BlockSpec((block, epochs, parts, deg_count), lambda g, o: (g, 0, 0, 0)),
             pl.BlockSpec((block, deg_count, half_lats), lambda g, o: (g, 0, 0)),
+            pl.BlockSpec(aux.shape, lambda g, o: (0, 0)),
         ],
-        out_specs=pl.BlockSpec((block, rows, half_lats), lambda g, o: (g, 0, 0)),
-    )
+        out_specs=pl.BlockSpec((devices, width), lambda g, o: (0, 0)),
+        scratch_shapes=[pltpu.VMEM((128, half_lats), jnp.float32)] * 2,
+    )
+    rows = 2 * epochs * parts
     return pl.pallas_call(
-        _synth_kernel,
+        _payload_kernel,
         grid_spec=grid_spec,
-        out_shape=jax.ShapeDtypeStruct((slot_cap, rows, half_lats), jnp.bfloat16),
+        out_shape=jax.ShapeDtypeStruct((devices, width), jnp.bfloat16),
         compiler_params=pltpu.CompilerParams(dimension_semantics=("arbitrary",)),
         cost_estimate=pl.CostEstimate(
             flops=2 * slot_cap * rows * deg_count * half_lats,
-            bytes_accessed=legendre.size * 2 + coeffs.size * 2 + slot_cap * rows * half_lats * 2,
+            bytes_accessed=legendre.size * 2 + coeffs.size * 2 + devices * width * 2,
             transcendentals=0,
         ),
-    )(orders, coeffs, legendre)
+    )(orders, coeffs, legendre, aux)
 
 
 def _analysis_kernel(orders_ref, both_ref, leg_ref, out_ref):
@@ -164,35 +220,32 @@
     devices = lax.axis_size(("gx", "gy"))
     rows_each = lat_rows // devices
 
-    synth = synthesize(coeffs, legendre, orders).reshape(slot_cap, 2, epoch_count * 2, half_lats)
-    full_lats = jnp.concatenate([synth[:, 0], synth[:, 1, :, ::-1]], axis=-1)
-
-    onehot = one_hot_rows(lat_map, lat_rows)
-    permuted = jnp.einsum(
-        "sxk,kr->sxr", full_lats, onehot, preferred_element_type=jnp.float32
-    ).astype(jnp.bfloat16)
-    sends = permuted.reshape(slot_cap, epoch_count * 2, devices, rows_each)
-    sends = jnp.transpose(sends, (2, 0, 1, 3)).reshape(devices, slot_cap, epoch_count * 2 * rows_each)
     inner = inner_length(lon_count)
     outer = lon_count // inner
     blocks = deg_count // outer
-    block_of = jnp.where(orders >= 0, orders // outer, -1)
-    order_code = jnp.stack([block_of, orders % outer], axis=-1).astype(jnp.bfloat16)
-    order_code = jnp.broadcast_to(order_code[None], (devices, slot_cap, 2))
-    payload = jnp.concatenate([sends, order_code], axis=-1).reshape(devices, -1)
-    width = payload.shape[1]
-    padded = -(-width // 256) * 256
-    payload = jnp.pad(payload, ((0, 0), (0, padded - width))).reshape(devices, padded // 128, 128)
+    assert slot_cap * 2 * epoch_count <= 128 and devices <= 128
+
+    onehot = one_hot_rows(lat_map, lat_rows)
+
+    lane_pad = 128 - slot_cap
+    block_of = jnp.pad(jnp.where(orders >= 0, orders // outer, -1), (0, lane_pad), constant_values=-1)
+    offset = jnp.pad(orders % outer, (0, lane_pad))
+    lat_pairs = jnp.pad(jnp.transpose(lat_map.reshape(devices, rows_each)), ((0, 0), (0, 128 - devices)))
+    aux = jnp.concatenate([lat_pairs, block_of[None], offset[None]], axis=0)
+    payload = synthesize_payload(coeffs, legendre, orders, aux, devices)
     got = lax.all_to_all(payload, ("gx", "gy"), 0, 0, tiled=True)
-    got = got.reshape(devices, padded)[:, :width].reshape(devices * slot_cap, -1)
-    data = got[:, :-2]
-    by_d = (got[:, -1:] == jnp.arange(outer, dtype=jnp.bfloat16)[None, :]).astype(jnp.bfloat16)
-    in_c = got[:, -2:-1] == jnp.arange(blocks, dtype=jnp.bfloat16)[None, :]
+    used = slot_cap * 2 * epoch_count
+    data = jnp.stack([got[:, t * 128:t * 128 + used] for t in range(rows_each)], axis=1)
+    data = jnp.transpose(data.reshape(devices, rows_each, slot_cap, -1), (0, 2, 1, 3))
+    data = data.reshape(devices * slot_cap, -1)
+    c_code = got[:, rows_each * 128:rows_each * 128 + slot_cap].reshape(-1, 1)
+    d_code = got[:, (rows_each + 1) * 128:(rows_each + 1) * 128 + slot_cap].reshape(-1, 1)
+    by_d = (d_code == jnp.arange(outer, dtype=jnp.bfloat16)[None, :]).astype(jnp.bfloat16)
+    in_c = c_code == jnp.arange(blocks, dtype=jnp.bfloat16)[None, :]
     spread = jnp.where(in_c[:, :, None], data[:, None, :], jnp.zeros((), jnp.bfloat16))
     dense = jnp.einsum("sd,scr->dcr", by_d, spread, preferred_element_type=jnp.float32)
-    dense = dense.reshape(outer, blocks, epoch_count, 2, rows_each)
-    x_parts = jnp.stack([dense[:, :, :, 0, :], -dense[:, :, :, 1, :]])
-    x_parts = jnp.transpose(x_parts, (0, 1, 2, 4, 3)).reshape(2, outer, blocks, rows_each * epoch_count)
+    dense = dense.reshape(outer, blocks, rows_each * epoch_count, 2)
+    x_parts = jnp.stack([dense[..., 0], -dense[..., 1]])
     grid, four_cos, four_sin = transform_blocks(x_parts, lon_count)
     grid_rows = grid.reshape(rows_each, epoch_count, lon_count)
 

time: 62.4 us -> 66.1 us (1.059)
  other arithmetic: 2.17 us -> 4.36 us
  Pallas kernels: 15.6 us -> 17.7 us
    pallas_call x1, Pallas kernels: 7.45 us -> 9.54 us  [synthesize_payload(): pl.pallas_call(_payload_kernel, grid_spec=grid_spec, out_shape=jax.ShapeD...]
    slice x3 -> x4, local copies, waits for them, and re-layouts: 2.02 us -> 0.25 us  [the longest x2 0.12 us: shards(): got[:, (rows_each + 1) * 128:(rows_each + 1) * 128 + slot_cap]]
    all_to_all x0 -> x1, other arithmetic: none -> 1.58 us  [shards(): got = lax.all_to_all(payload, ('gx', 'gy'), 0, 0, tiled=True)]
    unnamed x8 -> x7, local copies, waits for them, and re-layouts: 0.05 us -> 0.82 us
    another operation x4 -> x1, other arithmetic: 0.72 us -> 0.02 us  [the longest x2 0.69 us: shards(): jnp.stack([block_of, orders % outer], axis=-1).astype(jnp.bfloat16)]
    all_to_all x0 -> x2, local copies, waits for them, and re-layouts: none -> 0.69 us  [shards(): got = lax.all_to_all(payload, ('gx', 'gy'), 0, 0, tiled=True)]
    select_n x0 -> x1, other arithmetic: none -> 0.67 us  [shards(): jnp.where(orders >= 0, orders // outer, -1)]
    reshape x3 -> x2, local copies, waits for them, and re-layouts: 1.39 us -> 0.87 us  [shards(): lat_map.reshape(devices, rows_each)]
where the time goes in v5:
time: 66.1 us; the launch traced here: 65.8 us
  waiting for transfers between devices  18 us (27%)
  Pallas kernels  17.7 us (27%)
  starting transfers between devices  15.7 us (24%)
  local copies, waits for them, and re-layouts  6.24 us (9%)
  other arithmetic  4.36 us (7%)
  matrix products  2.94 us (4%)
  between operations  0.95 us (1%)
    all_to_all x1, starting transfers between devices, shards(): got = lax.all_to_all(payload, ('gx', 'gy'), 0, 0, tiled=True)  11.5 us
    pallas_call x1, Pallas kernels, synthesize_payload(): pl.pallas_call(_payload_kernel, grid_spec=grid_spec, out_shape=jax.ShapeD...  9.54 us
    all_to_all x1, waiting for transfers between devices, shards(): got = lax.all_to_all(payload, ('gx', 'gy'), 0, 0, tiled=True)  9.37 us
    all_to_all x1, waiting for transfers between devices, shards(): back = lax.all_to_all(back, ('gx', 'gy'), 0, 0, tiled=True)  8.61 us
    pallas_call x1, Pallas kernels, analyze(): pl.pallas_call(_analysis_kernel, grid_spec=grid_spec, out_shape=jax.Shape...  8.13 us
    all_to_all x1, starting transfers between devices, shards(): back = lax.all_to_all(back, ('gx', 'gy'), 0, 0, tiled=True)  4.21 us
    all_to_all x1, other arithmetic, shards(): got = lax.all_to_all(payload, ('gx', 'gy'), 0, 0, tiled=True)  1.58 us
    dot_general x4, matrix products, mm(): return jnp.einsum(spec, left, right, precision=highest)  1.42 us
  transfers between devices with their start and end apart: 2, of which 2 were waited for; matrix products, arithmetic and copies ran while one was open for 2% of the time, Pallas kernels for 0%

profile of v5, /device:TPU:1, one launch (start us, length us, event | category | flops | bytes accessed | tf_op | source)
XLA Modules:
  0.0 65.8 jit_solution(6017427313255145517)
XLA Ops:
  0.6 0.7 %compare_select_fusion = (s32[24]{0:T(128)S(1)}, s32[24]{0:T(128)S(1)}) fusion(s32[24]{0:T(128)} %orders_ref.3), kind=kLoop, calls=%fused_computation.98 | loop fusion | flops 336 | bytes 288 | tf_op jit(solution)/shard_map/jit(_where)/select_n | solution.py:231
  1.3 0.8 %reshape.290 = s32[128,2]{1,0:T(8,128)S(1)} reshape(s32[256]{0:T(256)} %param.8) | data formatting | bytes 2048 | tf_op jit(solution)/shard_map/reshape | solution.py:233
  2.1 0.1 copy.31
  2.2 0.6 pad_add_fusion.aux_ref
  2.8 9.5 %shard_map.68 = bf16[128,512]{1,0:T(8,128)(2,1)} custom-call(s32[24]{0:T(128)} %orders_ref.3, bf16[24,2,2,2160]{3,2,1,0:T(2,128)(2,1)} %coef_ref.1, bf16[24,2160,128]{2,1,0:T(8,128)(2,1)} %leg_ref.3, s32[4,128]{1,0:T(4,128)} %pad_add_fusion.aux_ref), custom_call_target="tpu_custom_call" | custom-call | flops 106168320 | bytes 13816832 | tf_op jit(solution)/shard_map/pallas_call | solution.py:105
  12.3 0.5 broadcast.315
  12.9 1.6 %reduce = bf16[128,512]{1,0:T(8,128)(2,1)S(1)} reduce(bf16[128,1,512]{2,0,1:T(8,128)(2,1)} %bitcast.104, bf16[]{:T(256)} %broadcast.315), dimensions={1}, to_apply=%copy.32.reduce_sub_computation | reduce | bytes 262146 | tf_op jit(solution)/shard_map/all_to_all | solution.py:236
  14.4 0.7 %reshape.308 = bf16[128,2,256]{2,1,0:T(2,128)(2,1)} reshape(bf16[128,512]{1,0:T(8,128)(2,1)S(1)} %reduce) | data formatting | bytes 262144
  15.1 11.5 %all-to-all-start = ((bf16[128,2,256]{2,1,0:T(2,128)(2,1)}), bf16[128,2,256]{2,1,0:T(2,128)(2,1)S(1)}, u32[]{:S(2)}, u32[]{:S(2)}) async-start(bf16[128,2,256]{2,1,0:T(2,128)(2,1)} %reshape.308), calls=%async_computation | async-start | bytes 262144 | tf_op jit(solution)/shard_map/all_to_all | solution.py:236
  26.7 0.1 fusion.53
  26.8 0.2 fusion.46
  26.9 0.2 sine_negate_fusion
  27.1 0.1 select_multiply_fusion
  27.2 0.1 fusion.56
  27.3 9.4 %all-to-all-done = bf16[128,2,256]{2,1,0:T(2,128)(2,1)S(1)} async-done(((bf16[128,2,256]{2,1,0:T(2,128)(2,1)}), bf16[128,2,256]{2,1,0:T(2,128)(2,1)S(1)}, u32[]{:S(2)}, u32[]{:S(2)}) %all-to-all-start) | async-done | bytes 131104 | tf_op jit(solution)/shard_map/all_to_all | solution.py:236
  36.6 0.1 reshape.309
  36.7 0.2 copy.33
  36.9 0.1 copy.34
  37.1 0.1 eq.78
  37.2 0.1 copy.35
  37.3 0.1 eq.82
  37.4 0.1 iota_compare_fusion.4
  37.5 0.2 copy.36
  37.7 0.3 broadcast_in_dim.70
  38.0 0.6 fusion
  38.7 0.4 convolution_bitcast_fusion.1
  39.1 0.4 fusion.5
  39.5 0.3 convolution_bitcast_fusion
  39.9 0.3 convolution_bitcast_fusion.3
  40.2 0.0 copy-start
  40.3 0.0 copy-start.1
  40.3 0.7 %fusion.3 = bf16[3072,8]{0,1:T(8,128)(2,1)S(1)} fusion(bf16[30,72,8]{1,0,2:T(8,128)(2,1)S(1)} %bitcast.115, pred[3072,30]{0,1:T(8,128)(4,1)S(1)} %iota_compare_fusion.4, bf16[3072]{0:T(1024)(128)(2,1)S(1)} %eq.78), kind=kOutput, calls=%fused_computation.4 | convolution fusion | flops 108281856 | bytes 182016 | tf_op jit(solution)/shard_map/sd,cdr->scr/dot_general | solution.py:256
  41.0 0.4 copy.44
  41.4 0.5 convert_element_type.108
  41.9 0.7 reshape.293
  42.6 4.2 %all-to-all-start.1 = ((bf16[128,2,128]{2,1,0:T(2,128)(2,1)}), bf16[128,2,128]{2,1,0:T(2,128)(2,1)S(1)}, u32[]{:S(2)}, u32[]{:S(2)}) async-start(bf16[128,2,128]{2,1,0:T(2,128)(2,1)} %reshape.293), calls=%async_computation.1 | async-start | bytes 131072 | tf_op jit(solution)/shard_map/all_to_all | solution.py:262
  46.8 0.1 copy.40
  46.9 0.8 %reshape_reshape.3 = bf16[2,2,4320]{2,1,0:T(2,128)(2,1)} reshape(bf16[4,72,60]{2,1,0:T(8,128)(2,1)S(1)} %copy.40) | data formatting | bytes 69120 | tf_op jit(solution)/shard_map/reshape;reshape | solution.py:250
  47.7 8.6 %all-to-all-done.1 = bf16[128,2,128]{2,1,0:T(2,128)(2,1)S(1)} async-done(((bf16[128,2,128]{2,1,0:T(2,128)(2,1)}), bf16[128,2,128]{2,1,0:T(2,128)(2,1)S(1)}, u32[]{:S(2)}, u32[]{:S(2)}) %all-to-all-start.1) | async-done | bytes 65568 | tf_op jit(solution)/shard_map/all_to_all | solution.py:262
  56.3 0.1 copy.45
  56.4 0.2 copy.46
  56.6 0.0 copy-done
  56.6 0.2 fusion.16
  56.9 0.1 rev.3
  57.0 0.0 copy-done.1
  57.1 0.6 pad_maximum_fusion.4.both_ref
  57.7 8.1 %shard_map.69 = bf16[24,2,2,2160]{3,2,1,0:T(2,128)(2,1)} custom-call(s32[24]{0:T(128)} %orders_ref.3, bf16[24,8,128]{2,1,0:T(8,128)(2,1)} %pad_maximum_fusion.4.both_ref, bf16[24,2160,128]{2,1,0:T(8,128)(2,1)} %leg_ref.3), custom_call_target="tpu_custom_call" | custom-call | flops 106168320 | bytes 13734912 | tf_op jit(solution)/shard_map/pallas_call | solution.py:147
  (20 shorter events, 0.3 us)
Async XLA Ops:
  15.1 21.5 %all-to-all-start = ((bf16[128,2,256]{2,1,0:T(2,128)(2,1)}), bf16[128,2,256]{2,1,0:T(2,128)(2,1)S(1)}, u32[]{:S(2)}, u32[]{:S(2)}) async-start(bf16[128,2,256]{2,1,0:T(2,128)(2,1)} %reshape.308), calls=%async_computation | async-start | bytes 262144 | tf_op jit(solution)/shard_map/all_to_all | solution.py:236
  40.2 16.4 %copy-start = (s32[256]{0:T(256)S(1)}, s32[256]{0:T(256)}, u32[]{:S(2)}) copy-start(s32[256]{0:T(256)} %param.8) | copy-start | bytes 3076
  40.3 16.7 %copy-start.1 = (f32[128]{0:T(128)S(1)}, f32[128]{0:T(128)}, u32[]{:S(2)}) copy-start(f32[128]{0:T(128)} %param.9) | copy-start | bytes 1540
  42.6 13.7 %all-to-all-start.1 = ((bf16[128,2,128]{2,1,0:T(2,128)(2,1)}), bf16[128,2,128]{2,1,0:T(2,128)(2,1)S(1)}, u32[]{:S(2)}, u32[]{:S(2)}) async-start(bf16[128,2,128]{2,1,0:T(2,128)(2,1)} %reshape.293), calls=%async_computation.1 | async-start | bytes 131072 | tf_op jit(solution)/shard_map/all_to_all | solution.py:262

commit v6 on v4

--- a/solution.py
+++ b/solution.py
@@ -59,15 +59,22 @@
     )(orders, coeffs, legendre)
 
 
-def _analysis_kernel(orders_ref, both_ref, leg_ref, out_ref):
+def _analysis_kernel(orders_ref, ret_ref, pick_ref, w_ref, leg_ref, out_ref):
     step = pl.program_id(0)
     block, epochs, parts, deg_count = out_ref.shape
     half = epochs * parts
+    held = ret_ref[...]
+    north = jnp.dot(held, pick_ref[0], preferred_element_type=jnp.float32)
+    south = jnp.dot(held, pick_ref[1], preferred_element_type=jnp.float32)
+    sym = ((north + south) * w_ref[...]).astype(jnp.bfloat16).astype(jnp.float32)
+    anti = ((north - south) * w_ref[...]).astype(jnp.bfloat16).astype(jnp.float32)
     for i in range(block):
         order = orders_ref[step * block + i]
         usable, even = _masks(order, deg_count)
+        rows = slice(i * half, (i + 1) * half)
+        both = jnp.concatenate([sym[rows], anti[rows]], axis=0).astype(jnp.bfloat16)
         res = lax.dot_general(
-            both_ref[i], leg_ref[i], (((1,), (1,)), ((), ())), preferred_element_type=jnp.float32
+            both, leg_ref[i], (((1,), (1,)), ((), ())), preferred_element_type=jnp.float32
         )
         chosen = jnp.where(even, res[:half], res[half:])
         chosen = jnp.where(usable, chosen, jnp.float32(0.0)).astype(out_ref.dtype)
@@ -75,15 +82,19 @@
             out_ref[i, e] = chosen[e * parts:(e + 1) * parts]
 
 
-def analyze(both, legendre, orders, epochs, parts):
-    slot_cap, rows, half_lats = both.shape
-    deg_count = legendre.shape[1]
+def analyze(returned, pick, weights, legendre, orders, epochs, parts):
+    slot_cap = orders.shape[0]
+    _, lat_rows = returned.shape
+    deg_count, half_lats = legendre.shape[1:]
     block = SLOTS_PER_STEP
+    half = epochs * parts
     grid_spec = pltpu.PrefetchScalarGridSpec(
         num_scalar_prefetch=1,
         grid=(slot_cap // block,),
         in_specs=[
-            pl.BlockSpec((block, rows, half_lats), lambda g, o: (g, 0, 0)),
+            pl.BlockSpec((block * half, lat_rows), lambda g, o: (g, 0)),
+            pl.BlockSpec(pick.shape, lambda g, o: (0, 0, 0)),
+            pl.BlockSpec(weights.shape, lambda g, o: (0, 0)),
             pl.BlockSpec((block, deg_count, half_lats), lambda g, o: (g, 0, 0)),
         ],
         out_specs=pl.BlockSpec((block, epochs, parts, deg_count), lambda g, o: (g, 0, 0, 0)),
@@ -94,11 +105,11 @@
         out_shape=jax.ShapeDtypeStruct((slot_cap, epochs, parts, deg_count), jnp.bfloat16),
         compiler_params=pltpu.CompilerParams(dimension_semantics=("arbitrary",)),
         cost_estimate=pl.CostEstimate(
-            flops=2 * slot_cap * rows * deg_count * half_lats,
-            bytes_accessed=legendre.size * 2 + both.size * 2 + slot_cap * epochs * parts * deg_count * 2,
+            flops=2 * slot_cap * 2 * half * deg_count * half_lats,
+            bytes_accessed=legendre.size * 2 + returned.size * 2 + slot_cap * half * deg_count * 2,
             transcendentals=0,
         ),
-    )(orders, both, legendre)
+    )(orders, returned, pick, weights, legendre)
 
 
 def inner_length(lon_count):
@@ -208,16 +219,12 @@
     back = jnp.pad(back, ((0, 0), (0, padded - width))).reshape(devices, padded // 128, 128)
     back = lax.all_to_all(back, ("gx", "gy"), 0, 0, tiled=True)
     back = back.reshape(devices, padded)[:, :width].reshape(devices, slot_cap, epoch_count, 2, rows_each)
-    returned = jnp.transpose(back, (1, 2, 3, 0, 4)).reshape(slot_cap, epoch_count * 2, lat_rows)
-    natural = jnp.einsum(
-        "sxr,kr->sxk", returned, onehot, preferred_element_type=jnp.float32
-    )
-    northern = natural[..., :half_lats]
-    southern = natural[..., half_lats:][..., ::-1]
-    sym_part = ((northern + southern) * weights).astype(jnp.bfloat16)
-    anti_part = ((northern - southern) * weights).astype(jnp.bfloat16)
-    both = jnp.concatenate([sym_part, anti_part], axis=1)
-    spectra = analyze(both, legendre, orders, epoch_count, 2)
+    returned = jnp.transpose(back, (1, 2, 3, 0, 4)).reshape(slot_cap * epoch_count * 2, lat_rows)
+    lat_ids = jnp.arange(half_lats, dtype=jnp.int32)[None, :]
+    pick = jnp.stack([lat_map[:, None] == lat_ids, lat_map[:, None] == lat_rows - 1 - lat_ids])
+    spectra = analyze(
+        returned, pick.astype(jnp.bfloat16), weights.reshape(1, -1), legendre, orders, epoch_count, 2
+    )
     return (grid_rows, spectra)
 
 

time: 62.4 us -> 68.4 us (1.096)
  local copies, waits for them, and re-layouts: 6.82 us -> 13.5 us
  waiting for transfers between devices: 17.5 us -> 16.7 us
    reshape x0 -> x1, local copies, waits for them, and re-layouts: none -> 5.45 us  [shards(): jnp.transpose(back, (1, 2, 3, 0, 4))]
    transpose x1, local copies, waits for them, and re-layouts: 0.18 us -> 1.58 us  [shards(): jnp.transpose(back, (1, 2, 3, 0, 4))]
  transfers between devices with their start and end apart: 2 -> 2, of which waited for: 2 -> 2; matrix products, arithmetic and copies ran while one was open for 2% -> 3% of each run, Pallas kernels for 0% -> 0%
where the time goes in v6:
time: 68.4 us; the launch traced here: 68.1 us
  waiting for transfers between devices  16.7 us (24%)
  starting transfers between devices  16 us (23%)
  Pallas kernels  15.8 us (23%)
  local copies, waits for them, and re-layouts  13.5 us (20%)
  matrix products  2.9 us (4%)
  other arithmetic  2.28 us (3%)
  between operations  0.95 us (1%)
    all_to_all x1, starting transfers between devices, shards(): got = lax.all_to_all(payload, ('gx', 'gy'), 0, 0, tiled=True)  11.5 us
    all_to_all x1, waiting for transfers between devices, shards(): got = lax.all_to_all(payload, ('gx', 'gy'), 0, 0, tiled=True)  8.75 us
    pallas_call x1, Pallas kernels, analyze(): pl.pallas_call(_analysis_kernel, grid_spec=grid_spec, out_shape=jax.Shape...  8.34 us
    all_to_all x1, waiting for transfers between devices, shards(): back = lax.all_to_all(back, ('gx', 'gy'), 0, 0, tiled=True)  7.94 us
    pallas_call x1, Pallas kernels, synthesize(): pl.pallas_call(_synth_kernel, grid_spec=grid_spec, out_shape=jax.ShapeDty...  7.45 us
    reshape x1, local copies, waits for them, and re-layouts, shards(): jnp.transpose(back, (1, 2, 3, 0, 4))  5.45 us
    all_to_all x1, starting transfers between devices, shards(): back = lax.all_to_all(back, ('gx', 'gy'), 0, 0, tiled=True)  4.48 us
    transpose x1, local copies, waits for them, and re-layouts, shards(): jnp.transpose(back, (1, 2, 3, 0, 4))  1.58 us
  transfers between devices with their start and end apart: 2, of which 2 were waited for; matrix products, arithmetic and copies ran while one was open for 3% of the time, Pallas kernels for 0%

profile of v6, /device:TPU:1, one launch (start us, length us, event | category | flops | bytes accessed | tf_op | source)
XLA Modules:
  0.0 68.1 jit_solution(16704290045363706009)
XLA Ops:
  0.6 0.7 convert_bitcast_fusion
  1.3 0.0 copy-start
  1.3 7.5 %shard_map.68 = bf16[24,8,128]{2,1,0:T(8,128)(2,1)} custom-call(s32[24]{0:T(128)} %orders_ref.3, bf16[24,2,2,2160]{3,2,1,0:T(2,128)(2,1)} %coef_ref.1, bf16[24,2160,128]{2,1,0:T(8,128)(2,1)} %leg_ref.3), custom_call_target="tpu_custom_call" | custom-call | flops 106168320 | bytes 13734912 | tf_op jit(solution)/shard_map/pallas_call | solution.py:49
  8.8 0.8 %fusion.65 = (bf16[24,1,4,128]{3,2,1,0:T(4,128)(2,1)S(1)}, bf16[24,1,4,128]{3,2,1,0:T(4,128)(2,1)S(1)}) fusion(bf16[24,2,4,128]{3,2,1,0:T(4,128)(2,1)} %bitcast.117), kind=kLoop, calls=%fused_computation.116 | loop fusion | bytes 98304 | tf_op jit(solution)/shard_map/slice | solution.py:179
  9.6 0.1 rev.3
  9.7 0.0 copy-done
  9.7 0.2 convolution_convert_fusion
  9.8 0.2 copy.50
  10.0 0.1 copy.51
  10.2 0.1 broadcast_in_dim.36
  10.3 0.8 %copy.53 = bf16[128,2,128]{2,1,0:T(2,128)(2,1)} copy(bf16[128,2,128]{0,2,1:T(8,128)(2,1)S(1)} %bitcast.112) | data formatting | bytes 131072 | tf_op jit(solution)/shard_map/reshape | solution.py:196
  11.1 11.5 %all-to-all-start = ((bf16[128,2,128]{2,1,0:T(2,128)(2,1)}), bf16[128,2,128]{2,1,0:T(2,128)(2,1)S(1)}, u32[]{:S(2)}, u32[]{:S(2)}) async-start(bf16[128,2,128]{2,1,0:T(2,128)(2,1)} %copy.53), calls=%async_computation | async-start | bytes 131072 | tf_op jit(solution)/shard_map/all_to_all | solution.py:197
  22.6 0.1 fusion.52
  22.7 0.1 fusion.55
  22.8 0.2 sine_negate_fusion
  23.0 0.1 iota_compare_fusion.5
  23.1 0.1 select_multiply_fusion
  23.2 0.2 fusion.45
  23.3 8.8 %all-to-all-done = bf16[128,2,128]{2,1,0:T(2,128)(2,1)S(1)} async-done(((bf16[128,2,128]{2,1,0:T(2,128)(2,1)}), bf16[128,2,128]{2,1,0:T(2,128)(2,1)S(1)}, u32[]{:S(2)}, u32[]{:S(2)}) %all-to-all-start) | async-done | bytes 65568 | tf_op jit(solution)/shard_map/all_to_all | solution.py:197
  32.1 0.6 reshape.399
  32.7 1.0 %slice_reduce_fusion.1 = (bf16[3072]{0:T(1024)(128)(2,1)S(1)}, bf16[3072]{0:T(1024)(128)(2,1)S(1)}) fusion(bf16[3072,10]{1,0:T(8,128)(2,1)S(1)} %reshape.399), kind=kLoop, calls=%fused_computation.15 | loop fusion | bytes 24576 | tf_op jit(solution)/shard_map/slice | solution.py:200
  33.7 0.1 iota_compare_fusion.4
  33.8 0.2 copy.54
  34.0 0.6 fusion
  34.7 0.4 convolution_bitcast_fusion.1
  35.2 0.4 fusion.5
  35.5 0.3 convolution_bitcast_fusion
  35.9 0.3 convolution_bitcast_fusion.3
  36.3 0.7 %fusion.3 = bf16[3072,8]{0,1:T(8,128)(2,1)S(1)} fusion(bf16[30,72,8]{1,0,2:T(8,128)(2,1)S(1)} %bitcast.121, pred[3072,30]{0,1:T(8,128)(4,1)S(1)} %iota_compare_fusion.4, bf16[3072]{0:T(1024)(128)(2,1)S(1)} %get-tuple-element.2), kind=kOutput, calls=%fused_computation.4 | convolution fusion | flops 108281856 | bytes 182016 | tf_op jit(solution)/shard_map/sd,cdr->scr/dot_general | solution.py:214
  37.0 0.4 copy.62
  37.4 0.5 convert_element_type.116
  37.9 0.7 reshape.403
  38.6 4.5 %all-to-all-start.1 = ((bf16[128,2,128]{2,1,0:T(2,128)(2,1)}), bf16[128,2,128]{2,1,0:T(2,128)(2,1)S(1)}, u32[]{:S(2)}, u32[]{:S(2)}) async-start(bf16[128,2,128]{2,1,0:T(2,128)(2,1)} %reshape.403), calls=%async_computation.1 | async-start | bytes 131072 | tf_op jit(solution)/shard_map/all_to_all | solution.py:220
  43.1 0.7 add_convert_fusion.pick_ref
  43.8 0.1 copy.58
  43.9 0.8 %reshape_reshape.3 = bf16[2,2,4320]{2,1,0:T(2,128)(2,1)} reshape(bf16[4,72,60]{2,1,0:T(8,128)(2,1)S(1)} %copy.58) | data formatting | bytes 69120 | tf_op jit(solution)/shard_map/reshape;reshape | solution.py:208
  44.6 7.9 %all-to-all-done.1 = bf16[128,2,128]{2,1,0:T(2,128)(2,1)S(1)} async-done(((bf16[128,2,128]{2,1,0:T(2,128)(2,1)}), bf16[128,2,128]{2,1,0:T(2,128)(2,1)S(1)}, u32[]{:S(2)}, u32[]{:S(2)}) %all-to-all-start.1) | async-done | bytes 65568 | tf_op jit(solution)/shard_map/all_to_all | solution.py:220
  52.6 0.1 copy.63
  52.7 1.6 %copy.64 = bf16[24,2,2,128,2]{4,3,2,1,0:T(8,128)(2,1)S(1)} copy(bf16[24,2,2,128,2]{3,4,2,1,0:T(2,128)(2,1)S(1)} %bitcast.119) | data formatting | bytes 98304 | tf_op jit(solution)/shard_map/transpose | solution.py:222
  54.3 5.4 %reshape.406.ret_ref = bf16[96,256]{1,0:T(8,128)(2,1)} reshape(bf16[24,2,2,128,2]{4,3,2,1,0:T(8,128)(2,1)S(1)} %copy.64) | data formatting | bytes 98304 | tf_op jit(solution)/shard_map/reshape | solution.py:222
  59.8 8.3 %shard_map.69 = bf16[24,2,2,2160]{3,2,1,0:T(2,128)(2,1)} custom-call(s32[24]{0:T(128)} %orders_ref.3, bf16[96,256]{1,0:T(8,128)(2,1)} %reshape.406.ret_ref, bf16[2,256,128]{2,1,0:T(8,128)(2,1)} %add_convert_fusion.pick_ref, f32[1,128]{1,0:T(1,128)} %bitcast.124, bf16[24,2160,128]{2,1,0:T(8,128)(2,1)} %leg_ref.3), custom_call_target="tpu_custom_call" | custom-call | flops 106168320 | bytes 13734912 | tf_op jit(solution)/shard_map/pallas_call | solution.py:102
  (23 shorter events, 0.3 us)
Async XLA Ops:
  1.3 8.4 %copy-start = (s32[256]{0:T(256)S(1)}, s32[256]{0:T(256)}, u32[]{:S(2)}) copy-start(s32[256]{0:T(256)} %param.8) | copy-start | bytes 3076
  11.1 21.0 %all-to-all-start = ((bf16[128,2,128]{2,1,0:T(2,128)(2,1)}), bf16[128,2,128]{2,1,0:T(2,128)(2,1)S(1)}, u32[]{:S(2)}, u32[]{:S(2)}) async-start(bf16[128,2,128]{2,1,0:T(2,128)(2,1)} %copy.53), calls=%async_computation | async-start | bytes 131072 | tf_op jit(solution)/shard_map/all_to_all | solution.py:197
  38.6 14.0 %all-to-all-start.1 = ((bf16[128,2,128]{2,1,0:T(2,128)(2,1)}), bf16[128,2,128]{2,1,0:T(2,128)(2,1)S(1)}, u32[]{:S(2)}, u32[]{:S(2)}) async-start(bf16[128,2,128]{2,1,0:T(2,128)(2,1)} %reshape.403), calls=%async_computation.1 | async-start | bytes 131072 | tf_op jit(solution)/shard_map/all_to_all | solution.py:220

commit v7 on v4

--- a/solution.py
+++ b/solution.py
@@ -7,6 +7,7 @@
 from jax.experimental.pallas import tpu as pltpu
 from jax.sharding import PartitionSpec as P
 
+ORDER_OUTER = 72
 
 SLOTS_PER_STEP = 12
 
@@ -29,14 +30,18 @@
         masked = jnp.where(usable, rows, zero)
         signed = jnp.where(even, masked, -masked)
         lhs = jnp.concatenate([masked, signed], axis=0)
-        out_ref[i] = jnp.dot(lhs, leg_ref[i], preferred_element_type=jnp.float32).astype(out_ref.dtype)
+        res = jnp.dot(lhs, leg_ref[i], preferred_element_type=jnp.float32)
+        held = jnp.full((1, res.shape[1]), order, jnp.int32).astype(jnp.float32)
+        block_of = jnp.floor((held + 0.5) / ORDER_OUTER)
+        code = jnp.concatenate([block_of, held - ORDER_OUTER * block_of], axis=0)
+        out_ref[i] = jnp.concatenate([res, code], axis=0).astype(out_ref.dtype)
 
 
 def synthesize(coeffs, legendre, orders):
     slot_cap, epochs, parts, deg_count = coeffs.shape
     half_lats = legendre.shape[2]
     block = SLOTS_PER_STEP
-    rows = 2 * epochs * parts
+    rows = 2 * epochs * parts + 2
     grid_spec = pltpu.PrefetchScalarGridSpec(
         num_scalar_prefetch=1,
         grid=(slot_cap // block,),
@@ -164,7 +169,8 @@
     devices = lax.axis_size(("gx", "gy"))
     rows_each = lat_rows // devices
 
-    synth = synthesize(coeffs, legendre, orders).reshape(slot_cap, 2, epoch_count * 2, half_lats)
+    synth_out = synthesize(coeffs, legendre, orders)
+    synth = synth_out[:, :-2].reshape(slot_cap, 2, epoch_count * 2, half_lats)
     full_lats = jnp.concatenate([synth[:, 0], synth[:, 1, :, ::-1]], axis=-1)
 
     onehot = one_hot_rows(lat_map, lat_rows)
@@ -176,8 +182,8 @@
     inner = inner_length(lon_count)
     outer = lon_count // inner
     blocks = deg_count // outer
-    block_of = jnp.where(orders >= 0, orders // outer, -1)
-    order_code = jnp.stack([block_of, orders % outer], axis=-1).astype(jnp.bfloat16)
+    assert outer == ORDER_OUTER
+    order_code = synth_out[:, -2:, 0]
     order_code = jnp.broadcast_to(order_code[None], (devices, slot_cap, 2))
     payload = jnp.concatenate([sends, order_code], axis=-1).reshape(devices, -1)
     width = payload.shape[1]

time: 62.4 us -> 62.8 us (level)
  local copies, waits for them, and re-layouts: 6.82 us -> 7.79 us
  other arithmetic: 2.17 us -> 1.49 us
    slice x0 -> x3, local copies, waits for them, and re-layouts: none -> 1.71 us  [the longest x2 0.91 us: shards(): order_code = synth_out[:, -2:, 0]]
    slice x1, local copies, waits for them, and re-layouts: 0.77 us -> 0.02 us  [shards(): full_lats = jnp.concatenate([synth[:, 0], synth[:, 1, :, ::-1]], axis=-1)]
    another operation x3 -> x1, other arithmetic: 0.71 us -> 0.02 us  [the longest x2 0.69 us: shards(): jnp.stack([block_of, orders % outer], axis=-1).astype(jnp.bfloat16)]
where the time goes in v7:
time: 62.8 us; the launch traced here: 62.5 us
  waiting for transfers between devices  17.5 us (28%)
  starting transfers between devices  16 us (25%)
  Pallas kernels  15.6 us (25%)
  local copies, waits for them, and re-layouts  7.79 us (12%)
  matrix products  3.12 us (5%)
  other arithmetic  1.49 us (2%)
  between operations  0.99 us (2%)
    all_to_all x1, starting transfers between devices, shards(): got = lax.all_to_all(payload, ('gx', 'gy'), 0, 0, tiled=True)  11.5 us
    all_to_all x1, waiting for transfers between devices, shards(): got = lax.all_to_all(payload, ('gx', 'gy'), 0, 0, tiled=True)  8.87 us
    all_to_all x1, waiting for transfers between devices, shards(): back = lax.all_to_all(back, ('gx', 'gy'), 0, 0, tiled=True)  8.62 us
    pallas_call x1, Pallas kernels, analyze(): pl.pallas_call(_analysis_kernel, grid_spec=grid_spec, out_shape=jax.Shape...  8.13 us
    pallas_call x1, Pallas kernels, synthesize(): pl.pallas_call(_synth_kernel, grid_spec=grid_spec, out_shape=jax.ShapeDty...  7.47 us
    all_to_all x1, starting transfers between devices, shards(): back = lax.all_to_all(back, ('gx', 'gy'), 0, 0, tiled=True)  4.48 us
    dot_general x4, matrix products, mm(): return jnp.einsum(spec, left, right, precision=highest)  1.42 us
  transfers between devices with their start and end apart: 2, of which 2 were waited for; matrix products, arithmetic and copies ran while one was open for 2% of the time, Pallas kernels for 0%

profile of v7, /device:TPU:1, one launch (start us, length us, event | category | flops | bytes accessed | tf_op | source)
XLA Modules:
  0.0 62.5 jit_solution(2740053411834626752)
XLA Ops:
  0.6 0.0 copy-start
  0.6 7.5 %shard_map.68 = bf16[24,10,128]{2,1,0:T(8,128)(2,1)} custom-call(s32[24]{0:T(128)} %orders_ref.3, bf16[24,2,2,2160]{3,2,1,0:T(2,128)(2,1)} %coef_ref.1, bf16[24,2160,128]{2,1,0:T(8,128)(2,1)} %leg_ref.3), custom_call_target="tpu_custom_call" | custom-call | flops 132710400 | bytes 13747200 | tf_op jit(solution)/shard_map/pallas_call | solution.py:54
  8.1 0.8 %slice.83 = bf16[24,8,128]{2,1,0:T(8,128)(2,1)S(1)} slice(bf16[24,10,128]{2,1,0:T(8,128)(2,1)} %shard_map.68), slice={[0:24], [0:8], [0:128]} | slice | bytes 98304 | tf_op jit(solution)/shard_map/slice | solution.py:173
  8.9 0.8 %slice.86 = bf16[24,2,1]{2,1,0:T(2,128)(2,1)S(1)} slice(bf16[24,10,128]{2,1,0:T(8,128)(2,1)} %shard_map.68), slice={[0:24], [8:10], [0:1]} | slice | bytes 192 | tf_op jit(solution)/shard_map/slice | solution.py:186
  9.8 0.1 rev.6
  9.9 0.0 copy-done
  9.9 0.2 convolution_convert_fusion
  10.1 0.2 copy.61
  10.2 0.1 copy.62
  10.3 0.1 copy.63
  10.4 0.1 broadcast_in_dim.39
  10.6 0.8 %copy.65 = bf16[128,2,128]{2,1,0:T(2,128)(2,1)} copy(bf16[128,2,128]{0,2,1:T(8,128)(2,1)S(1)} %bitcast.110) | data formatting | bytes 131072 | tf_op jit(solution)/shard_map/reshape | solution.py:191
  11.4 11.5 %all-to-all-start = ((bf16[128,2,128]{2,1,0:T(2,128)(2,1)}), bf16[128,2,128]{2,1,0:T(2,128)(2,1)S(1)}, u32[]{:S(2)}, u32[]{:S(2)}) async-start(bf16[128,2,128]{2,1,0:T(2,128)(2,1)} %copy.65), calls=%async_computation | async-start | bytes 131072 | tf_op jit(solution)/shard_map/all_to_all | solution.py:192
  22.9 0.1 fusion.55
  23.0 0.1 fusion.58
  23.1 0.2 sine_negate_fusion
  23.3 0.1 select_multiply_fusion
  23.4 0.2 fusion.48
  23.5 8.9 %all-to-all-done = bf16[128,2,128]{2,1,0:T(2,128)(2,1)S(1)} async-done(((bf16[128,2,128]{2,1,0:T(2,128)(2,1)}), bf16[128,2,128]{2,1,0:T(2,128)(2,1)S(1)}, u32[]{:S(2)}, u32[]{:S(2)}) %all-to-all-start) | async-done | bytes 65568 | tf_op jit(solution)/shard_map/all_to_all | solution.py:192
  32.4 0.6 reshape.306
  33.0 1.0 %slice_reduce_fusion.1 = (bf16[3072]{0:T(1024)(128)(2,1)S(1)}, bf16[3072]{0:T(1024)(128)(2,1)S(1)}) fusion(bf16[3072,10]{1,0:T(8,128)(2,1)S(1)} %reshape.306), kind=kLoop, calls=%fused_computation.15 | loop fusion | bytes 24576 | tf_op jit(solution)/shard_map/slice | solution.py:195
  34.0 0.1 iota_compare_fusion.4
  34.1 0.3 copy.66
  34.3 0.6 fusion
  35.0 0.4 convolution_bitcast_fusion.1
  35.5 0.4 fusion.5
  35.8 0.3 convolution_bitcast_fusion
  36.2 0.3 convolution_bitcast_fusion.3
  36.6 0.0 copy-start.1
  36.6 0.7 %fusion.3 = bf16[3072,8]{0,1:T(8,128)(2,1)S(1)} fusion(bf16[30,72,8]{1,0,2:T(8,128)(2,1)S(1)} %bitcast.119, pred[3072,30]{0,1:T(8,128)(4,1)S(1)} %iota_compare_fusion.4, bf16[3072]{0:T(1024)(128)(2,1)S(1)} %get-tuple-element.2), kind=kOutput, calls=%fused_computation.4 | convolution fusion | flops 108281856 | bytes 182016 | tf_op jit(solution)/shard_map/sd,cdr->scr/dot_general | solution.py:209
  37.4 0.4 copy.74
  37.7 0.5 convert_element_type.114
  38.3 0.7 %reshape.310 = bf16[128,2,128]{2,1,0:T(2,128)(2,1)} reshape(bf16[128,256]{1,0:T(8,128)(2,1)S(1)} %pad.9) | data formatting | bytes 131072 | tf_op jit(solution)/shard_map/reshape | solution.py:214
  38.9 4.5 %all-to-all-start.1 = ((bf16[128,2,128]{2,1,0:T(2,128)(2,1)}), bf16[128,2,128]{2,1,0:T(2,128)(2,1)S(1)}, u32[]{:S(2)}, u32[]{:S(2)}) async-start(bf16[128,2,128]{2,1,0:T(2,128)(2,1)} %reshape.310), calls=%async_computation.1 | async-start | bytes 131072 | tf_op jit(solution)/shard_map/all_to_all | solution.py:215
  43.4 0.1 copy.70
  43.5 0.8 %reshape_reshape.3 = bf16[2,2,4320]{2,1,0:T(2,128)(2,1)} reshape(bf16[4,72,60]{2,1,0:T(8,128)(2,1)S(1)} %copy.70) | data formatting | bytes 69120 | tf_op jit(solution)/shard_map/reshape;reshape | solution.py:203
  44.3 8.6 %all-to-all-done.1 = bf16[128,2,128]{2,1,0:T(2,128)(2,1)S(1)} async-done(((bf16[128,2,128]{2,1,0:T(2,128)(2,1)}), bf16[128,2,128]{2,1,0:T(2,128)(2,1)S(1)}, u32[]{:S(2)}, u32[]{:S(2)}) %all-to-all-start.1) | async-done | bytes 65568 | tf_op jit(solution)/shard_map/all_to_all | solution.py:215
  52.9 0.1 copy.75
  53.1 0.2 copy.76
  53.2 0.2 fusion.16
  53.5 0.1 rev.7
  53.6 0.0 copy-done.1
  53.7 0.6 %pad_maximum_fusion.5.both_ref = bf16[24,8,128]{2,1,0:T(8,128)(2,1)} fusion(bf16[24,4,128]{2,1,0:T(4,128)(2,1)S(1)} %get-tuple-element.13, bf16[24,4,128]{2,1,0:T(4,128)(2,1)S(1)} %get-tuple-element.12), kind=kLoop, calls=%fused_computation.61 | loop fusion | flops 98304 | bytes 98304 | tf_op jit(solution)/shard_map/concatenate | solution.py:225
  54.3 8.1 %shard_map.69 = bf16[24,2,2,2160]{3,2,1,0:T(2,128)(2,1)} custom-call(s32[24]{0:T(128)} %orders_ref.3, bf16[24,8,128]{2,1,0:T(8,128)(2,1)} %pad_maximum_fusion.5.both_ref, bf16[24,2160,128]{2,1,0:T(8,128)(2,1)} %leg_ref.3), custom_call_target="tpu_custom_call" | custom-call | flops 106168320 | bytes 13734912 | tf_op jit(solution)/shard_map/pallas_call | solution.py:96
  (25 shorter events, 0.4 us)
Async XLA Ops:
  0.6 9.2 %copy-start = (s32[256]{0:T(256)S(1)}, s32[256]{0:T(256)}, u32[]{:S(2)}) copy-start(s32[256]{0:T(256)} %param.8) | copy-start | bytes 3076
  11.4 21.0 %all-to-all-start = ((bf16[128,2,128]{2,1,0:T(2,128)(2,1)}), bf16[128,2,128]{2,1,0:T(2,128)(2,1)S(1)}, u32[]{:S(2)}, u32[]{:S(2)}) async-start(bf16[128,2,128]{2,1,0:T(2,128)(2,1)} %copy.65), calls=%async_computation | async-start | bytes 131072 | tf_op jit(solution)/shard_map/all_to_all | solution.py:192
  36.6 17.0 %copy-start.1 = (f32[128]{0:T(128)S(1)}, f32[128]{0:T(128)}, u32[]{:S(2)}) copy-start(f32[128]{0:T(128)} %param.9) | copy-start | bytes 1540
  38.9 14.0 %all-to-all-start.1 = ((bf16[128,2,128]{2,1,0:T(2,128)(2,1)}), bf16[128,2,128]{2,1,0:T(2,128)(2,1)S(1)}, u32[]{:S(2)}, u32[]{:S(2)}) async-start(bf16[128,2,128]{2,1,0:T(2,128)(2,1)} %reshape.310), calls=%async_computation.1 | async-start | bytes 131072 | tf_op jit(solution)/shard_map/all_to_all | solution.py:215

commit v8 on v7

--- a/solution.py
+++ b/solution.py
@@ -19,7 +19,7 @@
     return usable, even
 
 
-def _synth_kernel(orders_ref, coef_ref, leg_ref, out_ref):
+def _synth_kernel(orders_ref, coef_ref, leg_ref, out_ref, code_ref):
     step = pl.program_id(0)
     block, epochs, _, deg_count = coef_ref.shape
     zero = jnp.zeros((), coef_ref.dtype)
@@ -34,14 +34,15 @@
         held = jnp.full((1, res.shape[1]), order, jnp.int32).astype(jnp.float32)
         block_of = jnp.floor((held + 0.5) / ORDER_OUTER)
         code = jnp.concatenate([block_of, held - ORDER_OUTER * block_of], axis=0)
-        out_ref[i] = jnp.concatenate([res, code], axis=0).astype(out_ref.dtype)
+        out_ref[i] = res.astype(out_ref.dtype)
+        code_ref[i] = code.astype(code_ref.dtype)
 
 
 def synthesize(coeffs, legendre, orders):
     slot_cap, epochs, parts, deg_count = coeffs.shape
     half_lats = legendre.shape[2]
     block = SLOTS_PER_STEP
-    rows = 2 * epochs * parts + 2
+    rows = 2 * epochs * parts
     grid_spec = pltpu.PrefetchScalarGridSpec(
         num_scalar_prefetch=1,
         grid=(slot_cap // block,),
@@ -49,12 +50,18 @@
             pl.BlockSpec((block, epochs, parts, deg_count), lambda g, o: (g, 0, 0, 0)),
             pl.BlockSpec((block, deg_count, half_lats), lambda g, o: (g, 0, 0)),
         ],
-        out_specs=pl.BlockSpec((block, rows, half_lats), lambda g, o: (g, 0, 0)),
+        out_specs=[
+            pl.BlockSpec((block, rows, half_lats), lambda g, o: (g, 0, 0)),
+            pl.BlockSpec((block, 2, half_lats), lambda g, o: (g, 0, 0)),
+        ],
     )
     return pl.pallas_call(
         _synth_kernel,
         grid_spec=grid_spec,
-        out_shape=jax.ShapeDtypeStruct((slot_cap, rows, half_lats), jnp.bfloat16),
+        out_shape=[
+            jax.ShapeDtypeStruct((slot_cap, rows, half_lats), jnp.bfloat16),
+            jax.ShapeDtypeStruct((slot_cap, 2, half_lats), jnp.bfloat16),
+        ],
         compiler_params=pltpu.CompilerParams(dimension_semantics=("arbitrary",)),
         cost_estimate=pl.CostEstimate(
             flops=2 * slot_cap * rows * deg_count * half_lats,
@@ -169,8 +176,8 @@
     devices = lax.axis_size(("gx", "gy"))
     rows_each = lat_rows // devices
 
-    synth_out = synthesize(coeffs, legendre, orders)
-    synth = synth_out[:, :-2].reshape(slot_cap, 2, epoch_count * 2, half_lats)
+    synth, codes = synthesize(coeffs, legendre, orders)
+    synth = synth.reshape(slot_cap, 2, epoch_count * 2, half_lats)
     full_lats = jnp.concatenate([synth[:, 0], synth[:, 1, :, ::-1]], axis=-1)
 
     onehot = one_hot_rows(lat_map, lat_rows)
@@ -183,7 +190,7 @@
     outer = lon_count // inner
     blocks = deg_count // outer
     assert outer == ORDER_OUTER
-    order_code = synth_out[:, -2:, 0]
+    order_code = codes[:, :, 0]
     order_code = jnp.broadcast_to(order_code[None], (devices, slot_cap, 2))
     payload = jnp.concatenate([sends, order_code], axis=-1).reshape(devices, -1)
     width = payload.shape[1]

time: 62.8 us -> 62.6 us (level)
    slice x3 -> x1, local copies, waits for them, and re-layouts: 1.71 us -> 0.82 us  [shards(): order_code = codes[:, :, 0]]
    slice x1, local copies, waits for them, and re-layouts: 0.02 us -> 0.77 us  [shards(): full_lats = jnp.concatenate([synth[:, 0], synth[:, 1, :, ::-1]], axis=-1)]
where the time goes in v8:
time: 62.6 us; the launch traced here: 62.3 us
  waiting for transfers between devices  17.5 us (28%)
  starting transfers between devices  16 us (26%)
  Pallas kernels  15.6 us (25%)
  local copies, waits for them, and re-layouts  7.64 us (12%)
  matrix products  3.12 us (5%)
  other arithmetic  1.48 us (2%)
  between operations  0.98 us (2%)
    all_to_all x1, starting transfers between devices, shards(): got = lax.all_to_all(payload, ('gx', 'gy'), 0, 0, tiled=True)  11.5 us
    all_to_all x1, waiting for transfers between devices, shards(): got = lax.all_to_all(payload, ('gx', 'gy'), 0, 0, tiled=True)  8.87 us
    all_to_all x1, waiting for transfers between devices, shards(): back = lax.all_to_all(back, ('gx', 'gy'), 0, 0, tiled=True)  8.62 us
    pallas_call x1, Pallas kernels, analyze(): pl.pallas_call(_analysis_kernel, grid_spec=grid_spec, out_shape=jax.Shape...  8.13 us
    pallas_call x1, Pallas kernels, synthesize(): pl.pallas_call(_synth_kernel, grid_spec=grid_spec, out_shape=[jax.ShapeDt...  7.46 us
    all_to_all x1, starting transfers between devices, shards(): back = lax.all_to_all(back, ('gx', 'gy'), 0, 0, tiled=True)  4.47 us
    dot_general x4, matrix products, mm(): return jnp.einsum(spec, left, right, precision=highest)  1.43 us
  transfers between devices with their start and end apart: 2, of which 2 were waited for; matrix products, arithmetic and copies ran while one was open for 2% of the time, Pallas kernels for 0%

profile of v8, /device:TPU:1, one launch (start us, length us, event | category | flops | bytes accessed | tf_op | source)
XLA Modules:
  0.0 62.3 jit_solution(14664998660563279293)
XLA Ops:
  0.6 0.0 copy-start
  0.6 7.5 %shard_map.68 = (bf16[24,8,128]{2,1,0:T(8,128)(2,1)}, bf16[24,2,128]{2,1,0:T(2,128)(2,1)}) custom-call(s32[24]{0:T(128)} %orders_ref.3, bf16[24,2,2,2160]{3,2,1,0:T(2,128)(2,1)} %coef_ref.1, bf16[24,2160,128]{2,1,0:T(8,128)(2,1)} %leg_ref.3), custom_call_target="tpu_custom_call" | custom-call | flops 106168320 | bytes 13734912 | tf_op jit(solution)/shard_map/pallas_call | solution.py:58
  8.1 0.8 %fusion.67 = (bf16[24,1,4,128]{3,2,1,0:T(4,128)(2,1)S(1)}, bf16[24,1,4,128]{3,2,1,0:T(4,128)(2,1)S(1)}) fusion(bf16[24,2,4,128]{3,2,1,0:T(4,128)(2,1)} %bitcast.120), kind=kLoop, calls=%fused_computation.111 | loop fusion | bytes 98304 | tf_op jit(solution)/shard_map/slice | solution.py:181
  8.9 0.1 rev.6
  9.0 0.0 copy-done
  9.0 0.2 convolution_convert_fusion
  9.2 0.2 copy.61
  9.4 0.1 copy.62
  9.5 0.8 %copy.63 = bf16[24,2,1]{0,1,2:T(2,128)(2,1)S(1)} copy(bf16[24,2,1]{2,1,0:T(2,128)(2,1)} %bitcast.123) | data formatting | bytes 192 | tf_op jit(solution)/shard_map/slice | solution.py:193
  10.3 0.1 broadcast_in_dim.39
  10.5 0.8 %copy.65 = bf16[128,2,128]{2,1,0:T(2,128)(2,1)} copy(bf16[128,2,128]{0,2,1:T(8,128)(2,1)S(1)} %bitcast.111) | data formatting | bytes 131072 | tf_op jit(solution)/shard_map/reshape | solution.py:198
  11.2 11.5 %all-to-all-start = ((bf16[128,2,128]{2,1,0:T(2,128)(2,1)}), bf16[128,2,128]{2,1,0:T(2,128)(2,1)S(1)}, u32[]{:S(2)}, u32[]{:S(2)}) async-start(bf16[128,2,128]{2,1,0:T(2,128)(2,1)} %copy.65), calls=%async_computation | async-start | bytes 131072 | tf_op jit(solution)/shard_map/all_to_all | solution.py:199
  22.7 0.1 fusion.55
  22.8 0.1 fusion.58
  22.9 0.2 sine_negate_fusion
  23.1 0.1 select_multiply_fusion
  23.2 0.2 fusion.48
  23.4 8.9 %all-to-all-done = bf16[128,2,128]{2,1,0:T(2,128)(2,1)S(1)} async-done(((bf16[128,2,128]{2,1,0:T(2,128)(2,1)}), bf16[128,2,128]{2,1,0:T(2,128)(2,1)S(1)}, u32[]{:S(2)}, u32[]{:S(2)}) %all-to-all-start) | async-done | bytes 65568 | tf_op jit(solution)/shard_map/all_to_all | solution.py:199
  32.2 0.6 reshape.306
  32.8 1.0 %slice_reduce_fusion.1 = (bf16[3072]{0:T(1024)(128)(2,1)S(1)}, bf16[3072]{0:T(1024)(128)(2,1)S(1)}) fusion(bf16[3072,10]{1,0:T(8,128)(2,1)S(1)} %reshape.306), kind=kLoop, calls=%fused_computation.15 | loop fusion | bytes 24576 | tf_op jit(solution)/shard_map/slice | solution.py:202
  33.9 0.1 iota_compare_fusion.4
  33.9 0.2 copy.66
  34.2 0.6 fusion
  34.8 0.4 convolution_bitcast_fusion.1
  35.3 0.4 fusion.5
  35.7 0.3 convolution_bitcast_fusion
  36.0 0.3 convolution_bitcast_fusion.3
  36.4 0.0 copy-start.1
  36.5 0.7 %fusion.3 = bf16[3072,8]{0,1:T(8,128)(2,1)S(1)} fusion(bf16[30,72,8]{1,0,2:T(8,128)(2,1)S(1)} %bitcast.119, pred[3072,30]{0,1:T(8,128)(4,1)S(1)} %iota_compare_fusion.4, bf16[3072]{0:T(1024)(128)(2,1)S(1)} %get-tuple-element.6), kind=kOutput, calls=%fused_computation.4 | convolution fusion | flops 108281856 | bytes 182016 | tf_op jit(solution)/shard_map/sd,cdr->scr/dot_general | solution.py:216
  37.2 0.4 copy.74
  37.6 0.5 convert_element_type.114
  38.1 0.7 %reshape.310 = bf16[128,2,128]{2,1,0:T(2,128)(2,1)} reshape(bf16[128,256]{1,0:T(8,128)(2,1)S(1)} %pad.9) | data formatting | bytes 131072 | tf_op jit(solution)/shard_map/reshape | solution.py:221
  38.7 4.5 %all-to-all-start.1 = ((bf16[128,2,128]{2,1,0:T(2,128)(2,1)}), bf16[128,2,128]{2,1,0:T(2,128)(2,1)S(1)}, u32[]{:S(2)}, u32[]{:S(2)}) async-start(bf16[128,2,128]{2,1,0:T(2,128)(2,1)} %reshape.310), calls=%async_computation.1 | async-start | bytes 131072 | tf_op jit(solution)/shard_map/all_to_all | solution.py:222
  43.2 0.1 copy.70
  43.3 0.8 %reshape_reshape.3 = bf16[2,2,4320]{2,1,0:T(2,128)(2,1)} reshape(bf16[4,72,60]{2,1,0:T(8,128)(2,1)S(1)} %copy.70) | data formatting | bytes 69120 | tf_op jit(solution)/shard_map/reshape;reshape | solution.py:210
  44.1 8.6 %all-to-all-done.1 = bf16[128,2,128]{2,1,0:T(2,128)(2,1)S(1)} async-done(((bf16[128,2,128]{2,1,0:T(2,128)(2,1)}), bf16[128,2,128]{2,1,0:T(2,128)(2,1)S(1)}, u32[]{:S(2)}, u32[]{:S(2)}) %all-to-all-start.1) | async-done | bytes 65568 | tf_op jit(solution)/shard_map/all_to_all | solution.py:222
  52.7 0.1 copy.75
  52.9 0.2 copy.76
  53.1 0.2 fusion.16
  53.3 0.1 rev.7
  53.5 0.0 copy-done.1
  53.5 0.6 %pad_maximum_fusion.5.both_ref = bf16[24,8,128]{2,1,0:T(8,128)(2,1)} fusion(bf16[24,4,128]{2,1,0:T(4,128)(2,1)S(1)} %get-tuple-element.17, bf16[24,4,128]{2,1,0:T(4,128)(2,1)S(1)} %get-tuple-element.16), kind=kLoop, calls=%fused_computation.61 | loop fusion | flops 98304 | bytes 98304 | tf_op jit(solution)/shard_map/concatenate | solution.py:232
  54.1 8.1 %shard_map.69 = bf16[24,2,2,2160]{3,2,1,0:T(2,128)(2,1)} custom-call(s32[24]{0:T(128)} %orders_ref.3, bf16[24,8,128]{2,1,0:T(8,128)(2,1)} %pad_maximum_fusion.5.both_ref, bf16[24,2160,128]{2,1,0:T(8,128)(2,1)} %leg_ref.3), custom_call_target="tpu_custom_call" | custom-call | flops 106168320 | bytes 13734912 | tf_op jit(solution)/shard_map/pallas_call | solution.py:103
  (24 shorter events, 0.3 us)
Async XLA Ops:
  0.6 8.4 %copy-start = (s32[256]{0:T(256)S(1)}, s32[256]{0:T(256)}, u32[]{:S(2)}) copy-start(s32[256]{0:T(256)} %param.8) | copy-start | bytes 3076
  11.2 21.0 %all-to-all-start = ((bf16[128,2,128]{2,1,0:T(2,128)(2,1)}), bf16[128,2,128]{2,1,0:T(2,128)(2,1)S(1)}, u32[]{:S(2)}, u32[]{:S(2)}) async-start(bf16[128,2,128]{2,1,0:T(2,128)(2,1)} %copy.65), calls=%async_computation | async-start | bytes 131072 | tf_op jit(solution)/shard_map/all_to_all | solution.py:199
  36.4 17.0 %copy-start.1 = (f32[128]{0:T(128)S(1)}, f32[128]{0:T(128)}, u32[]{:S(2)}) copy-start(f32[128]{0:T(128)} %param.9) | copy-start | bytes 1540
  38.7 14.0 %all-to-all-start.1 = ((bf16[128,2,128]{2,1,0:T(2,128)(2,1)}), bf16[128,2,128]{2,1,0:T(2,128)(2,1)S(1)}, u32[]{:S(2)}, u32[]{:S(2)}) async-start(bf16[128,2,128]{2,1,0:T(2,128)(2,1)} %reshape.310), calls=%async_computation.1 | async-start | bytes 131072 | tf_op jit(solution)/shard_map/all_to_all | solution.py:222

commit v9 on v4

--- a/solution.py
+++ b/solution.py
@@ -118,7 +118,7 @@
 
 
 def transform_blocks(x_parts, lon_count):
-    highest = lax.Precision.HIGHEST
+    highest = lax.Precision.HIGH
     _, outer, blocks, signals = x_parts.shape
     inner = lon_count // outer
     a_idx = jnp.arange(outer, dtype=jnp.int32)

time: 62.4 us -> 62.1 us (level)
  no operation moved by 1% of the time
where the time goes in v9:
time: 62.1 us; the launch traced here: 61.8 us
  waiting for transfers between devices  17.5 us (28%)
  starting transfers between devices  16 us (26%)
  Pallas kernels  15.6 us (25%)
  local copies, waits for them, and re-layouts  6.82 us (11%)
  matrix products  2.78 us (4%)
  other arithmetic  2.17 us (3%)
  between operations  0.98 us (2%)
    all_to_all x1, starting transfers between devices, shards(): got = lax.all_to_all(payload, ('gx', 'gy'), 0, 0, tiled=True)  11.5 us
    all_to_all x1, waiting for transfers between devices, shards(): got = lax.all_to_all(payload, ('gx', 'gy'), 0, 0, tiled=True)  8.87 us
    all_to_all x1, waiting for transfers between devices, shards(): back = lax.all_to_all(back, ('gx', 'gy'), 0, 0, tiled=True)  8.62 us
    pallas_call x1, Pallas kernels, analyze(): pl.pallas_call(_analysis_kernel, grid_spec=grid_spec, out_shape=jax.Shape...  8.13 us
    pallas_call x1, Pallas kernels, synthesize(): pl.pallas_call(_synth_kernel, grid_spec=grid_spec, out_shape=jax.ShapeDty...  7.45 us
    all_to_all x1, starting transfers between devices, shards(): back = lax.all_to_all(back, ('gx', 'gy'), 0, 0, tiled=True)  4.48 us
  transfers between devices with their start and end apart: 2, of which 2 were waited for; matrix products, arithmetic and copies ran while one was open for 2% of the time, Pallas kernels for 0%

profile of v9, /device:TPU:1, one launch (start us, length us, event | category | flops | bytes accessed | tf_op | source)
XLA Modules:
  0.0 61.8 jit_solution(2114265820258638389)
XLA Ops:
  0.6 0.7 %convert_bitcast_fusion = (bf16[24,1]{0,1:T(2,128)(2,1)S(1)}, bf16[24,1]{0,1:T(2,128)(2,1)S(1)}) fusion(s32[24]{0:T(128)} %orders_ref.3), kind=kLoop, calls=%fused_computation.109 | loop fusion | flops 384 | bytes 192 | tf_op jit(solution)/shard_map/stack | solution.py:180
  1.3 0.0 copy-start
  1.3 7.5 %shard_map.68 = bf16[24,8,128]{2,1,0:T(8,128)(2,1)} custom-call(s32[24]{0:T(128)} %orders_ref.3, bf16[24,2,2,2160]{3,2,1,0:T(2,128)(2,1)} %coef_ref.1, bf16[24,2160,128]{2,1,0:T(8,128)(2,1)} %leg_ref.3), custom_call_target="tpu_custom_call" | custom-call | flops 106168320 | bytes 13734912 | tf_op jit(solution)/shard_map/pallas_call | solution.py:49
  8.8 0.8 %fusion.69 = (bf16[24,1,4,128]{3,2,1,0:T(4,128)(2,1)S(1)}, bf16[24,1,4,128]{3,2,1,0:T(4,128)(2,1)S(1)}) fusion(bf16[24,2,4,128]{3,2,1,0:T(4,128)(2,1)} %bitcast.118), kind=kLoop, calls=%fused_computation.118 | loop fusion | bytes 98304 | tf_op jit(solution)/shard_map/slice | solution.py:168
  9.6 0.1 rev.6
  9.7 0.0 copy-done
  9.7 0.2 convolution_convert_fusion
  9.8 0.2 copy.58
  10.0 0.1 copy.59
  10.2 0.1 broadcast_in_dim.36
  10.3 0.8 %copy.61 = bf16[128,2,128]{2,1,0:T(2,128)(2,1)} copy(bf16[128,2,128]{0,2,1:T(8,128)(2,1)S(1)} %bitcast.113) | data formatting | bytes 131072 | tf_op jit(solution)/shard_map/reshape | solution.py:185
  11.1 11.5 %all-to-all-start = ((bf16[128,2,128]{2,1,0:T(2,128)(2,1)}), bf16[128,2,128]{2,1,0:T(2,128)(2,1)S(1)}, u32[]{:S(2)}, u32[]{:S(2)}) async-start(bf16[128,2,128]{2,1,0:T(2,128)(2,1)} %copy.61), calls=%async_computation | async-start | bytes 131072 | tf_op jit(solution)/shard_map/all_to_all | solution.py:186
  22.6 0.1 fusion.55
  22.7 0.1 fusion.58
  22.8 0.2 sine_negate_fusion
  23.0 0.1 select_multiply_fusion
  23.1 0.2 fusion.48
  23.2 8.9 %all-to-all-done = bf16[128,2,128]{2,1,0:T(2,128)(2,1)S(1)} async-done(((bf16[128,2,128]{2,1,0:T(2,128)(2,1)}), bf16[128,2,128]{2,1,0:T(2,128)(2,1)S(1)}, u32[]{:S(2)}, u32[]{:S(2)}) %all-to-all-start) | async-done | bytes 65568 | tf_op jit(solution)/shard_map/all_to_all | solution.py:186
  32.1 0.6 reshape.324
  32.7 1.0 %slice_reduce_fusion.1 = (bf16[3072]{0:T(1024)(128)(2,1)S(1)}, bf16[3072]{0:T(1024)(128)(2,1)S(1)}) fusion(bf16[3072,10]{1,0:T(8,128)(2,1)S(1)} %reshape.324), kind=kLoop, calls=%fused_computation.15 | loop fusion | bytes 24576 | tf_op jit(solution)/shard_map/slice | solution.py:189
  33.7 0.1 iota_compare_fusion.4
  33.8 0.2 copy.62
  34.0 0.6 fusion
  34.7 0.3 convolution_bitcast_fusion.1
  35.1 0.3 fusion.5
  35.3 0.3 convolution_bitcast_fusion
  35.6 0.3 convolution_bitcast_fusion.3
  36.0 0.0 copy-start.1
  36.0 0.7 %fusion.3 = bf16[3072,8]{0,1:T(8,128)(2,1)S(1)} fusion(bf16[30,72,8]{1,0,2:T(8,128)(2,1)S(1)} %bitcast.122, pred[3072,30]{0,1:T(8,128)(4,1)S(1)} %iota_compare_fusion.4, bf16[3072]{0:T(1024)(128)(2,1)S(1)} %get-tuple-element.2), kind=kOutput, calls=%fused_computation.4 | convolution fusion | flops 108281856 | bytes 182016 | tf_op jit(solution)/shard_map/sd,cdr->scr/dot_general | solution.py:203
  36.7 0.4 copy.70
  37.1 0.5 convert_element_type.119
  37.6 0.7 %reshape.328 = bf16[128,2,128]{2,1,0:T(2,128)(2,1)} reshape(bf16[128,256]{1,0:T(8,128)(2,1)S(1)} %pad.9) | data formatting | bytes 131072 | tf_op jit(solution)/shard_map/reshape | solution.py:208
  38.3 4.5 %all-to-all-start.1 = ((bf16[128,2,128]{2,1,0:T(2,128)(2,1)}), bf16[128,2,128]{2,1,0:T(2,128)(2,1)S(1)}, u32[]{:S(2)}, u32[]{:S(2)}) async-start(bf16[128,2,128]{2,1,0:T(2,128)(2,1)} %reshape.328), calls=%async_computation.1 | async-start | bytes 131072 | tf_op jit(solution)/shard_map/all_to_all | solution.py:209
  42.7 0.1 copy.66
  42.9 0.8 %reshape_reshape.3 = bf16[2,2,4320]{2,1,0:T(2,128)(2,1)} reshape(bf16[4,72,60]{2,1,0:T(8,128)(2,1)S(1)} %copy.66) | data formatting | bytes 69120 | tf_op jit(solution)/shard_map/reshape;reshape | solution.py:197
  43.6 8.6 %all-to-all-done.1 = bf16[128,2,128]{2,1,0:T(2,128)(2,1)S(1)} async-done(((bf16[128,2,128]{2,1,0:T(2,128)(2,1)}), bf16[128,2,128]{2,1,0:T(2,128)(2,1)S(1)}, u32[]{:S(2)}, u32[]{:S(2)}) %all-to-all-start.1) | async-done | bytes 65568 | tf_op jit(solution)/shard_map/all_to_all | solution.py:209
  52.3 0.1 copy.71
  52.4 0.2 copy.72
  52.6 0.2 fusion.16
  52.9 0.1 rev.7
  53.0 0.0 copy-done.1
  53.0 0.6 %pad_maximum_fusion.5.both_ref = bf16[24,8,128]{2,1,0:T(8,128)(2,1)} fusion(bf16[24,4,128]{2,1,0:T(4,128)(2,1)S(1)} %get-tuple-element.13, bf16[24,4,128]{2,1,0:T(4,128)(2,1)S(1)} %get-tuple-element.12), kind=kLoop, calls=%fused_computation.61 | loop fusion | flops 98304 | bytes 98304 | tf_op jit(solution)/shard_map/concatenate | solution.py:219
  53.7 8.1 %shard_map.69 = bf16[24,2,2,2160]{3,2,1,0:T(2,128)(2,1)} custom-call(s32[24]{0:T(128)} %orders_ref.3, bf16[24,8,128]{2,1,0:T(8,128)(2,1)} %pad_maximum_fusion.5.both_ref, bf16[24,2160,128]{2,1,0:T(8,128)(2,1)} %leg_ref.3), custom_call_target="tpu_custom_call" | custom-call | flops 106168320 | bytes 13734912 | tf_op jit(solution)/shard_map/pallas_call | solution.py:91
  (25 shorter events, 0.4 us)
Async XLA Ops:
  1.3 8.4 %copy-start = (s32[256]{0:T(256)S(1)}, s32[256]{0:T(256)}, u32[]{:S(2)}) copy-start(s32[256]{0:T(256)} %param.8) | copy-start | bytes 3076
  11.1 21.0 %all-to-all-start = ((bf16[128,2,128]{2,1,0:T(2,128)(2,1)}), bf16[128,2,128]{2,1,0:T(2,128)(2,1)S(1)}, u32[]{:S(2)}, u32[]{:S(2)}) async-start(bf16[128,2,128]{2,1,0:T(2,128)(2,1)} %copy.61), calls=%async_computation | async-start | bytes 131072 | tf_op jit(solution)/shard_map/all_to_all | solution.py:186
  36.0 17.0 %copy-start.1 = (f32[128]{0:T(128)S(1)}, f32[128]{0:T(128)}, u32[]{:S(2)}) copy-start(f32[128]{0:T(128)} %param.9) | copy-start | bytes 1540
  38.3 14.0 %all-to-all-start.1 = ((bf16[128,2,128]{2,1,0:T(2,128)(2,1)}), bf16[128,2,128]{2,1,0:T(2,128)(2,1)S(1)}, u32[]{:S(2)}, u32[]{:S(2)}) async-start(bf16[128,2,128]{2,1,0:T(2,128)(2,1)} %reshape.328), calls=%async_computation.1 | async-start | bytes 131072 | tf_op jit(solution)/shard_map/all_to_all | solution.py:209

commit v10 on v9

--- a/solution.py
+++ b/solution.py
@@ -118,7 +118,7 @@
 
 
 def transform_blocks(x_parts, lon_count):
-    highest = lax.Precision.HIGH
+    highest = lax.Precision.DEFAULT
     _, outer, blocks, signals = x_parts.shape
     inner = lon_count // outer
     a_idx = jnp.arange(outer, dtype=jnp.int32)

time: 62.1 us -> 61.8 us (level)
  no operation moved by 1% of the time
where the time goes in v10:
time: 61.8 us; the launch traced here: 61.5 us
  waiting for transfers between devices  17.5 us (28%)
  starting transfers between devices  16 us (26%)
  Pallas kernels  15.6 us (25%)
  local copies, waits for them, and re-layouts  6.81 us (11%)
  matrix products  2.47 us (4%)
  other arithmetic  2.21 us (4%)
  between operations  0.98 us (2%)
    all_to_all x1, starting transfers between devices, shards(): got = lax.all_to_all(payload, ('gx', 'gy'), 0, 0, tiled=True)  11.5 us
    all_to_all x1, waiting for transfers between devices, shards(): got = lax.all_to_all(payload, ('gx', 'gy'), 0, 0, tiled=True)  8.87 us
    all_to_all x1, waiting for transfers between devices, shards(): back = lax.all_to_all(back, ('gx', 'gy'), 0, 0, tiled=True)  8.62 us
    pallas_call x1, Pallas kernels, analyze(): pl.pallas_call(_analysis_kernel, grid_spec=grid_spec, out_shape=jax.Shape...  8.13 us
    pallas_call x1, Pallas kernels, synthesize(): pl.pallas_call(_synth_kernel, grid_spec=grid_spec, out_shape=jax.ShapeDty...  7.45 us
    all_to_all x1, starting transfers between devices, shards(): back = lax.all_to_all(back, ('gx', 'gy'), 0, 0, tiled=True)  4.48 us
  transfers between devices with their start and end apart: 2, of which 2 were waited for; matrix products, arithmetic and copies ran while one was open for 2% of the time, Pallas kernels for 0%

profile of v10, /device:TPU:1, one launch (start us, length us, event | category | flops | bytes accessed | tf_op | source)
XLA Modules:
  0.0 61.5 jit_solution(4261785507987479093)
XLA Ops:
  0.6 0.7 %convert_bitcast_fusion = (bf16[24,1]{0,1:T(2,128)(2,1)S(1)}, bf16[24,1]{0,1:T(2,128)(2,1)S(1)}) fusion(s32[24]{0:T(128)} %orders_ref.3), kind=kLoop, calls=%fused_computation.109 | loop fusion | flops 384 | bytes 192 | tf_op jit(solution)/shard_map/stack | solution.py:180
  1.3 0.0 copy-start
  1.3 7.5 %shard_map.68 = bf16[24,8,128]{2,1,0:T(8,128)(2,1)} custom-call(s32[24]{0:T(128)} %orders_ref.3, bf16[24,2,2,2160]{3,2,1,0:T(2,128)(2,1)} %coef_ref.1, bf16[24,2160,128]{2,1,0:T(8,128)(2,1)} %leg_ref.3), custom_call_target="tpu_custom_call" | custom-call | flops 106168320 | bytes 13734912 | tf_op jit(solution)/shard_map/pallas_call | solution.py:49
  8.8 0.8 %fusion.69 = (bf16[24,1,4,128]{3,2,1,0:T(4,128)(2,1)S(1)}, bf16[24,1,4,128]{3,2,1,0:T(4,128)(2,1)S(1)}) fusion(bf16[24,2,4,128]{3,2,1,0:T(4,128)(2,1)} %bitcast.118), kind=kLoop, calls=%fused_computation.118 | loop fusion | bytes 98304 | tf_op jit(solution)/shard_map/slice | solution.py:168
  9.6 0.1 rev.6
  9.7 0.0 copy-done
  9.7 0.2 convolution_convert_fusion
  9.8 0.2 copy.58
  10.0 0.1 copy.59
  10.2 0.1 broadcast_in_dim.36
  10.3 0.8 %copy.61 = bf16[128,2,128]{2,1,0:T(2,128)(2,1)} copy(bf16[128,2,128]{0,2,1:T(8,128)(2,1)S(1)} %bitcast.111) | data formatting | bytes 131072 | tf_op jit(solution)/shard_map/reshape | solution.py:185
  11.1 11.5 %all-to-all-start = ((bf16[128,2,128]{2,1,0:T(2,128)(2,1)}), bf16[128,2,128]{2,1,0:T(2,128)(2,1)S(1)}, u32[]{:S(2)}, u32[]{:S(2)}) async-start(bf16[128,2,128]{2,1,0:T(2,128)(2,1)} %copy.61), calls=%async_computation | async-start | bytes 131072 | tf_op jit(solution)/shard_map/all_to_all | solution.py:186
  22.6 0.1 fusion.55
  22.7 0.1 fusion.58
  22.8 0.2 fusion.48
  23.0 0.1 select_multiply_fusion
  23.1 0.2 sine_negate_fusion
  23.2 8.9 %all-to-all-done = bf16[128,2,128]{2,1,0:T(2,128)(2,1)S(1)} async-done(((bf16[128,2,128]{2,1,0:T(2,128)(2,1)}), bf16[128,2,128]{2,1,0:T(2,128)(2,1)S(1)}, u32[]{:S(2)}, u32[]{:S(2)}) %all-to-all-start) | async-done | bytes 65568 | tf_op jit(solution)/shard_map/all_to_all | solution.py:186
  32.1 0.6 reshape.324
  32.7 1.0 %slice_reduce_fusion.1 = (bf16[3072]{0:T(1024)(128)(2,1)S(1)}, bf16[3072]{0:T(1024)(128)(2,1)S(1)}) fusion(bf16[3072,10]{1,0:T(8,128)(2,1)S(1)} %reshape.324), kind=kLoop, calls=%fused_computation.15 | loop fusion | bytes 24576 | tf_op jit(solution)/shard_map/slice | solution.py:189
  33.7 0.1 iota_compare_fusion.4
  33.8 0.2 copy.62
  34.0 0.6 fusion
  34.7 0.2 convolution_bitcast_fusion.1
  35.0 0.2 fusion.5
  35.1 0.2 convolution_bitcast_fusion
  35.4 0.2 convolution_bitcast_fusion.3
  35.7 0.0 copy-start.1
  35.7 0.7 %fusion.3 = bf16[3072,8]{0,1:T(8,128)(2,1)S(1)} fusion(bf16[30,72,8]{1,0,2:T(8,128)(2,1)S(1)} %bitcast.122, pred[3072,30]{0,1:T(8,128)(4,1)S(1)} %iota_compare_fusion.4, bf16[3072]{0:T(1024)(128)(2,1)S(1)} %get-tuple-element.2), kind=kOutput, calls=%fused_computation.4 | convolution fusion | flops 108281856 | bytes 182016 | tf_op jit(solution)/shard_map/sd,cdr->scr/dot_general | solution.py:203
  36.4 0.4 copy.70
  36.8 0.5 convert_element_type.119
  37.3 0.7 %reshape.328 = bf16[128,2,128]{2,1,0:T(2,128)(2,1)} reshape(bf16[128,256]{1,0:T(8,128)(2,1)S(1)} %pad.9) | data formatting | bytes 131072 | tf_op jit(solution)/shard_map/reshape | solution.py:208
  38.0 4.5 %all-to-all-start.1 = ((bf16[128,2,128]{2,1,0:T(2,128)(2,1)}), bf16[128,2,128]{2,1,0:T(2,128)(2,1)S(1)}, u32[]{:S(2)}, u32[]{:S(2)}) async-start(bf16[128,2,128]{2,1,0:T(2,128)(2,1)} %reshape.328), calls=%async_computation.1 | async-start | bytes 131072 | tf_op jit(solution)/shard_map/all_to_all | solution.py:209
  42.5 0.1 copy.66
  42.6 0.8 %reshape_reshape.3 = bf16[2,2,4320]{2,1,0:T(2,128)(2,1)} reshape(bf16[4,72,60]{2,1,0:T(8,128)(2,1)S(1)} %copy.66) | data formatting | bytes 69120 | tf_op jit(solution)/shard_map/reshape;reshape | solution.py:197
  43.4 8.6 %all-to-all-done.1 = bf16[128,2,128]{2,1,0:T(2,128)(2,1)S(1)} async-done(((bf16[128,2,128]{2,1,0:T(2,128)(2,1)}), bf16[128,2,128]{2,1,0:T(2,128)(2,1)S(1)}, u32[]{:S(2)}, u32[]{:S(2)}) %all-to-all-start.1) | async-done | bytes 65568 | tf_op jit(solution)/shard_map/all_to_all | solution.py:209
  52.0 0.1 copy.71
  52.1 0.2 copy.72
  52.3 0.2 fusion.16
  52.6 0.1 rev.7
  52.7 0.0 copy-done.1
  52.7 0.6 %pad_maximum_fusion.5.both_ref = bf16[24,8,128]{2,1,0:T(8,128)(2,1)} fusion(bf16[24,4,128]{2,1,0:T(4,128)(2,1)S(1)} %get-tuple-element.13, bf16[24,4,128]{2,1,0:T(4,128)(2,1)S(1)} %get-tuple-element.12), kind=kLoop, calls=%fused_computation.61 | loop fusion | flops 98304 | bytes 98304 | tf_op jit(solution)/shard_map/concatenate | solution.py:219
  53.4 8.1 %shard_map.69 = bf16[24,2,2,2160]{3,2,1,0:T(2,128)(2,1)} custom-call(s32[24]{0:T(128)} %orders_ref.3, bf16[24,8,128]{2,1,0:T(8,128)(2,1)} %pad_maximum_fusion.5.both_ref, bf16[24,2160,128]{2,1,0:T(8,128)(2,1)} %leg_ref.3), custom_call_target="tpu_custom_call" | custom-call | flops 106168320 | bytes 13734912 | tf_op jit(solution)/shard_map/pallas_call | solution.py:91
  (25 shorter events, 0.4 us)
Async XLA Ops:
  1.3 8.4 %copy-start = (s32[256]{0:T(256)S(1)}, s32[256]{0:T(256)}, u32[]{:S(2)}) copy-start(s32[256]{0:T(256)} %param.8) | copy-start | bytes 3076
  11.1 21.0 %all-to-all-start = ((bf16[128,2,128]{2,1,0:T(2,128)(2,1)}), bf16[128,2,128]{2,1,0:T(2,128)(2,1)S(1)}, u32[]{:S(2)}, u32[]{:S(2)}) async-start(bf16[128,2,128]{2,1,0:T(2,128)(2,1)} %copy.61), calls=%async_computation | async-start | bytes 131072 | tf_op jit(solution)/shard_map/all_to_all | solution.py:186
  35.7 17.0 %copy-start.1 = (f32[128]{0:T(128)S(1)}, f32[128]{0:T(128)}, u32[]{:S(2)}) copy-start(f32[128]{0:T(128)} %param.9) | copy-start | bytes 1540
  38.0 14.0 %all-to-all-start.1 = ((bf16[128,2,128]{2,1,0:T(2,128)(2,1)}), bf16[128,2,128]{2,1,0:T(2,128)(2,1)S(1)}, u32[]{:S(2)}, u32[]{:S(2)}) async-start(bf16[128,2,128]{2,1,0:T(2,128)(2,1)} %reshape.328), calls=%async_computation.1 | async-start | bytes 131072 | tf_op jit(solution)/shard_map/all_to_all | solution.py:209

commit v11 on v9

--- a/solution.py
+++ b/solution.py
@@ -179,15 +179,15 @@
     block_of = jnp.where(orders >= 0, orders // outer, -1)
     order_code = jnp.stack([block_of, orders % outer], axis=-1).astype(jnp.bfloat16)
     order_code = jnp.broadcast_to(order_code[None], (devices, slot_cap, 2))
-    payload = jnp.concatenate([sends, order_code], axis=-1).reshape(devices, -1)
+    payload = jnp.concatenate([order_code, sends], axis=-1).reshape(devices, -1)
     width = payload.shape[1]
     padded = -(-width // 256) * 256
     payload = jnp.pad(payload, ((0, 0), (0, padded - width))).reshape(devices, padded // 128, 128)
     got = lax.all_to_all(payload, ("gx", "gy"), 0, 0, tiled=True)
     got = got.reshape(devices, padded)[:, :width].reshape(devices * slot_cap, -1)
-    data = got[:, :-2]
-    by_d = (got[:, -1:] == jnp.arange(outer, dtype=jnp.bfloat16)[None, :]).astype(jnp.bfloat16)
-    in_c = got[:, -2:-1] == jnp.arange(blocks, dtype=jnp.bfloat16)[None, :]
+    data = got[:, 2:]
+    by_d = (got[:, 1:2] == jnp.arange(outer, dtype=jnp.bfloat16)[None, :]).astype(jnp.bfloat16)
+    in_c = got[:, 0:1] == jnp.arange(blocks, dtype=jnp.bfloat16)[None, :]
     spread = jnp.where(in_c[:, :, None], data[:, None, :], jnp.zeros((), jnp.bfloat16))
     dense = jnp.einsum("sd,scr->dcr", by_d, spread, preferred_element_type=jnp.float32)
     dense = dense.reshape(outer, blocks, epoch_count, 2, rows_each)

time: 62.1 us -> 62.1 us (level)
    slice x2 -> x3, local copies, waits for them, and re-layouts: 1.25 us -> 1.29 us  [the longest x1 0.77 us: shards(): got[:, 1:2] == jnp.arange(outer, dtype=jnp.bfloat16)[None, :]]
where the time goes in v11:
time: 62.1 us; the launch traced here: 61.9 us
  waiting for transfers between devices  17.5 us (28%)
  starting transfers between devices  16 us (26%)
  Pallas kernels  15.6 us (25%)
  local copies, waits for them, and re-layouts  6.86 us (11%)
  matrix products  2.78 us (4%)
  other arithmetic  2.18 us (4%)
  between operations  0.98 us (2%)
    all_to_all x1, starting transfers between devices, shards(): got = lax.all_to_all(payload, ('gx', 'gy'), 0, 0, tiled=True)  11.5 us
    all_to_all x1, waiting for transfers between devices, shards(): got = lax.all_to_all(payload, ('gx', 'gy'), 0, 0, tiled=True)  8.87 us
    all_to_all x1, waiting for transfers between devices, shards(): back = lax.all_to_all(back, ('gx', 'gy'), 0, 0, tiled=True)  8.61 us
    pallas_call x1, Pallas kernels, analyze(): pl.pallas_call(_analysis_kernel, grid_spec=grid_spec, out_shape=jax.Shape...  8.13 us
    pallas_call x1, Pallas kernels, synthesize(): pl.pallas_call(_synth_kernel, grid_spec=grid_spec, out_shape=jax.ShapeDty...  7.45 us
    all_to_all x1, starting transfers between devices, shards(): back = lax.all_to_all(back, ('gx', 'gy'), 0, 0, tiled=True)  4.49 us
  transfers between devices with their start and end apart: 2, of which 2 were waited for; matrix products, arithmetic and copies ran while one was open for 2% of the time, Pallas kernels for 0%

profile of v11, /device:TPU:1, one launch (start us, length us, event | category | flops | bytes accessed | tf_op | source)
XLA Modules:
  0.0 61.9 jit_solution(11772400917364249773)
XLA Ops:
  0.6 0.7 %convert_bitcast_fusion = (bf16[24,1]{0,1:T(2,128)(2,1)S(1)}, bf16[24,1]{0,1:T(2,128)(2,1)S(1)}) fusion(s32[24]{0:T(128)} %orders_ref.3), kind=kLoop, calls=%fused_computation.109 | loop fusion | flops 384 | bytes 192 | tf_op jit(solution)/shard_map/stack | solution.py:180
  1.3 0.0 copy-start
  1.3 7.5 %shard_map.68 = bf16[24,8,128]{2,1,0:T(8,128)(2,1)} custom-call(s32[24]{0:T(128)} %orders_ref.3, bf16[24,2,2,2160]{3,2,1,0:T(2,128)(2,1)} %coef_ref.1, bf16[24,2160,128]{2,1,0:T(8,128)(2,1)} %leg_ref.3), custom_call_target="tpu_custom_call" | custom-call | flops 106168320 | bytes 13734912 | tf_op jit(solution)/shard_map/pallas_call | solution.py:49
  8.8 0.8 %fusion.69 = (bf16[24,1,4,128]{3,2,1,0:T(4,128)(2,1)S(1)}, bf16[24,1,4,128]{3,2,1,0:T(4,128)(2,1)S(1)}) fusion(bf16[24,2,4,128]{3,2,1,0:T(4,128)(2,1)} %bitcast.116), kind=kLoop, calls=%fused_computation.118 | loop fusion | bytes 98304 | tf_op jit(solution)/shard_map/slice | solution.py:168
  9.6 0.1 rev.6
  9.7 0.0 copy-done
  9.7 0.2 convolution_convert_fusion
  9.8 0.2 copy.58
  10.0 0.1 copy.59
  10.2 0.1 broadcast_in_dim.36
  10.3 0.8 %copy.61 = bf16[128,2,128]{2,1,0:T(2,128)(2,1)} copy(bf16[128,2,128]{0,2,1:T(8,128)(2,1)S(1)} %bitcast.111) | data formatting | bytes 131072 | tf_op jit(solution)/shard_map/reshape | solution.py:185
  11.1 11.5 %all-to-all-start = ((bf16[128,2,128]{2,1,0:T(2,128)(2,1)}), bf16[128,2,128]{2,1,0:T(2,128)(2,1)S(1)}, u32[]{:S(2)}, u32[]{:S(2)}) async-start(bf16[128,2,128]{2,1,0:T(2,128)(2,1)} %copy.61), calls=%async_computation | async-start | bytes 131072 | tf_op jit(solution)/shard_map/all_to_all | solution.py:186
  22.6 0.1 fusion.55
  22.7 0.1 fusion.58
  22.8 0.2 sine_negate_fusion
  23.0 0.1 select_multiply_fusion
  23.1 0.2 fusion.48
  23.2 8.9 %all-to-all-done = bf16[128,2,128]{2,1,0:T(2,128)(2,1)S(1)} async-done(((bf16[128,2,128]{2,1,0:T(2,128)(2,1)}), bf16[128,2,128]{2,1,0:T(2,128)(2,1)S(1)}, u32[]{:S(2)}, u32[]{:S(2)}) %all-to-all-start) | async-done | bytes 65568 | tf_op jit(solution)/shard_map/all_to_all | solution.py:186
  32.1 0.6 reshape.324
  32.7 0.8 %slice_reduce_fusion.1 = (bf16[3072]{0:T(1024)(128)(2,1)S(1)}, bf16[3072]{0:T(1024)(128)(2,1)S(1)}) fusion(bf16[3072,10]{1,0:T(8,128)(2,1)S(1)} %reshape.324), kind=kLoop, calls=%fused_computation.15 | loop fusion | bytes 24576 | tf_op jit(solution)/shard_map/slice | solution.py:189
  33.5 0.3 slice.80
  33.8 0.1 iota_compare_fusion.4
  33.8 0.2 copy.62
  34.1 0.6 fusion
  34.7 0.3 convolution_bitcast_fusion.1
  35.1 0.3 fusion.5
  35.4 0.3 convolution_bitcast_fusion
  35.7 0.3 convolution_bitcast_fusion.3
  36.0 0.0 copy-start.1
  36.0 0.7 %fusion.3 = bf16[3072,8]{0,1:T(8,128)(2,1)S(1)} fusion(bf16[30,72,8]{1,0,2:T(8,128)(2,1)S(1)} %bitcast.120, pred[3072,30]{0,1:T(8,128)(4,1)S(1)} %iota_compare_fusion.4, bf16[3072]{0:T(1024)(128)(2,1)S(1)} %get-tuple-element.2), kind=kOutput, calls=%fused_computation.4 | convolution fusion | flops 108281856 | bytes 182016 | tf_op jit(solution)/shard_map/sd,cdr->scr/dot_general | solution.py:203
  36.8 0.4 copy.70
  37.1 0.5 convert_element_type.119
  37.7 0.7 %reshape.328 = bf16[128,2,128]{2,1,0:T(2,128)(2,1)} reshape(bf16[128,256]{1,0:T(8,128)(2,1)S(1)} %pad.9) | data formatting | bytes 131072 | tf_op jit(solution)/shard_map/reshape | solution.py:208
  38.3 4.5 %all-to-all-start.1 = ((bf16[128,2,128]{2,1,0:T(2,128)(2,1)}), bf16[128,2,128]{2,1,0:T(2,128)(2,1)S(1)}, u32[]{:S(2)}, u32[]{:S(2)}) async-start(bf16[128,2,128]{2,1,0:T(2,128)(2,1)} %reshape.328), calls=%async_computation.1 | async-start | bytes 131072 | tf_op jit(solution)/shard_map/all_to_all | solution.py:209
  42.8 0.1 copy.66
  42.9 0.8 %reshape_reshape.3 = bf16[2,2,4320]{2,1,0:T(2,128)(2,1)} reshape(bf16[4,72,60]{2,1,0:T(8,128)(2,1)S(1)} %copy.66) | data formatting | bytes 69120 | tf_op jit(solution)/shard_map/reshape;reshape | solution.py:197
  43.7 8.6 %all-to-all-done.1 = bf16[128,2,128]{2,1,0:T(2,128)(2,1)S(1)} async-done(((bf16[128,2,128]{2,1,0:T(2,128)(2,1)}), bf16[128,2,128]{2,1,0:T(2,128)(2,1)S(1)}, u32[]{:S(2)}, u32[]{:S(2)}) %all-to-all-start.1) | async-done | bytes 65568 | tf_op jit(solution)/shard_map/all_to_all | solution.py:209
  52.3 0.1 copy.71
  52.5 0.2 copy.72
  52.6 0.2 fusion.16
  52.9 0.1 rev.7
  53.0 0.0 copy-done.1
  53.1 0.6 %pad_maximum_fusion.5.both_ref = bf16[24,8,128]{2,1,0:T(8,128)(2,1)} fusion(bf16[24,4,128]{2,1,0:T(4,128)(2,1)S(1)} %get-tuple-element.13, bf16[24,4,128]{2,1,0:T(4,128)(2,1)S(1)} %get-tuple-element.12), kind=kLoop, calls=%fused_computation.61 | loop fusion | flops 98304 | bytes 98304 | tf_op jit(solution)/shard_map/concatenate | solution.py:219
  53.7 8.1 %shard_map.69 = bf16[24,2,2,2160]{3,2,1,0:T(2,128)(2,1)} custom-call(s32[24]{0:T(128)} %orders_ref.3, bf16[24,8,128]{2,1,0:T(8,128)(2,1)} %pad_maximum_fusion.5.both_ref, bf16[24,2160,128]{2,1,0:T(8,128)(2,1)} %leg_ref.3), custom_call_target="tpu_custom_call" | custom-call | flops 106168320 | bytes 13734912 | tf_op jit(solution)/shard_map/pallas_call | solution.py:91
  (25 shorter events, 0.4 us)
Async XLA Ops:
  1.3 8.4 %copy-start = (s32[256]{0:T(256)S(1)}, s32[256]{0:T(256)}, u32[]{:S(2)}) copy-start(s32[256]{0:T(256)} %param.8) | copy-start | bytes 3076
  11.1 21.0 %all-to-all-start = ((bf16[128,2,128]{2,1,0:T(2,128)(2,1)}), bf16[128,2,128]{2,1,0:T(2,128)(2,1)S(1)}, u32[]{:S(2)}, u32[]{:S(2)}) async-start(bf16[128,2,128]{2,1,0:T(2,128)(2,1)} %copy.61), calls=%async_computation | async-start | bytes 131072 | tf_op jit(solution)/shard_map/all_to_all | solution.py:186
  36.0 17.0 %copy-start.1 = (f32[128]{0:T(128)S(1)}, f32[128]{0:T(128)}, u32[]{:S(2)}) copy-start(f32[128]{0:T(128)} %param.9) | copy-start | bytes 1540
  38.3 14.0 %all-to-all-start.1 = ((bf16[128,2,128]{2,1,0:T(2,128)(2,1)}), bf16[128,2,128]{2,1,0:T(2,128)(2,1)S(1)}, u32[]{:S(2)}, u32[]{:S(2)}) async-start(bf16[128,2,128]{2,1,0:T(2,128)(2,1)} %reshape.328), calls=%async_computation.1 | async-start | bytes 131072 | tf_op jit(solution)/shard_map/all_to_all | solution.py:209

commit v12 on v9

--- a/solution.py
+++ b/solution.py
@@ -110,7 +110,10 @@
 
 
 def one_hot_rows(lat_map, lat_rows):
-    return (lat_map[None, :] == jnp.arange(lat_rows, dtype=jnp.int32)[:, None]).astype(jnp.bfloat16)
+    half = lat_rows // 2
+    slot = jnp.arange(lat_rows, dtype=jnp.int32)
+    latitude = jnp.where(slot < half, slot, lat_rows + half - 1 - slot)
+    return (lat_map[None, :] == latitude[:, None]).astype(jnp.bfloat16)
 
 
 def angle(numer, denom):
@@ -165,7 +168,7 @@
     rows_each = lat_rows // devices
 
     synth = synthesize(coeffs, legendre, orders).reshape(slot_cap, 2, epoch_count * 2, half_lats)
-    full_lats = jnp.concatenate([synth[:, 0], synth[:, 1, :, ::-1]], axis=-1)
+    full_lats = jnp.concatenate([synth[:, 0], synth[:, 1]], axis=-1)
 
     onehot = one_hot_rows(lat_map, lat_rows)
     permuted = jnp.einsum(
@@ -213,7 +216,7 @@
         "sxr,kr->sxk", returned, onehot, preferred_element_type=jnp.float32
     )
     northern = natural[..., :half_lats]
-    southern = natural[..., half_lats:][..., ::-1]
+    southern = natural[..., half_lats:]
     sym_part = ((northern + southern) * weights).astype(jnp.bfloat16)
     anti_part = ((northern - southern) * weights).astype(jnp.bfloat16)
     both = jnp.concatenate([sym_part, anti_part], axis=1)

time: 62.1 us -> 62 us (level)
  no operation moved by 1% of the time
where the time goes in v12:
time: 62 us; the launch traced here: 61.7 us
  waiting for transfers between devices  17.5 us (28%)
  starting transfers between devices  16 us (26%)
  Pallas kernels  15.6 us (25%)
  local copies, waits for them, and re-layouts  6.58 us (11%)
  matrix products  2.92 us (5%)
  other arithmetic  2.18 us (4%)
  between operations  0.97 us (2%)
    all_to_all x1, starting transfers between devices, shards(): got = lax.all_to_all(payload, ('gx', 'gy'), 0, 0, tiled=True)  11.5 us
    all_to_all x1, waiting for transfers between devices, shards(): got = lax.all_to_all(payload, ('gx', 'gy'), 0, 0, tiled=True)  8.87 us
    all_to_all x1, waiting for transfers between devices, shards(): back = lax.all_to_all(back, ('gx', 'gy'), 0, 0, tiled=True)  8.62 us
    pallas_call x1, Pallas kernels, analyze(): pl.pallas_call(_analysis_kernel, grid_spec=grid_spec, out_shape=jax.Shape...  8.13 us
    pallas_call x1, Pallas kernels, synthesize(): pl.pallas_call(_synth_kernel, grid_spec=grid_spec, out_shape=jax.ShapeDty...  7.45 us
    all_to_all x1, starting transfers between devices, shards(): back = lax.all_to_all(back, ('gx', 'gy'), 0, 0, tiled=True)  4.46 us
  transfers between devices with their start and end apart: 2, of which 2 were waited for; matrix products, arithmetic and copies ran while one was open for 2% of the time, Pallas kernels for 0%

profile of v12, /device:TPU:1, one launch (start us, length us, event | category | flops | bytes accessed | tf_op | source)
XLA Modules:
  0.0 61.7 jit_solution(4112653323020082957)
XLA Ops:
  0.6 0.7 %convert_bitcast_fusion = (bf16[24,1]{0,1:T(2,128)(2,1)S(1)}, bf16[24,1]{0,1:T(2,128)(2,1)S(1)}) fusion(s32[24]{0:T(128)} %orders_ref.3), kind=kLoop, calls=%fused_computation.115 | loop fusion | flops 384 | bytes 192 | tf_op jit(solution)/shard_map/stack | solution.py:183
  1.3 0.0 copy-start
  1.3 7.5 %shard_map.68 = bf16[24,8,128]{2,1,0:T(8,128)(2,1)} custom-call(s32[24]{0:T(128)} %orders_ref.3, bf16[24,2,2,2160]{3,2,1,0:T(2,128)(2,1)} %coef_ref.1, bf16[24,2160,128]{2,1,0:T(8,128)(2,1)} %leg_ref.3), custom_call_target="tpu_custom_call" | custom-call | flops 106168320 | bytes 13734912 | tf_op jit(solution)/shard_map/pallas_call | solution.py:49
  8.8 0.8 %fusion.72 = (bf16[24,1,4,128]{3,2,1,0:T(4,128)(2,1)S(1)}, bf16[24,1,4,128]{3,2,1,0:T(4,128)(2,1)S(1)}) fusion(bf16[24,2,4,128]{3,2,1,0:T(4,128)(2,1)} %bitcast.119), kind=kLoop, calls=%fused_computation.124 | loop fusion | bytes 98304 | tf_op jit(solution)/shard_map/slice | solution.py:171
  9.6 0.0 copy-done
  9.6 0.2 convolution_convert_fusion
  9.8 0.2 copy.58
  10.0 0.1 copy.59
  10.1 0.1 broadcast_in_dim.36
  10.3 0.8 %copy.61 = bf16[128,2,128]{2,1,0:T(2,128)(2,1)} copy(bf16[128,2,128]{0,2,1:T(8,128)(2,1)S(1)} %bitcast.114) | data formatting | bytes 131072 | tf_op jit(solution)/shard_map/reshape | solution.py:188
  11.1 11.5 %all-to-all-start = ((bf16[128,2,128]{2,1,0:T(2,128)(2,1)}), bf16[128,2,128]{2,1,0:T(2,128)(2,1)S(1)}, u32[]{:S(2)}, u32[]{:S(2)}) async-start(bf16[128,2,128]{2,1,0:T(2,128)(2,1)} %copy.61), calls=%async_computation | async-start | bytes 131072 | tf_op jit(solution)/shard_map/all_to_all | solution.py:189
  22.6 0.1 fusion.58
  22.7 0.1 fusion.61
  22.8 0.2 sine_negate_fusion
  23.0 0.1 select_multiply_fusion
  23.0 0.2 fusion.51
  23.2 8.9 %all-to-all-done = bf16[128,2,128]{2,1,0:T(2,128)(2,1)S(1)} async-done(((bf16[128,2,128]{2,1,0:T(2,128)(2,1)}), bf16[128,2,128]{2,1,0:T(2,128)(2,1)S(1)}, u32[]{:S(2)}, u32[]{:S(2)}) %all-to-all-start) | async-done | bytes 65568 | tf_op jit(solution)/shard_map/all_to_all | solution.py:189
  32.1 0.6 reshape.332
  32.7 1.0 %slice_reduce_fusion.1 = (bf16[3072]{0:T(1024)(128)(2,1)S(1)}, bf16[3072]{0:T(1024)(128)(2,1)S(1)}) fusion(bf16[3072,10]{1,0:T(8,128)(2,1)S(1)} %reshape.332), kind=kLoop, calls=%fused_computation.15 | loop fusion | bytes 24576 | tf_op jit(solution)/shard_map/slice | solution.py:192
  33.7 0.1 iota_compare_fusion.3
  33.8 0.2 copy.62
  34.0 0.6 fusion
  34.7 0.3 convolution_bitcast_fusion.1
  35.0 0.3 fusion.5
  35.3 0.3 convolution_bitcast_fusion
  35.6 0.3 convolution_bitcast_fusion.3
  36.0 0.0 copy-start.1
  36.0 0.7 %fusion.3 = bf16[3072,8]{0,1:T(8,128)(2,1)S(1)} fusion(bf16[30,72,8]{1,0,2:T(8,128)(2,1)S(1)} %bitcast.123, pred[3072,30]{0,1:T(8,128)(4,1)S(1)} %iota_compare_fusion.3, bf16[3072]{0:T(1024)(128)(2,1)S(1)} %get-tuple-element.2), kind=kOutput, calls=%fused_computation.4 | convolution fusion | flops 108281856 | bytes 182016 | tf_op jit(solution)/shard_map/sd,cdr->scr/dot_general | solution.py:206
  36.7 0.4 copy.70
  37.1 0.5 convert_element_type.119
  37.6 0.7 %reshape.336 = bf16[128,2,128]{2,1,0:T(2,128)(2,1)} reshape(bf16[128,256]{1,0:T(8,128)(2,1)S(1)} %pad.9) | data formatting | bytes 131072 | tf_op jit(solution)/shard_map/reshape | solution.py:211
  38.3 4.5 %all-to-all-start.1 = ((bf16[128,2,128]{2,1,0:T(2,128)(2,1)}), bf16[128,2,128]{2,1,0:T(2,128)(2,1)S(1)}, u32[]{:S(2)}, u32[]{:S(2)}) async-start(bf16[128,2,128]{2,1,0:T(2,128)(2,1)} %reshape.336), calls=%async_computation.1 | async-start | bytes 131072 | tf_op jit(solution)/shard_map/all_to_all | solution.py:212
  42.7 0.1 copy.66
  42.9 0.8 %reshape_reshape.3 = bf16[2,2,4320]{2,1,0:T(2,128)(2,1)} reshape(bf16[4,72,60]{2,1,0:T(8,128)(2,1)S(1)} %copy.66) | data formatting | bytes 69120 | tf_op jit(solution)/shard_map/reshape;reshape | solution.py:200
  43.6 8.6 %all-to-all-done.1 = bf16[128,2,128]{2,1,0:T(2,128)(2,1)S(1)} async-done(((bf16[128,2,128]{2,1,0:T(2,128)(2,1)}), bf16[128,2,128]{2,1,0:T(2,128)(2,1)S(1)}, u32[]{:S(2)}, u32[]{:S(2)}) %all-to-all-start.1) | async-done | bytes 65568 | tf_op jit(solution)/shard_map/all_to_all | solution.py:212
  52.2 0.1 copy.71
  52.4 0.2 copy.72
  52.6 0.3 fusion.15
  52.9 0.0 copy-done.1
  52.9 0.6 %pad_maximum_fusion.5.both_ref = bf16[24,8,128]{2,1,0:T(8,128)(2,1)} fusion(bf16[24,4,128]{2,1,0:T(4,128)(2,1)S(1)} %get-tuple-element.13, bf16[24,4,128]{2,1,0:T(4,128)(2,1)S(1)} %get-tuple-element.12), kind=kLoop, calls=%fused_computation.65 | loop fusion | flops 98304 | bytes 98304 | tf_op jit(solution)/shard_map/concatenate | solution.py:222
  53.6 8.1 %shard_map.69 = bf16[24,2,2,2160]{3,2,1,0:T(2,128)(2,1)} custom-call(s32[24]{0:T(128)} %orders_ref.3, bf16[24,8,128]{2,1,0:T(8,128)(2,1)} %pad_maximum_fusion.5.both_ref, bf16[24,2160,128]{2,1,0:T(8,128)(2,1)} %leg_ref.3), custom_call_target="tpu_custom_call" | custom-call | flops 106168320 | bytes 13734912 | tf_op jit(solution)/shard_map/pallas_call | solution.py:91
  (24 shorter events, 0.3 us)
Async XLA Ops:
  1.3 8.3 %copy-start = (s32[256]{0:T(256)S(1)}, s32[256]{0:T(256)}, u32[]{:S(2)}) copy-start(s32[256]{0:T(256)} %param.8) | copy-start | bytes 3076
  11.1 21.0 %all-to-all-start = ((bf16[128,2,128]{2,1,0:T(2,128)(2,1)}), bf16[128,2,128]{2,1,0:T(2,128)(2,1)S(1)}, u32[]{:S(2)}, u32[]{:S(2)}) async-start(bf16[128,2,128]{2,1,0:T(2,128)(2,1)} %copy.61), calls=%async_computation | async-start | bytes 131072 | tf_op jit(solution)/shard_map/all_to_all | solution.py:189
  36.0 16.9 %copy-start.1 = (f32[128]{0:T(128)S(1)}, f32[128]{0:T(128)}, u32[]{:S(2)}) copy-start(f32[128]{0:T(128)} %param.9) | copy-start | bytes 1540
  38.3 14.0 %all-to-all-start.1 = ((bf16[128,2,128]{2,1,0:T(2,128)(2,1)}), bf16[128,2,128]{2,1,0:T(2,128)(2,1)S(1)}, u32[]{:S(2)}, u32[]{:S(2)}) async-start(bf16[128,2,128]{2,1,0:T(2,128)(2,1)} %reshape.336), calls=%async_computation.1 | async-start | bytes 131072 | tf_op jit(solution)/shard_map/all_to_all | solution.py:212

commit v13 on v9

--- a/solution.py
+++ b/solution.py
@@ -59,7 +59,7 @@
     )(orders, coeffs, legendre)
 
 
-def _analysis_kernel(orders_ref, both_ref, leg_ref, out_ref):
+def _analysis_kernel(orders_ref, sym_ref, anti_ref, leg_ref, out_ref):
     step = pl.program_id(0)
     block, epochs, parts, deg_count = out_ref.shape
     half = epochs * parts
@@ -67,7 +67,8 @@
         order = orders_ref[step * block + i]
         usable, even = _masks(order, deg_count)
         res = lax.dot_general(
-            both_ref[i], leg_ref[i], (((1,), (1,)), ((), ())), preferred_element_type=jnp.float32
+            jnp.concatenate([sym_ref[i], anti_ref[i]], axis=0), leg_ref[i], (((1,), (1,)), ((), ())),
+            preferred_element_type=jnp.float32,
         )
         chosen = jnp.where(even, res[:half], res[half:])
         chosen = jnp.where(usable, chosen, jnp.float32(0.0)).astype(out_ref.dtype)
@@ -75,15 +76,17 @@
             out_ref[i, e] = chosen[e * parts:(e + 1) * parts]
 
 
-def analyze(both, legendre, orders, epochs, parts):
-    slot_cap, rows, half_lats = both.shape
+def analyze(sym, anti, legendre, orders, epochs, parts):
+    slot_cap, half, half_lats = sym.shape
+    rows = 2 * half
     deg_count = legendre.shape[1]
     block = SLOTS_PER_STEP
     grid_spec = pltpu.PrefetchScalarGridSpec(
         num_scalar_prefetch=1,
         grid=(slot_cap // block,),
         in_specs=[
-            pl.BlockSpec((block, rows, half_lats), lambda g, o: (g, 0, 0)),
+            pl.BlockSpec((block, half, half_lats), lambda g, o: (g, 0, 0)),
+            pl.BlockSpec((block, half, half_lats), lambda g, o: (g, 0, 0)),
             pl.BlockSpec((block, deg_count, half_lats), lambda g, o: (g, 0, 0)),
         ],
         out_specs=pl.BlockSpec((block, epochs, parts, deg_count), lambda g, o: (g, 0, 0, 0)),
@@ -95,10 +98,10 @@
         compiler_params=pltpu.CompilerParams(dimension_semantics=("arbitrary",)),
         cost_estimate=pl.CostEstimate(
             flops=2 * slot_cap * rows * deg_count * half_lats,
-            bytes_accessed=legendre.size * 2 + both.size * 2 + slot_cap * epochs * parts * deg_count * 2,
+            bytes_accessed=legendre.size * 2 + 2 * sym.size * 2 + slot_cap * epochs * parts * deg_count * 2,
             transcendentals=0,
         ),
-    )(orders, both, legendre)
+    )(orders, sym, anti, legendre)
 
 
 def inner_length(lon_count):
@@ -216,8 +219,7 @@
     southern = natural[..., half_lats:][..., ::-1]
     sym_part = ((northern + southern) * weights).astype(jnp.bfloat16)
     anti_part = ((northern - southern) * weights).astype(jnp.bfloat16)
-    both = jnp.concatenate([sym_part, anti_part], axis=1)
-    spectra = analyze(both, legendre, orders, epoch_count, 2)
+    spectra = analyze(sym_part, anti_part, legendre, orders, epoch_count, 2)
     return (grid_rows, spectra)
 
 

time: 62.1 us -> 62.1 us (level)
    concatenate x1 -> x0, other arithmetic: 0.65 us -> none  [shards(): both = jnp.concatenate([sym_part, anti_part], axis=1)]
where the time goes in v13:
time: 62.1 us; the launch traced here: 61.8 us
  waiting for transfers between devices  17.5 us (28%)
  starting transfers between devices  16 us (26%)
  Pallas kernels  15.6 us (25%)
  local copies, waits for them, and re-layouts  6.82 us (11%)
  matrix products  2.78 us (4%)
  other arithmetic  2.14 us (3%)
  between operations  0.97 us (2%)
    all_to_all x1, starting transfers between devices, shards(): got = lax.all_to_all(payload, ('gx', 'gy'), 0, 0, tiled=True)  11.5 us
    all_to_all x1, waiting for transfers between devices, shards(): got = lax.all_to_all(payload, ('gx', 'gy'), 0, 0, tiled=True)  8.87 us
    all_to_all x1, waiting for transfers between devices, shards(): back = lax.all_to_all(back, ('gx', 'gy'), 0, 0, tiled=True)  8.62 us
    pallas_call x1, Pallas kernels, analyze(): pl.pallas_call(_analysis_kernel, grid_spec=grid_spec, out_shape=jax.Shape...  8.15 us
    pallas_call x1, Pallas kernels, synthesize(): pl.pallas_call(_synth_kernel, grid_spec=grid_spec, out_shape=jax.ShapeDty...  7.45 us
    all_to_all x1, starting transfers between devices, shards(): back = lax.all_to_all(back, ('gx', 'gy'), 0, 0, tiled=True)  4.48 us
  transfers between devices with their start and end apart: 2, of which 2 were waited for; matrix products, arithmetic and copies ran while one was open for 2% of the time, Pallas kernels for 0%

profile of v13, /device:TPU:1, one launch (start us, length us, event | category | flops | bytes accessed | tf_op | source)
XLA Modules:
  0.0 61.8 jit_solution(6182501069058595670)
XLA Ops:
  0.6 0.7 %convert_bitcast_fusion = (bf16[24,1]{0,1:T(2,128)(2,1)S(1)}, bf16[24,1]{0,1:T(2,128)(2,1)S(1)}) fusion(s32[24]{0:T(128)} %orders_ref.3), kind=kLoop, calls=%fused_computation.108 | loop fusion | flops 384 | bytes 192 | tf_op jit(solution)/shard_map/stack | solution.py:183
  1.3 0.0 copy-start
  1.3 7.5 %shard_map.68 = bf16[24,8,128]{2,1,0:T(8,128)(2,1)} custom-call(s32[24]{0:T(128)} %orders_ref.3, bf16[24,2,2,2160]{3,2,1,0:T(2,128)(2,1)} %coef_ref.1, bf16[24,2160,128]{2,1,0:T(8,128)(2,1)} %leg_ref.3), custom_call_target="tpu_custom_call" | custom-call | flops 106168320 | bytes 13734912 | tf_op jit(solution)/shard_map/pallas_call | solution.py:49
  8.8 0.8 %fusion.69 = (bf16[24,1,4,128]{3,2,1,0:T(4,128)(2,1)S(1)}, bf16[24,1,4,128]{3,2,1,0:T(4,128)(2,1)S(1)}) fusion(bf16[24,2,4,128]{3,2,1,0:T(4,128)(2,1)} %bitcast.118), kind=kLoop, calls=%fused_computation.117 | loop fusion | bytes 98304 | tf_op jit(solution)/shard_map/slice | solution.py:171
  9.6 0.1 rev.6
  9.7 0.0 copy-done
  9.7 0.2 convolution_convert_fusion
  9.8 0.2 copy.58
  10.0 0.1 copy.59
  10.2 0.1 broadcast_in_dim.36
  10.3 0.8 %copy.61 = bf16[128,2,128]{2,1,0:T(2,128)(2,1)} copy(bf16[128,2,128]{0,2,1:T(8,128)(2,1)S(1)} %bitcast.113) | data formatting | bytes 131072 | tf_op jit(solution)/shard_map/reshape | solution.py:188
  11.1 11.5 %all-to-all-start = ((bf16[128,2,128]{2,1,0:T(2,128)(2,1)}), bf16[128,2,128]{2,1,0:T(2,128)(2,1)S(1)}, u32[]{:S(2)}, u32[]{:S(2)}) async-start(bf16[128,2,128]{2,1,0:T(2,128)(2,1)} %copy.61), calls=%async_computation | async-start | bytes 131072 | tf_op jit(solution)/shard_map/all_to_all | solution.py:189
  22.6 0.1 fusion.55
  22.7 0.1 fusion.58
  22.8 0.2 sine_negate_fusion
  23.0 0.1 select_multiply_fusion
  23.1 0.2 fusion.48
  23.2 8.9 %all-to-all-done = bf16[128,2,128]{2,1,0:T(2,128)(2,1)S(1)} async-done(((bf16[128,2,128]{2,1,0:T(2,128)(2,1)}), bf16[128,2,128]{2,1,0:T(2,128)(2,1)S(1)}, u32[]{:S(2)}, u32[]{:S(2)}) %all-to-all-start) | async-done | bytes 65568 | tf_op jit(solution)/shard_map/all_to_all | solution.py:189
  32.1 0.6 reshape.324
  32.7 1.0 %slice_reduce_fusion.1 = (bf16[3072]{0:T(1024)(128)(2,1)S(1)}, bf16[3072]{0:T(1024)(128)(2,1)S(1)}) fusion(bf16[3072,10]{1,0:T(8,128)(2,1)S(1)} %reshape.324), kind=kLoop, calls=%fused_computation.15 | loop fusion | bytes 24576 | tf_op jit(solution)/shard_map/slice | solution.py:192
  33.7 0.1 iota_compare_fusion.4
  33.8 0.2 copy.62
  34.0 0.6 fusion
  34.7 0.3 convolution_bitcast_fusion.1
  35.1 0.3 fusion.5
  35.3 0.3 convolution_bitcast_fusion
  35.6 0.3 convolution_bitcast_fusion.3
  36.0 0.0 copy-start.1
  36.0 0.7 %fusion.3 = bf16[3072,8]{0,1:T(8,128)(2,1)S(1)} fusion(bf16[30,72,8]{1,0,2:T(8,128)(2,1)S(1)} %bitcast.122, pred[3072,30]{0,1:T(8,128)(4,1)S(1)} %iota_compare_fusion.4, bf16[3072]{0:T(1024)(128)(2,1)S(1)} %get-tuple-element.2), kind=kOutput, calls=%fused_computation.4 | convolution fusion | flops 108281856 | bytes 182016 | tf_op jit(solution)/shard_map/sd,cdr->scr/dot_general | solution.py:206
  36.7 0.4 copy.70
  37.1 0.5 convert_element_type.119
  37.6 0.7 %reshape.328 = bf16[128,2,128]{2,1,0:T(2,128)(2,1)} reshape(bf16[128,256]{1,0:T(8,128)(2,1)S(1)} %pad.9) | data formatting | bytes 131072 | tf_op jit(solution)/shard_map/reshape | solution.py:211
  38.3 4.5 %all-to-all-start.1 = ((bf16[128,2,128]{2,1,0:T(2,128)(2,1)}), bf16[128,2,128]{2,1,0:T(2,128)(2,1)S(1)}, u32[]{:S(2)}, u32[]{:S(2)}) async-start(bf16[128,2,128]{2,1,0:T(2,128)(2,1)} %reshape.328), calls=%async_computation.1 | async-start | bytes 131072 | tf_op jit(solution)/shard_map/all_to_all | solution.py:212
  42.7 0.1 copy.66
  42.9 0.8 %reshape_reshape.3 = bf16[2,2,4320]{2,1,0:T(2,128)(2,1)} reshape(bf16[4,72,60]{2,1,0:T(8,128)(2,1)S(1)} %copy.66) | data formatting | bytes 69120 | tf_op jit(solution)/shard_map/reshape;reshape | solution.py:200
  43.6 8.6 %all-to-all-done.1 = bf16[128,2,128]{2,1,0:T(2,128)(2,1)S(1)} async-done(((bf16[128,2,128]{2,1,0:T(2,128)(2,1)}), bf16[128,2,128]{2,1,0:T(2,128)(2,1)S(1)}, u32[]{:S(2)}, u32[]{:S(2)}) %all-to-all-start.1) | async-done | bytes 65568 | tf_op jit(solution)/shard_map/all_to_all | solution.py:212
  52.3 0.1 copy.71
  52.4 0.2 copy.72
  52.6 0.2 fusion.16
  52.9 0.1 rev.7
  53.0 0.0 copy-done.1
  53.0 0.6 %multiply_convert_fusion.2 = (bf16[24,4,128]{2,1,0:T(4,128)(2,1)}, bf16[24,4,128]{2,1,0:T(4,128)(2,1)}) fusion(f32[24,4,128]{2,1,0:T(4,128)S(1)} %rev.7, f32[24,4,128]{2,0,1:T(8,128)S(1)} %get-tuple-element.14, f32[128]{0:T(128)S(1)} %copy-done.1), kind=kLoop, calls=%fused_computation.61 | loop fusion | flops 73728 | bytes 147968 | tf_op jit(solution)/shard_map/convert_element_type | solution.py:221
  53.6 8.2 %shard_map.69 = bf16[24,2,2,2160]{3,2,1,0:T(2,128)(2,1)} custom-call(s32[24]{0:T(128)} %orders_ref.3, bf16[24,4,128]{2,1,0:T(4,128)(2,1)} %get-tuple-element.13.sym_ref, bf16[24,4,128]{2,1,0:T(4,128)(2,1)} %get-tuple-element.12.anti_ref, bf16[24,2160,128]{2,1,0:T(8,128)(2,1)} %leg_ref.3), custom_call_target="tpu_custom_call" | custom-call | flops 106168320 | bytes 13734912 | tf_op jit(solution)/shard_map/pallas_call | solution.py:94
  (24 shorter events, 0.3 us)
Async XLA Ops:
  1.3 8.4 %copy-start = (s32[256]{0:T(256)S(1)}, s32[256]{0:T(256)}, u32[]{:S(2)}) copy-start(s32[256]{0:T(256)} %param.8) | copy-start | bytes 3076
  11.1 21.0 %all-to-all-start = ((bf16[128,2,128]{2,1,0:T(2,128)(2,1)}), bf16[128,2,128]{2,1,0:T(2,128)(2,1)S(1)}, u32[]{:S(2)}, u32[]{:S(2)}) async-start(bf16[128,2,128]{2,1,0:T(2,128)(2,1)} %copy.61), calls=%async_computation | async-start | bytes 131072 | tf_op jit(solution)/shard_map/all_to_all | solution.py:189
  36.0 17.0 %copy-start.1 = (f32[128]{0:T(128)S(1)}, f32[128]{0:T(128)}, u32[]{:S(2)}) copy-start(f32[128]{0:T(128)} %param.9) | copy-start | bytes 1540
  38.3 14.0 %all-to-all-start.1 = ((bf16[128,2,128]{2,1,0:T(2,128)(2,1)}), bf16[128,2,128]{2,1,0:T(2,128)(2,1)S(1)}, u32[]{:S(2)}, u32[]{:S(2)}) async-start(bf16[128,2,128]{2,1,0:T(2,128)(2,1)} %reshape.328), calls=%async_computation.1 | async-start | bytes 131072 | tf_op jit(solution)/shard_map/all_to_all | solution.py:212

commit v14 on v13

--- a/solution.py
+++ b/solution.py
@@ -113,7 +113,10 @@
 
 
 def one_hot_rows(lat_map, lat_rows):
-    return (lat_map[None, :] == jnp.arange(lat_rows, dtype=jnp.int32)[:, None]).astype(jnp.bfloat16)
+    half = lat_rows // 2
+    slot = jnp.arange(lat_rows, dtype=jnp.int32)
+    latitude = jnp.where(slot < half, slot, lat_rows + half - 1 - slot)
+    return (lat_map[None, :] == latitude[:, None]).astype(jnp.bfloat16)
 
 
 def angle(numer, denom):
@@ -168,7 +171,7 @@
     rows_each = lat_rows // devices
 
     synth = synthesize(coeffs, legendre, orders).reshape(slot_cap, 2, epoch_count * 2, half_lats)
-    full_lats = jnp.concatenate([synth[:, 0], synth[:, 1, :, ::-1]], axis=-1)
+    full_lats = jnp.concatenate([synth[:, 0], synth[:, 1]], axis=-1)
 
     onehot = one_hot_rows(lat_map, lat_rows)
     permuted = jnp.einsum(
@@ -216,7 +219,7 @@
         "sxr,kr->sxk", returned, onehot, preferred_element_type=jnp.float32
     )
     northern = natural[..., :half_lats]
-    southern = natural[..., half_lats:][..., ::-1]
+    southern = natural[..., half_lats:]
     sym_part = ((northern + southern) * weights).astype(jnp.bfloat16)
     anti_part = ((northern - southern) * weights).astype(jnp.bfloat16)
     spectra = analyze(sym_part, anti_part, legendre, orders, epoch_count, 2)

time: 62.1 us -> 61.9 us (level)
  no operation moved by 1% of the time
where the time goes in v14:
time: 61.9 us; the launch traced here: 61.7 us
  waiting for transfers between devices  17.5 us (28%)
  starting transfers between devices  16 us (26%)
  Pallas kernels  15.6 us (25%)
  local copies, waits for them, and re-layouts  6.58 us (11%)
  matrix products  2.92 us (5%)
  other arithmetic  2.15 us (3%)
  between operations  0.97 us (2%)
    all_to_all x1, starting transfers between devices, shards(): got = lax.all_to_all(payload, ('gx', 'gy'), 0, 0, tiled=True)  11.5 us
    all_to_all x1, waiting for transfers between devices, shards(): got = lax.all_to_all(payload, ('gx', 'gy'), 0, 0, tiled=True)  8.87 us
    all_to_all x1, waiting for transfers between devices, shards(): back = lax.all_to_all(back, ('gx', 'gy'), 0, 0, tiled=True)  8.62 us
    pallas_call x1, Pallas kernels, analyze(): pl.pallas_call(_analysis_kernel, grid_spec=grid_spec, out_shape=jax.Shape...  8.15 us
    pallas_call x1, Pallas kernels, synthesize(): pl.pallas_call(_synth_kernel, grid_spec=grid_spec, out_shape=jax.ShapeDty...  7.45 us
    all_to_all x1, starting transfers between devices, shards(): back = lax.all_to_all(back, ('gx', 'gy'), 0, 0, tiled=True)  4.46 us
  transfers between devices with their start and end apart: 2, of which 2 were waited for; matrix products, arithmetic and copies ran while one was open for 2% of the time, Pallas kernels for 0%

profile of v14, /device:TPU:1, one launch (start us, length us, event | category | flops | bytes accessed | tf_op | source)
XLA Modules:
  0.0 61.7 jit_solution(3063189895688853884)
XLA Ops:
  0.6 0.7 %convert_bitcast_fusion = (bf16[24,1]{0,1:T(2,128)(2,1)S(1)}, bf16[24,1]{0,1:T(2,128)(2,1)S(1)}) fusion(s32[24]{0:T(128)} %orders_ref.3), kind=kLoop, calls=%fused_computation.114 | loop fusion | flops 384 | bytes 192 | tf_op jit(solution)/shard_map/stack | solution.py:186
  1.3 0.0 copy-start
  1.3 7.5 %shard_map.68 = bf16[24,8,128]{2,1,0:T(8,128)(2,1)} custom-call(s32[24]{0:T(128)} %orders_ref.3, bf16[24,2,2,2160]{3,2,1,0:T(2,128)(2,1)} %coef_ref.1, bf16[24,2160,128]{2,1,0:T(8,128)(2,1)} %leg_ref.3), custom_call_target="tpu_custom_call" | custom-call | flops 106168320 | bytes 13734912 | tf_op jit(solution)/shard_map/pallas_call | solution.py:49
  8.8 0.8 %fusion.72 = (bf16[24,1,4,128]{3,2,1,0:T(4,128)(2,1)S(1)}, bf16[24,1,4,128]{3,2,1,0:T(4,128)(2,1)S(1)}) fusion(bf16[24,2,4,128]{3,2,1,0:T(4,128)(2,1)} %bitcast.119), kind=kLoop, calls=%fused_computation.123 | loop fusion | bytes 98304 | tf_op jit(solution)/shard_map/slice | solution.py:174
  9.6 0.0 copy-done
  9.6 0.2 convolution_convert_fusion
  9.8 0.2 copy.58
  10.0 0.1 copy.59
  10.1 0.1 broadcast_in_dim.36
  10.3 0.8 %copy.61 = bf16[128,2,128]{2,1,0:T(2,128)(2,1)} copy(bf16[128,2,128]{0,2,1:T(8,128)(2,1)S(1)} %bitcast.114) | data formatting | bytes 131072 | tf_op jit(solution)/shard_map/reshape | solution.py:191
  11.1 11.5 %all-to-all-start = ((bf16[128,2,128]{2,1,0:T(2,128)(2,1)}), bf16[128,2,128]{2,1,0:T(2,128)(2,1)S(1)}, u32[]{:S(2)}, u32[]{:S(2)}) async-start(bf16[128,2,128]{2,1,0:T(2,128)(2,1)} %copy.61), calls=%async_computation | async-start | bytes 131072 | tf_op jit(solution)/shard_map/all_to_all | solution.py:192
  22.6 0.1 fusion.58
  22.7 0.1 fusion.61
  22.8 0.2 sine_negate_fusion
  23.0 0.1 select_multiply_fusion
  23.0 0.2 fusion.51
  23.2 8.9 %all-to-all-done = bf16[128,2,128]{2,1,0:T(2,128)(2,1)S(1)} async-done(((bf16[128,2,128]{2,1,0:T(2,128)(2,1)}), bf16[128,2,128]{2,1,0:T(2,128)(2,1)S(1)}, u32[]{:S(2)}, u32[]{:S(2)}) %all-to-all-start) | async-done | bytes 65568 | tf_op jit(solution)/shard_map/all_to_all | solution.py:192
  32.1 0.6 reshape.332
  32.7 1.0 %slice_reduce_fusion.1 = (bf16[3072]{0:T(1024)(128)(2,1)S(1)}, bf16[3072]{0:T(1024)(128)(2,1)S(1)}) fusion(bf16[3072,10]{1,0:T(8,128)(2,1)S(1)} %reshape.332), kind=kLoop, calls=%fused_computation.15 | loop fusion | bytes 24576 | tf_op jit(solution)/shard_map/slice | solution.py:195
  33.7 0.1 iota_compare_fusion.3
  33.8 0.2 copy.62
  34.0 0.6 fusion
  34.7 0.3 convolution_bitcast_fusion.1
  35.0 0.3 fusion.5
  35.3 0.3 convolution_bitcast_fusion
  35.6 0.3 convolution_bitcast_fusion.3
  36.0 0.0 copy-start.1
  36.0 0.7 %fusion.3 = bf16[3072,8]{0,1:T(8,128)(2,1)S(1)} fusion(bf16[30,72,8]{1,0,2:T(8,128)(2,1)S(1)} %bitcast.123, pred[3072,30]{0,1:T(8,128)(4,1)S(1)} %iota_compare_fusion.3, bf16[3072]{0:T(1024)(128)(2,1)S(1)} %get-tuple-element.2), kind=kOutput, calls=%fused_computation.4 | convolution fusion | flops 108281856 | bytes 182016 | tf_op jit(solution)/shard_map/sd,cdr->scr/dot_general | solution.py:209
  36.7 0.4 copy.70
  37.1 0.5 convert_element_type.119
  37.6 0.7 %reshape.336 = bf16[128,2,128]{2,1,0:T(2,128)(2,1)} reshape(bf16[128,256]{1,0:T(8,128)(2,1)S(1)} %pad.9) | data formatting | bytes 131072 | tf_op jit(solution)/shard_map/reshape | solution.py:214
  38.3 4.5 %all-to-all-start.1 = ((bf16[128,2,128]{2,1,0:T(2,128)(2,1)}), bf16[128,2,128]{2,1,0:T(2,128)(2,1)S(1)}, u32[]{:S(2)}, u32[]{:S(2)}) async-start(bf16[128,2,128]{2,1,0:T(2,128)(2,1)} %reshape.336), calls=%async_computation.1 | async-start | bytes 131072 | tf_op jit(solution)/shard_map/all_to_all | solution.py:215
  42.7 0.1 copy.66
  42.9 0.8 %reshape_reshape.3 = bf16[2,2,4320]{2,1,0:T(2,128)(2,1)} reshape(bf16[4,72,60]{2,1,0:T(8,128)(2,1)S(1)} %copy.66) | data formatting | bytes 69120 | tf_op jit(solution)/shard_map/reshape;reshape | solution.py:203
  43.6 8.6 %all-to-all-done.1 = bf16[128,2,128]{2,1,0:T(2,128)(2,1)S(1)} async-done(((bf16[128,2,128]{2,1,0:T(2,128)(2,1)}), bf16[128,2,128]{2,1,0:T(2,128)(2,1)S(1)}, u32[]{:S(2)}, u32[]{:S(2)}) %all-to-all-start.1) | async-done | bytes 65568 | tf_op jit(solution)/shard_map/all_to_all | solution.py:215
  52.2 0.1 copy.71
  52.4 0.2 copy.72
  52.6 0.3 fusion.15
  52.9 0.0 copy-done.1
  52.9 0.6 %multiply_convert_fusion.2 = (bf16[24,4,128]{2,1,0:T(4,128)(2,1)}, bf16[24,4,128]{2,1,0:T(4,128)(2,1)}) fusion(f32[24,4,128]{2,0,1:T(8,128)S(1)} %get-tuple-element.15, f32[24,4,128]{2,0,1:T(8,128)S(1)} %get-tuple-element.14, f32[128]{0:T(128)S(1)} %copy-done.1), kind=kLoop, calls=%fused_computation.65 | loop fusion | flops 73728 | bytes 147968 | tf_op jit(solution)/shard_map/convert_element_type | solution.py:224
  53.5 8.2 %shard_map.69 = bf16[24,2,2,2160]{3,2,1,0:T(2,128)(2,1)} custom-call(s32[24]{0:T(128)} %orders_ref.3, bf16[24,4,128]{2,1,0:T(4,128)(2,1)} %get-tuple-element.13.sym_ref, bf16[24,4,128]{2,1,0:T(4,128)(2,1)} %get-tuple-element.12.anti_ref, bf16[24,2160,128]{2,1,0:T(8,128)(2,1)} %leg_ref.3), custom_call_target="tpu_custom_call" | custom-call | flops 106168320 | bytes 13734912 | tf_op jit(solution)/shard_map/pallas_call | solution.py:94
  (23 shorter events, 0.3 us)
Async XLA Ops:
  1.3 8.3 %copy-start = (s32[256]{0:T(256)S(1)}, s32[256]{0:T(256)}, u32[]{:S(2)}) copy-start(s32[256]{0:T(256)} %param.8) | copy-start | bytes 3076
  11.1 21.0 %all-to-all-start = ((bf16[128,2,128]{2,1,0:T(2,128)(2,1)}), bf16[128,2,128]{2,1,0:T(2,128)(2,1)S(1)}, u32[]{:S(2)}, u32[]{:S(2)}) async-start(bf16[128,2,128]{2,1,0:T(2,128)(2,1)} %copy.61), calls=%async_computation | async-start | bytes 131072 | tf_op jit(solution)/shard_map/all_to_all | solution.py:192
  36.0 16.9 %copy-start.1 = (f32[128]{0:T(128)S(1)}, f32[128]{0:T(128)}, u32[]{:S(2)}) copy-start(f32[128]{0:T(128)} %param.9) | copy-start | bytes 1540
  38.3 14.0 %all-to-all-start.1 = ((bf16[128,2,128]{2,1,0:T(2,128)(2,1)}), bf16[128,2,128]{2,1,0:T(2,128)(2,1)S(1)}, u32[]{:S(2)}, u32[]{:S(2)}) async-start(bf16[128,2,128]{2,1,0:T(2,128)(2,1)} %reshape.336), calls=%async_computation.1 | async-start | bytes 131072 | tf_op jit(solution)/shard_map/all_to_all | solution.py:215
